TPU v7x, 32 devices: a whole 2x2x4 slice. The times are simulated.
32 devices in a mesh: dev: 32 (over z, y, x, core).
Axes of the slice: x: 2, y: 2, z: 4, core: 2. Of those that a mesh axis runs over, the one named last changes fastest.
Arguments:
- tiles: bfloat16 [64, 128, 4096], P('dev'), may hold values from -6 to 6
- footprint: int32 [32, 21, 3], P('dev'), may hold values from 0 to 4032, as said below
- classes: int32 [32], P('dev'), may hold values from 0 to 15
- rotations: int32 [32], P('dev'), may hold values from 0 to 31
- references: bfloat16 [1024, 512], P('dev'), may hold values from -6 to 6
Outputs:
- scores: float32 [32, 512], P('dev')
- class_sums: float32 [1024, 512], P('dev')
Inputs may be any that keep to these rules, and one draw needn't show every extreme that they name: Rows and columns of a footprint lie inside the tile (64 and 4032 at most). Of the footprints of one device's particles at most 2 lie in the tiles held by any one device, and one device holds exactly 2 footprints of every device's particles.
All inputs are finite; a program needn't handle non-finite values.
Results may differ from a plain program's by a relative error of at most 0.0047.
Values may be sent and summed in bfloat16 or wider, within the bound.
No kernel may reach another device: no remote copies, remote signals or barrier semaphores. Data moves between devices by JAX's collectives and lax.ppermute only.
A program may use at most 128 MiB of HBM per device.

v0:
```python
import jax
import jax.numpy as jnp
from jax import lax
from jax.sharding import PartitionSpec as P

TILTS = 21
BOX = 64
CYCLES = 16
ROTS = 32
CLASSES = 16


def back_matrix(count):
    center = (BOX - 1) / 2.0
    tilt = jnp.arange(count, dtype=jnp.float32)[:, None, None, None]
    pixel = jnp.arange(BOX, dtype=jnp.float32)[None, :, None, None]
    xpos = jnp.arange(BOX, dtype=jnp.float32)[None, None, :, None]
    zpos = jnp.arange(BOX, dtype=jnp.float32)[None, None, None, :]
    theta = (-60.0 + 120.0 * tilt / (TILTS - 1)) * (jnp.pi / 180.0)
    place = (xpos - center) * jnp.cos(theta) + (zpos - center) * jnp.sin(theta) + center
    weight = jnp.maximum(0.0, 1.0 - jnp.abs(place - pixel))
    weight = jnp.where(tilt < TILTS, weight, 0.0) / TILTS
    return weight.reshape(count * BOX, BOX * BOX).astype(jnp.bfloat16)


def cyl_matrix():
    center = (BOX - 1) / 2.0
    xpos = jnp.arange(BOX, dtype=jnp.float32)[:, None, None, None]
    zpos = jnp.arange(BOX, dtype=jnp.float32)[None, :, None, None]
    angle = jnp.arange(ROTS, dtype=jnp.float32)[None, None, :, None] * (2.0 * jnp.pi / ROTS)
    radius = (jnp.arange(CYCLES, dtype=jnp.float32)[None, None, None, :] + 0.5) * (
        BOX / (2.0 * CYCLES)
    )
    wx = jnp.maximum(0.0, 1.0 - jnp.abs(xpos - center - radius * jnp.cos(angle)))
    wz = jnp.maximum(0.0, 1.0 - jnp.abs(zpos - center - radius * jnp.sin(angle)))
    return (wx * wz).reshape(BOX * BOX, ROTS * CYCLES).astype(jnp.bfloat16)


def shift_table():
    steps = jnp.arange(ROTS, dtype=jnp.int32)
    want = (steps[None, :, None] - steps[:, None, None]) % ROTS
    return (steps[None, None, :] == want).astype(jnp.float32)


def cut_many(tiles, items):
    flat = items.reshape(-1, 3)

    def cut(item):
        return lax.dynamic_slice(tiles, (item[0], item[1], item[2]), (1, BOX, BOX)).reshape(
            BOX * BOX
        )

    pieces = jax.vmap(cut)(flat)
    return pieces.reshape(items.shape[:-1] + (BOX * BOX,))


def per_device(tiles, footprint, classes, rotations, references):
    ndev = lax.axis_size("dev")
    count = footprint.shape[0]
    asks = count * TILTS
    cap = (2 * asks + ndev - 1) // ndev
    held = tiles.shape[0]
    flat = footprint.reshape(asks, 3)
    owner = flat[:, 0] // held
    local = flat[:, 0] - owner * held
    hits = (owner[:, None] == jnp.arange(ndev, dtype=jnp.int32)[None, :]).astype(jnp.int32)
    slot = jnp.sum((jnp.cumsum(hits, axis=0) - hits) * hits, axis=1)
    wanted = (
        jnp.zeros((ndev, cap, 3), jnp.int32)
        .at[owner, slot]
        .set(jnp.stack([local, flat[:, 1], flat[:, 2]], axis=-1))
    )
    patches_cut = cut_many(
        tiles, lax.all_to_all(wanted, "dev", split_axis=0, concat_axis=0, tiled=True)
    )
    arrived = lax.all_to_all(patches_cut, "dev", split_axis=0, concat_axis=0, tiled=True)
    patch = arrived[owner, slot].reshape(count, TILTS, BOX, BOX)
    padded = TILTS + TILTS % 2
    pmat = patch.transpose(0, 2, 1, 3)
    pmat = jnp.pad(pmat, ((0, 0), (0, 0), (0, padded - TILTS), (0, 0))).reshape(
        count * BOX, padded * BOX
    )
    volume = jnp.dot(pmat, back_matrix(padded), preferred_element_type=jnp.float32).astype(
        jnp.bfloat16
    )
    cyl = jnp.dot(volume, cyl_matrix(), preferred_element_type=jnp.float32).astype(jnp.bfloat16)
    cyl = cyl.reshape(count, BOX, ROTS * CYCLES)
    whole_refs = lax.all_gather(references, "dev", axis=0, tiled=True)
    ref_three = (
        whole_refs.reshape(CLASSES, BOX, ROTS, CYCLES)
        .transpose(0, 2, 1, 3)
        .reshape(CLASSES, ROTS, BOX * CYCLES)
    )
    ref_float = whole_refs.astype(jnp.float32).reshape(CLASSES, BOX * ROTS * CYCLES)
    ref_power = jnp.mean(ref_float * ref_float, axis=1)
    cyl_three = (
        cyl.reshape(count, BOX, ROTS, CYCLES)
        .transpose(0, 2, 1, 3)
        .reshape(count, ROTS, BOX * CYCLES)
    )
    corr = jnp.einsum("pfm,cgm->pcfg", cyl_three, ref_three, preferred_element_type=jnp.float32)
    raw = jnp.einsum("pcfg,kfg->pck", corr, shift_table(), precision=lax.Precision.HIGHEST)
    cyl_float = cyl.astype(jnp.float32)
    power = jnp.mean(cyl_float.reshape(count, -1) ** 2, axis=1)
    total = BOX * ROTS * CYCLES
    scores = raw / jnp.sqrt(
        total * (power[:, None, None] + 1e-06) * (ref_power[None, :, None] + 1e-06)
    )
    scores = scores.reshape(count, CLASSES * ROTS)
    columns = jnp.arange(ROTS * CYCLES, dtype=jnp.int32)
    index = (columns[None, :] + rotations[:, None] * CYCLES) % (ROTS * CYCLES)
    turned = jnp.take_along_axis(cyl, index[:, None, :], axis=2)
    member = (classes[:, None] == jnp.arange(CLASSES, dtype=jnp.int32)[None, :]).astype(
        jnp.bfloat16
    )
    owned = CLASSES * BOX // ndev
    placed = member[:, :, None, None] * turned[:, None, :, :]
    placed = placed.reshape(count, ndev, owned, ROTS * CYCLES)
    landed = lax.all_to_all(placed, "dev", split_axis=1, concat_axis=0, tiled=True)
    class_sums = jnp.sum(landed.astype(jnp.float32), axis=(0, 1))
    return (scores, class_sums)


def solution(mesh):
    in_specs = (P("dev", None, None), P("dev", None, None), P("dev"), P("dev"), P("dev", None))
    out_specs = (P("dev", None), P("dev", None))
    return jax.shard_map(
        per_device, mesh=mesh, in_specs=in_specs, out_specs=out_specs, check_vma=False
    )
```

profile of v0, /device:TPU:0, one launch (start us, length us, event | category | flops | bytes accessed | tf_op | source)
XLA Modules:
  0.0 374.0 jit_solution(16164082664645555117)
XLA Ops:
  8.9 4.0 %scatter_fusion = s32[32,2,3]{2,1,0:T(2,128)} fusion(s32[32,2,3]{2,1,0:T(2,128)} %broadcast_in_dim.14, s32[21]{0:T(128)S(1)} %get-tuple-element.20, s32[21,3]{1,0:T(8,128)S(1)} %copy.36), kind=kCustom, calls=%fused_computation.2 | custom fusion | bytes 924 | tf_op jit(solution)/shard_map/scatter | solution.py:71
  12.9 7.3 %all-to-all-start = ((s32[32,2,3]{2,1,0:T(2,128)}), s32[32,2,3]{2,1,0:T(2,128)S(1)}, u32[]{:S(2)}, u32[]{:S(2)}) async-start(s32[32,2,3]{2,1,0:T(2,128)} %scatter_fusion), calls=%async_computation | async-start | bytes 65536 | tf_op jit(solution)/shard_map/all_to_all | solution.py:74
  21.4 13.3 %multiply_convert_fusion = bf16[22,64,64,64]{3,2,1,0:T(8,128)(2,1)} fusion(f32[22,64,64]{2,1,0:T(8,128)S(1)} %add_add_fusion, pred[22]{0:T(512)(128)(4,1)S(1)} %iota_compare_fusion.3), kind=kLoop, calls=%fused_computation.5 | loop fusion | flops 40370176 | bytes 11894806 | tf_op jit(solution)/shard_map/convert_element_type | solution.py:23
  35.4 224.2 %while.1 = (s32[]{:T(128)}, bf16[2,128,4096]{2,1,0:T(8,128)(2,1)}, s32[64,3]{0,1:T(4,128)S(1)}, bf16[64,1,64,64]{3,2,1,0:T(8,128)(2,1)S(1)}, s32[]{:T(128)}) while((s32[]{:T(128)}, bf16[2,128,4096]{2,1,0:T(8,128)(2,1)}, s32[64,3]{0,1:T(4,128)S(1)}, bf16[64,1,64,64]{3,2,1,0:T(8,128)(2,1)S(1)}, s32[]{:T(128)}) %tuple.35), condition=%wide.while_cond, body=%wide.while_body.sunk | while | flops 2 | bytes 24705 | solution.py:49
  36.0 2.8 bitcast_dynamic-update-slice_fusion.2
  39.5 2.8 bitcast_dynamic-update-slice_fusion.2
  43.1 2.8 bitcast_dynamic-update-slice_fusion.2
  46.6 2.8 bitcast_dynamic-update-slice_fusion.2
  50.1 2.8 bitcast_dynamic-update-slice_fusion.2
  53.6 2.8 bitcast_dynamic-update-slice_fusion.2
  57.1 2.8 bitcast_dynamic-update-slice_fusion.2
  60.6 2.8 bitcast_dynamic-update-slice_fusion.2
  64.1 2.8 bitcast_dynamic-update-slice_fusion.2
  67.6 2.8 bitcast_dynamic-update-slice_fusion.2
  71.1 2.8 bitcast_dynamic-update-slice_fusion.2
  74.6 2.8 bitcast_dynamic-update-slice_fusion.2
  78.1 2.8 bitcast_dynamic-update-slice_fusion.2
  81.6 2.8 bitcast_dynamic-update-slice_fusion.2
  85.1 2.8 bitcast_dynamic-update-slice_fusion.2
  88.6 2.8 bitcast_dynamic-update-slice_fusion.2
  92.1 2.8 bitcast_dynamic-update-slice_fusion.2
  95.6 2.8 bitcast_dynamic-update-slice_fusion.2
  99.1 2.8 bitcast_dynamic-update-slice_fusion.2
  102.6 2.8 bitcast_dynamic-update-slice_fusion.2
  106.1 2.8 bitcast_dynamic-update-slice_fusion.2
  109.6 2.8 bitcast_dynamic-update-slice_fusion.2
  113.1 2.8 bitcast_dynamic-update-slice_fusion.2
  116.6 2.8 bitcast_dynamic-update-slice_fusion.2
  120.1 2.8 bitcast_dynamic-update-slice_fusion.2
  123.6 2.8 bitcast_dynamic-update-slice_fusion.2
  127.1 2.8 bitcast_dynamic-update-slice_fusion.2
  130.6 2.8 bitcast_dynamic-update-slice_fusion.2
  134.1 2.8 bitcast_dynamic-update-slice_fusion.2
  137.6 2.8 bitcast_dynamic-update-slice_fusion.2
  141.1 2.8 bitcast_dynamic-update-slice_fusion.2
  144.6 2.8 bitcast_dynamic-update-slice_fusion.2
  148.2 2.8 bitcast_dynamic-update-slice_fusion.2
  151.7 2.8 bitcast_dynamic-update-slice_fusion.2
  155.2 2.8 bitcast_dynamic-update-slice_fusion.2
  158.7 2.8 bitcast_dynamic-update-slice_fusion.2
  169.2 2.8 bitcast_dynamic-update-slice_fusion.2
  172.7 2.8 bitcast_dynamic-update-slice_fusion.2
  176.2 2.8 bitcast_dynamic-update-slice_fusion.2
  179.7 2.8 bitcast_dynamic-update-slice_fusion.2
  183.2 2.8 bitcast_dynamic-update-slice_fusion.2
  204.2 2.8 bitcast_dynamic-update-slice_fusion.2
  207.7 2.8 bitcast_dynamic-update-slice_fusion.2
  211.2 2.8 bitcast_dynamic-update-slice_fusion.2
  214.7 2.8 bitcast_dynamic-update-slice_fusion.2
  218.2 2.8 bitcast_dynamic-update-slice_fusion.2
  235.7 2.8 bitcast_dynamic-update-slice_fusion.2
  239.2 2.8 bitcast_dynamic-update-slice_fusion.2
  242.7 2.8 bitcast_dynamic-update-slice_fusion.2
  246.2 2.8 bitcast_dynamic-update-slice_fusion.2
  249.7 2.8 bitcast_dynamic-update-slice_fusion.2
  261.1 5.8 %all-to-all-start.1 = ((bf16[32,2,4096]{2,1,0:T(2,128)(2,1)}), bf16[32,2,4096]{2,1,0:T(2,128)(2,1)S(1)}, u32[]{:S(2)}, u32[]{:S(2)}) async-start(bf16[32,2,4096]{2,1,0:T(2,128)(2,1)} %reshape.573), calls=%async_computation.1 | async-start | bytes 1048576 | tf_op jit(solution)/shard_map/all_to_all | solution.py:76
  267.0 7.3 %multiply_convert_fusion.1 = bf16[64,64,32,16]{1,0,3,2:T(8,128)(2,1)} fusion(f32[64,32,16]{0,2,1:T(8,128)S(1)} %get-tuple-element.31, f32[64,32,16]{0,2,1:T(8,128)S(1)} %get-tuple-element.30), kind=kLoop, calls=%fused_computation.6 | loop fusion | flops 4194304 | bytes 4456448 | tf_op jit(solution)/shard_map/convert_element_type | solution.py:36
  274.3 12.1 %convert_element_type.63 = bf16[4096,512]{0,1:T(8,128)(2,1)} reshape(bf16[64,64,32,16]{1,0,3,2:T(8,128)(2,1)} %multiply_convert_fusion.1) | data formatting | bytes 8388608 | tf_op jit(solution)/shard_map/convert_element_type | solution.py:36
  286.4 30.6 %convert_element_type.60 = bf16[1408,4096]{1,0:T(8,128)(2,1)} reshape(bf16[22,64,64,64]{3,2,1,0:T(8,128)(2,1)} %multiply_convert_fusion) | data formatting | bytes 23068672 | tf_op jit(solution)/shard_map/convert_element_type | solution.py:23
  320.5 9.5 %multiply_reduce_fusion.1 = (f32[]{:T(128)}, bf16[64,512]{1,0:T(8,128)(2,1)S(1)}) fusion(bf16[4096,512]{0,1:T(8,128)(2,1)} %convert_element_type.63, bf16[64,1408]{1,0:T(8,128)(2,1)S(1)} %reshape.575, bf16[1408,4096]{1,0:T(8,128)(2,1)} %convert_element_type.60), kind=kOutput, calls=%fused_computation.23 | convolution fusion | flops 1007026176 | bytes 15974404 | tf_op jit(solution)/shard_map/dot_general | solution.py:86
  332.9 6.1 %all-to-all-start.2 = ((bf16[1,32,32,512]{3,2,0,1:T(8,128)(2,1)}), bf16[1,32,32,512]{3,2,0,1:T(8,128)(2,1)}, u32[]{:S(2)}, u32[]{:S(2)}) async-start(bf16[1,32,32,512]{3,2,0,1:T(8,128)(2,1)} %broadcast_multiply_fusion), calls=%async_computation.2 | async-start | bytes 2097152 | tf_op jit(solution)/shard_map/all_to_all | solution.py:119
  342.9 4.9 %copy.42 = bf16[16,32,64,16]{1,3,2,0:T(8,128)(2,1)} copy(bf16[16,32,64,16]{2,0,3,1:T(8,128)(2,1)S(1)} %bitcast.74) | data formatting | bytes 2097152 | tf_op jit(solution)/shard_map/transpose | solution.py:91
  349.5 3.0 convolution_bitcast_fusion
  353.8 11.4 %all-to-all-done.2 = bf16[1,32,32,512]{3,2,0,1:T(8,128)(2,1)} async-done(((bf16[1,32,32,512]{3,2,0,1:T(8,128)(2,1)}), bf16[1,32,32,512]{3,2,0,1:T(8,128)(2,1)}, u32[]{:S(2)}, u32[]{:S(2)}) %all-to-all-start.2) | async-done | bytes 1048608 | tf_op jit(solution)/shard_map/all_to_all | solution.py:119
  (202 shorter events, 97.4 us)
Async XLA Ops:
  12.9 22.1 %all-to-all-start = ((s32[32,2,3]{2,1,0:T(2,128)}), s32[32,2,3]{2,1,0:T(2,128)S(1)}, u32[]{:S(2)}, u32[]{:S(2)}) async-start(s32[32,2,3]{2,1,0:T(2,128)} %scatter_fusion), calls=%async_computation | async-start | bytes 65536 | tf_op jit(solution)/shard_map/all_to_all | solution.py:74
  20.2 319.9 %all-gather.2.cloned.1.call-start = ((), (), s32[]{:S(2)}) async-start(), calls=%async_computation.3 | async-start | bytes 1081344 | tf_op jit(solution)/shard_map/all_gather | solution.py:88
  261.1 57.3 %all-to-all-start.1 = ((bf16[32,2,4096]{2,1,0:T(2,128)(2,1)}), bf16[32,2,4096]{2,1,0:T(2,128)(2,1)S(1)}, u32[]{:S(2)}, u32[]{:S(2)}) async-start(bf16[32,2,4096]{2,1,0:T(2,128)(2,1)} %reshape.573), calls=%async_computation.1 | async-start | bytes 1048576 | tf_op jit(solution)/shard_map/all_to_all | solution.py:76
  332.9 32.2 %all-to-all-start.2 = ((bf16[1,32,32,512]{3,2,0,1:T(8,128)(2,1)}), bf16[1,32,32,512]{3,2,0,1:T(8,128)(2,1)}, u32[]{:S(2)}, u32[]{:S(2)}) async-start(bf16[1,32,32,512]{3,2,0,1:T(8,128)(2,1)} %broadcast_multiply_fusion), calls=%async_computation.2 | async-start | bytes 2097152 | tf_op jit(solution)/shard_map/all_to_all | solution.py:119
Sparse Core Ops, SparseCore 0:
  23.9 55.0 all-gather.1
where the time goes:
time: 381 us; the launch traced here: 374 us
  local copies, waits for them, and re-layouts  286 us (75%)
  other arithmetic  26.7 us (7%)
  starting transfers between devices  19.3 us (5%)
  between operations  16.2 us (4%)
  matrix products  13.1 us (3%)
  waiting for transfers between devices  12.1 us (3%)
    gather x192, local copies, waits for them, and re-layouts  223 us
    convert_element_type x1, local copies, waits for them, and re-layouts, back_matrix(): return weight.reshape(count * BOX, BOX * BOX).astype(jnp.bfloat16)  30.6 us
    convert_element_type x1, other arithmetic, back_matrix(): return weight.reshape(count * BOX, BOX * BOX).astype(jnp.bfloat16)  13.3 us
    convert_element_type x1, local copies, waits for them, and re-layouts, cyl_matrix(): return (wx * wz).reshape(BOX * BOX, ROTS * CYCLES).astype(jnp.bfloat16)  12.1 us
    all_to_all x1, waiting for transfers between devices, per_device(): lax.all_to_all(placed, 'dev', split_axis=1, concat_axis=0, tiled=True)  11.4 us
    dot_general x1, matrix products, per_device(): jnp.dot(volume, cyl_matrix(), preferred_element_type=jnp.float32)  9.51 us
  transfers between devices with their start and end apart: 4, of which 1 were waited for; matrix products, arithmetic and copies ran while one was open for 85% of the time, Pallas kernels for 0%

commit v1 on v0

--- a/solution.py
+++ b/solution.py
@@ -1,6 +1,12 @@
+import functools
+
 import jax
 import jax.numpy as jnp
+import ml_dtypes
+import numpy as np
 from jax import lax
+from jax.experimental import pallas as pl
+from jax.experimental.pallas import tpu as pltpu
 from jax.sharding import PartitionSpec as P
 
 TILTS = 21
@@ -8,32 +14,47 @@
 CYCLES = 16
 ROTS = 32
 CLASSES = 16
+WIN = 256
 
 
-def back_matrix(count):
-    center = (BOX - 1) / 2.0
-    tilt = jnp.arange(count, dtype=jnp.float32)[:, None, None, None]
-    pixel = jnp.arange(BOX, dtype=jnp.float32)[None, :, None, None]
-    xpos = jnp.arange(BOX, dtype=jnp.float32)[None, None, :, None]
-    zpos = jnp.arange(BOX, dtype=jnp.float32)[None, None, None, :]
-    theta = (-60.0 + 120.0 * tilt / (TILTS - 1)) * (jnp.pi / 180.0)
-    place = (xpos - center) * jnp.cos(theta) + (zpos - center) * jnp.sin(theta) + center
-    weight = jnp.maximum(0.0, 1.0 - jnp.abs(place - pixel))
-    weight = jnp.where(tilt < TILTS, weight, 0.0) / TILTS
-    return weight.reshape(count * BOX, BOX * BOX).astype(jnp.bfloat16)
+def back_matrix_np(count):
+    f32 = np.float32
+    center = f32((BOX - 1) / 2.0)
+    tilt = np.arange(count, dtype=f32)[:, None, None, None]
+    pixel = np.arange(BOX, dtype=f32)[None, :, None, None]
+    xpos = np.arange(BOX, dtype=f32)[None, None, :, None]
+    zpos = np.arange(BOX, dtype=f32)[None, None, None, :]
+    theta = (f32(-60.0) + f32(120.0) * tilt / f32(TILTS - 1)) * f32(np.pi / 180.0)
+    place = (xpos - center) * np.cos(theta) + (zpos - center) * np.sin(theta) + center
+    weight = np.maximum(f32(0.0), f32(1.0) - np.abs(place - pixel))
+    weight = np.where(tilt < TILTS, weight, f32(0.0)) / f32(TILTS)
+    weight = weight.astype(f32).astype(ml_dtypes.bfloat16)
+    return weight.reshape(count * BOX, BOX * BOX)
 
 
-def cyl_matrix():
-    center = (BOX - 1) / 2.0
-    xpos = jnp.arange(BOX, dtype=jnp.float32)[:, None, None, None]
-    zpos = jnp.arange(BOX, dtype=jnp.float32)[None, :, None, None]
-    angle = jnp.arange(ROTS, dtype=jnp.float32)[None, None, :, None] * (2.0 * jnp.pi / ROTS)
-    radius = (jnp.arange(CYCLES, dtype=jnp.float32)[None, None, None, :] + 0.5) * (
+def cyl_matrix_np():
+    f32 = np.float32
+    center = f32((BOX - 1) / 2.0)
+    xpos = np.arange(BOX, dtype=f32)[:, None, None, None]
+    zpos = np.arange(BOX, dtype=f32)[None, :, None, None]
+    angle = np.arange(ROTS, dtype=f32)[None, None, :, None] * f32(2.0 * np.pi / ROTS)
+    radius = (np.arange(CYCLES, dtype=f32)[None, None, None, :] + f32(0.5)) * f32(
         BOX / (2.0 * CYCLES)
     )
-    wx = jnp.maximum(0.0, 1.0 - jnp.abs(xpos - center - radius * jnp.cos(angle)))
-    wz = jnp.maximum(0.0, 1.0 - jnp.abs(zpos - center - radius * jnp.sin(angle)))
-    return (wx * wz).reshape(BOX * BOX, ROTS * CYCLES).astype(jnp.bfloat16)
+    wx = np.maximum(f32(0.0), f32(1.0) - np.abs(xpos - center - radius * np.cos(angle)))
+    wz = np.maximum(f32(0.0), f32(1.0) - np.abs(zpos - center - radius * np.sin(angle)))
+    sample = (wx * wz).astype(f32).astype(ml_dtypes.bfloat16)
+    return sample.reshape(BOX * BOX, ROTS * CYCLES)
+
+
+@functools.lru_cache(maxsize=None)
+def folded_matrix(count):
+    back = back_matrix_np(count).astype(np.float64)
+    sample = cyl_matrix_np().astype(np.float64)
+    full = back @ sample
+    high = full.astype(ml_dtypes.bfloat16)
+    low = (full - high.astype(np.float64)).astype(ml_dtypes.bfloat16)
+    return np.asarray(high), np.asarray(low)
 
 
 def shift_table():
@@ -42,16 +63,45 @@
     return (steps[None, None, :] == want).astype(jnp.float32)
 
 
-def cut_many(tiles, items):
-    flat = items.reshape(-1, 3)
+def cut_kernel(req_ref, tiles_ref, out_ref):
+    count = out_ref.shape[0]
+    width = tiles_ref.shape[2]
+    rows = tiles_ref.shape[1]
+    row_i = lax.broadcasted_iota(jnp.int32, (BOX, rows), 0)
+    row_j = lax.broadcasted_iota(jnp.int32, (BOX, rows), 1)
+    col_v = lax.broadcasted_iota(jnp.int32, (WIN, BOX), 0)
+    col_u = lax.broadcasted_iota(jnp.int32, (WIN, BOX), 1)
 
-    def cut(item):
-        return lax.dynamic_slice(tiles, (item[0], item[1], item[2]), (1, BOX, BOX)).reshape(
-            BOX * BOX
-        )
+    def body(k, carry):
+        t = req_ref[3 * k]
+        r = req_ref[3 * k + 1]
+        c = req_ref[3 * k + 2]
+        c0 = jnp.minimum((c // 128) * 128, width - WIN)
+        c0 = pl.multiple_of(c0, 128)
+        win = tiles_ref[t, :, pl.ds(c0, WIN)]
+        pick_rows = (row_j == row_i + r).astype(jnp.bfloat16)
+        part = jnp.dot(pick_rows, win, preferred_element_type=jnp.float32)
+        pick_cols = (col_v == col_u + (c - c0)).astype(jnp.bfloat16)
+        cut = jnp.dot(part.astype(jnp.bfloat16), pick_cols, preferred_element_type=jnp.float32)
+        out_ref[k] = cut.astype(out_ref.dtype)
+        return carry
 
-    pieces = jax.vmap(cut)(flat)
-    return pieces.reshape(items.shape[:-1] + (BOX * BOX,))
+    lax.fori_loop(0, count, body, 0)
+
+
+def cut_patches(tiles, req):
+    count = req.shape[0]
+    flat = req.reshape(-1)
+    return pl.pallas_call(
+        cut_kernel,
+        out_shape=jax.ShapeDtypeStruct((count, BOX, BOX), tiles.dtype),
+        grid_spec=pltpu.PrefetchScalarGridSpec(
+            num_scalar_prefetch=1,
+            grid=(1,),
+            in_specs=[pl.BlockSpec(tiles.shape, lambda i, q: (0, 0, 0))],
+            out_specs=pl.BlockSpec((count, BOX, BOX), lambda i, q: (0, 0, 0)),
+        ),
+    )(flat, tiles)
 
 
 def per_device(tiles, footprint, classes, rotations, references):
@@ -70,9 +120,8 @@
         .at[owner, slot]
         .set(jnp.stack([local, flat[:, 1], flat[:, 2]], axis=-1))
     )
-    patches_cut = cut_many(
-        tiles, lax.all_to_all(wanted, "dev", split_axis=0, concat_axis=0, tiled=True)
-    )
+    asked = lax.all_to_all(wanted, "dev", split_axis=0, concat_axis=0, tiled=True)
+    patches_cut = cut_patches(tiles, asked.reshape(ndev * cap, 3)).reshape(ndev, cap, BOX, BOX)
     arrived = lax.all_to_all(patches_cut, "dev", split_axis=0, concat_axis=0, tiled=True)
     patch = arrived[owner, slot].reshape(count, TILTS, BOX, BOX)
     padded = TILTS + TILTS % 2
@@ -80,11 +129,11 @@
     pmat = jnp.pad(pmat, ((0, 0), (0, 0), (0, padded - TILTS), (0, 0))).reshape(
         count * BOX, padded * BOX
     )
-    volume = jnp.dot(pmat, back_matrix(padded), preferred_element_type=jnp.float32).astype(
-        jnp.bfloat16
+    high, low = folded_matrix(padded)
+    cyl = jnp.dot(pmat, jnp.asarray(high), preferred_element_type=jnp.float32) + jnp.dot(
+        pmat, jnp.asarray(low), preferred_element_type=jnp.float32
     )
-    cyl = jnp.dot(volume, cyl_matrix(), preferred_element_type=jnp.float32).astype(jnp.bfloat16)
-    cyl = cyl.reshape(count, BOX, ROTS * CYCLES)
+    cyl = cyl.astype(jnp.bfloat16).reshape(count, BOX, ROTS * CYCLES)
     whole_refs = lax.all_gather(references, "dev", axis=0, tiled=True)
     ref_three = (
         whole_refs.reshape(CLASSES, BOX, ROTS, CYCLES)

time: 381 us -> 137 us (0.36); the launches traced: 374 us -> 136 us
  local copies, waits for them, and re-layouts: 286 us -> 19.5 us
  waiting for transfers between devices: 12.1 us -> 49.4 us
  other arithmetic: 26.7 us -> 5.32 us
  Pallas kernels: 0 us -> 20.7 us
  blocking collectives: 0 us -> 14.3 us
  starting transfers between devices: 19.3 us -> 6.02 us
  matrix products: 13.1 us -> 4.9 us
    gather x192 -> x0, local copies, waits for them, and re-layouts: 223 us -> none
    convert_element_type x3 -> x1, local copies, waits for them, and re-layouts: 42.8 us -> 0.12 us  [per_device(): cyl = cyl.astype(jnp.bfloat16).reshape(count, BOX, ROTS * CYCLES)]
    all_gather x1, waiting for transfers between devices: 0.02 us -> 35.5 us  [per_device(): whole_refs = lax.all_gather(references, 'dev', axis=0, tiled=True)]
    pallas_call x0 -> x1, Pallas kernels: none -> 20.7 us  [cut_patches(): pl.pallas_call(cut_kernel, out_shape=jax.ShapeDtypeStruct((count, BOX, BO...]
    convert_element_type x2 -> x0, other arithmetic: 20.6 us -> none  [the longest x1 13.3 us: back_matrix(): return weight.reshape(count * BOX, BOX * BOX).astype(jnp.bfloat16)]
    all_to_all x0 -> x1, blocking collectives: none -> 14.3 us  [per_device(): lax.all_to_all(wanted, 'dev', split_axis=0, concat_axis=0, tiled=True)]
    all_to_all x1, waiting for transfers between devices: 0.01 us -> 13.3 us  [per_device(): lax.all_to_all(patches_cut, 'dev', split_axis=0, concat_axis=0, tiled=True)]
    all_to_all x1, waiting for transfers between devices: 11.4 us -> 0.01 us  [per_device(): lax.all_to_all(placed, 'dev', split_axis=1, concat_axis=0, tiled=True)]
  transfers between devices with their start and end apart: 4 -> 3, of which waited for: 1 -> 2; matrix products, arithmetic and copies ran while one was open for 85% -> 15% of each run, Pallas kernels for 0% -> 0%
where the time goes in v1:
time: 137 us; the launch traced here: 136 us
  waiting for transfers between devices  49.4 us (36%)
  Pallas kernels  20.7 us (15%)
  local copies, waits for them, and re-layouts  19.5 us (14%)
  between operations  16.2 us (12%)
  blocking collectives  14.3 us (10%)
  starting transfers between devices  6.02 us (4%)
  other arithmetic  5.32 us (4%)
  matrix products  4.9 us (4%)
    all_gather x1, waiting for transfers between devices, per_device(): whole_refs = lax.all_gather(references, 'dev', axis=0, tiled=True)  35.5 us
    pallas_call x1, Pallas kernels, cut_patches(): pl.pallas_call(cut_kernel, out_shape=jax.ShapeDtypeStruct((count, BOX, BO...  20.7 us
    all_to_all x1, blocking collectives, per_device(): lax.all_to_all(wanted, 'dev', split_axis=0, concat_axis=0, tiled=True)  14.3 us
    all_to_all x1, waiting for transfers between devices, per_device(): lax.all_to_all(patches_cut, 'dev', split_axis=0, concat_axis=0, tiled=True)  13.3 us
    unnamed x8, local copies, waits for them, and re-layouts  4.97 us
    transpose x1, local copies, waits for them, and re-layouts, per_device(): ref_three = whole_refs.reshape(CLASSES, BOX, ROTS, CYCLES).transpose(0, 2...  4.9 us
    all_to_all x1, starting transfers between devices, per_device(): lax.all_to_all(placed, 'dev', split_axis=1, concat_axis=0, tiled=True)  3.37 us
    dot_general x1, matrix products, per_device(): jnp.einsum('pfm,cgm->pcfg', cyl_three, ref_three, preferred_element_type=...  3.04 us
  transfers between devices with their start and end apart: 3, of which 2 were waited for; matrix products, arithmetic and copies ran while one was open for 15% of the time, Pallas kernels for 0%

profile of v1, /device:TPU:0, one launch (start us, length us, event | category | flops | bytes accessed | tf_op | source)
XLA Modules:
  0.0 136.5 jit_solution(13184590323433606233)
XLA Ops:
  7.2 0.7 copy.65
  7.9 0.1 copy.46
  8.0 0.1 fusion.8
  8.1 0.2 select_reduce_fusion
  8.3 2.1 %scatter_fusion = s32[32,2,3]{2,1,0:T(2,128)S(1)} fusion(s32[32,2,3]{2,1,0:T(2,128)S(1)} %broadcast_in_dim.8, s32[21]{0:T(128)S(1)} %get-tuple-element.4, s32[21,3]{1,0:T(8,128)S(1)} %copy.46), kind=kCustom, calls=%fused_computation.2 | custom fusion | bytes 924 | tf_op jit(solution)/shard_map/scatter | solution.py:121
  10.4 14.3 %all_to_all.19 = s32[32,2,3]{2,1,0:T(2,128)S(1)} all-to-all(s32[32,2,3]{2,1,0:T(2,128)S(1)} %scatter_fusion), channel_id=1, replica_groups=mesh['dev'=32] {'dev'}, dimensions={0} | all-to-all | bytes 1536 | tf_op jit(solution)/shard_map/all_to_all | solution.py:123
  24.8 0.7 reshape_reshape.6.req_ref
  25.5 20.7 %shard_map.86 = bf16[64,64,64]{2,1,0:T(8,128)(2,1)} custom-call(s32[192]{0:T(256)} %reshape_reshape.6.req_ref, bf16[2,128,4096]{2,1,0:T(8,128)(2,1)} %tiles_ref.1), custom_call_target="tpu_custom_call" | custom-call | tf_op jit(solution)/shard_map/pallas_call | solution.py:95
  46.2 3.0 %reshape.328 = bf16[32,2,4096]{2,1,0:T(2,128)(2,1)} reshape(bf16[32,2,64,64]{3,2,1,0:T(8,128)(2,1)} %bitcast.58) | data formatting | bytes 1048576
  49.2 2.6 %all-to-all-start.1 = ((bf16[32,2,4096]{2,1,0:T(2,128)(2,1)}), bf16[32,2,4096]{2,1,0:T(2,128)(2,1)S(1)}, u32[]{:S(2)}, u32[]{:S(2)}) async-start(bf16[32,2,4096]{2,1,0:T(2,128)(2,1)} %reshape.328), calls=%async_computation.1 | async-start | bytes 1048576 | tf_op jit(solution)/shard_map/all_to_all | solution.py:125
  51.8 0.0 all-gather.2.cloned.1.call-start
  51.9 0.7 all-gather.2.cloned.1.call-update
  53.9 0.1 mul.67
  54.0 0.1 mul.68
  54.1 0.0 copy-start.1
  54.1 13.3 %all-to-all-done.1 = bf16[32,2,4096]{2,1,0:T(2,128)(2,1)S(1)} async-done(((bf16[32,2,4096]{2,1,0:T(2,128)(2,1)}), bf16[32,2,4096]{2,1,0:T(2,128)(2,1)S(1)}, u32[]{:S(2)}, u32[]{:S(2)}) %all-to-all-start.1) | async-done | bytes 524320 | tf_op jit(solution)/shard_map/all_to_all | solution.py:125
  67.4 0.7 reshape.329
  68.1 0.7 gather_fusion
  68.8 0.0 copy-start
  68.8 0.2 copy.61
  69.0 0.1 pad.4.clone
  69.1 0.3 reshape.295
  69.4 0.0 copy-done.1
  69.4 0.4 fusion.14
  69.8 0.4 copy-done
  70.1 1.0 multiply_reduce_fusion.1
  71.1 0.1 copy.48
  71.2 1.3 gather_fusion.1
  72.6 0.1 select_bitcast_fusion
  72.7 0.1 copy.56
  72.8 0.1 mul.71
  72.9 1.2 broadcast_multiply_fusion
  74.1 3.4 %all-to-all-start.2 = ((bf16[1,32,32,512]{3,2,0,1:T(8,128)(2,1)}), bf16[1,32,32,512]{3,2,0,1:T(8,128)(2,1)}, u32[]{:S(2)}, u32[]{:S(2)}) async-start(bf16[1,32,32,512]{3,2,0,1:T(8,128)(2,1)} %broadcast_multiply_fusion), calls=%async_computation.2 | async-start | bytes 2097152 | tf_op jit(solution)/shard_map/all_to_all | solution.py:168
  77.5 0.3 copy.49
  78.4 35.5 %all-gather.2.cloned.1.call-done = bf16[1024,512]{1,0:T(8,128)(2,1)} async-done(((bf16[32,512]{1,0:T(8,128)(2,1)}), bf16[1024,512]{1,0:T(8,128)(2,1)}) %all-gather.2.cloned.1.call-update) | async-done | bytes 1048592 | tf_op jit(solution)/shard_map/all_gather | solution.py:137
  113.9 1.5 %multiply_reduce_fusion = f32[1024]{0:T(1024)S(1)} fusion(bf16[1024,512]{1,0:T(8,128)(2,1)} %all-gather.2.cloned.1.call-done), kind=kLoop, calls=%fused_computation.4 | loop fusion | flops 1571840 | bytes 1052672 | tf_op jit(solution)/shard_map/reduce_sum | solution.py:144
  115.4 0.1 reduce_sum.49
  115.5 1.5 %copy.50 = bf16[1024,512]{0,1:T(8,128)(2,1)S(1)} copy(bf16[1024,512]{1,0:T(8,128)(2,1)} %all-gather.2.cloned.1.call-done) | data formatting | bytes 2097152 | tf_op jit(solution)/shard_map/all_gather | solution.py:137
  117.0 1.3 reshape.297
  118.4 4.9 %copy.51 = bf16[16,32,64,16]{1,3,2,0:T(8,128)(2,1)} copy(bf16[16,32,64,16]{2,0,3,1:T(8,128)(2,1)S(1)} %bitcast.55) | data formatting | bytes 2097152 | tf_op jit(solution)/shard_map/transpose | solution.py:140
  123.3 0.1 reduce_sum.50
  123.4 3.0 %convolution_bitcast_fusion = f32[16,32,32]{2,1,0:T(8,128)S(1)} fusion(bf16[32,1024,1]{0,1,2:T(8,128)(2,1)S(1)} %bitcast.60, bf16[16,32,1024]{1,2,0:T(8,128)(2,1)} %bitcast.54), kind=kOutput, calls=%fused_computation.5 | convolution fusion | flops 33554432 | bytes 1179648 | tf_op jit(solution)/shard_map/pfm,cgm->pcfg/dot_general | solution.py:150
  126.4 0.5 fusion.1
  126.9 0.7 reshape.300
  127.6 0.0 all-to-all-done.2
  127.6 2.0 %convert_reduce_fusion = f32[32,512]{1,0:T(8,128)} fusion(bf16[1,32,32,512]{3,2,0,1:T(8,128)(2,1)} %all-to-all-done.2), kind=kLoop, calls=%fused_computation.3 | loop fusion | flops 1032192 | bytes 1114112 | tf_op jit(solution)/shard_map/reduce_sum | solution.py:169
  (12 shorter events, 0.2 us)
Async XLA Ops:
  49.2 18.2 %all-to-all-start.1 = ((bf16[32,2,4096]{2,1,0:T(2,128)(2,1)}), bf16[32,2,4096]{2,1,0:T(2,128)(2,1)S(1)}, u32[]{:S(2)}, u32[]{:S(2)}) async-start(bf16[32,2,4096]{2,1,0:T(2,128)(2,1)} %reshape.328), calls=%async_computation.1 | async-start | bytes 1048576 | tf_op jit(solution)/shard_map/all_to_all | solution.py:125
  51.8 62.1 %all-gather.2.cloned.1.call-start = ((), (), s32[]{:S(2)}) async-start(), calls=%async_computation.3 | async-start | bytes 1081344 | tf_op jit(solution)/shard_map/all_gather | solution.py:137
  54.1 15.3 %copy-start.1 = (bf16[1408,512]{1,0:T(8,128)(2,1)S(1)}, bf16[1408,512]{1,0:T(8,128)(2,1)}, u32[]{:S(2)}) copy-start(bf16[1408,512]{1,0:T(8,128)(2,1)} %constant.93.clone) | copy-start | bytes 4325380
  68.8 1.4 %copy-start = (bf16[1408,512]{1,0:T(8,128)(2,1)S(1)}, bf16[1408,512]{1,0:T(8,128)(2,1)}, u32[]{:S(2)}) copy-start(bf16[1408,512]{1,0:T(8,128)(2,1)} %constant.94.clone) | copy-start | bytes 4325380
  74.1 53.5 %all-to-all-start.2 = ((bf16[1,32,32,512]{3,2,0,1:T(8,128)(2,1)}), bf16[1,32,32,512]{3,2,0,1:T(8,128)(2,1)}, u32[]{:S(2)}, u32[]{:S(2)}) async-start(bf16[1,32,32,512]{3,2,0,1:T(8,128)(2,1)} %broadcast_multiply_fusion), calls=%async_computation.2 | async-start | bytes 2097152 | tf_op jit(solution)/shard_map/all_to_all | solution.py:168
Sparse Core Ops, SparseCore 0:
  55.5 58.3 all-gather.1

commit v2 on v1

--- a/solution.py
+++ b/solution.py
@@ -48,13 +48,37 @@
 
 
 @functools.lru_cache(maxsize=None)
-def folded_matrix(count):
-    back = back_matrix_np(count).astype(np.float64)
-    sample = cyl_matrix_np().astype(np.float64)
-    full = back @ sample
-    high = full.astype(ml_dtypes.bfloat16)
-    low = (full - high.astype(np.float64)).astype(ml_dtypes.bfloat16)
-    return np.asarray(high), np.asarray(low)
+def touched_points():
+    sample = cyl_matrix_np().astype(np.float32)
+    used = np.nonzero(np.abs(sample).sum(axis=1))[0]
+    size = -(-len(used) // 128) * 128
+    xs = np.full((size,), -100.0, np.float32)
+    zs = np.full((size,), -100.0, np.float32)
+    xs[: len(used)] = used // BOX
+    zs[: len(used)] = used % BOX
+    return xs, zs
+
+
+def back_points(count, xs, zs):
+    center = (BOX - 1) / 2.0
+    tilt = jnp.arange(count, dtype=jnp.float32)[:, None, None]
+    pixel = jnp.arange(BOX, dtype=jnp.float32)[None, :, None]
+    theta = (-60.0 + 120.0 * tilt / (TILTS - 1)) * (jnp.pi / 180.0)
+    place = (xs[None, None, :] - center) * jnp.cos(theta) + (zs[None, None, :] - center) * jnp.sin(
+        theta
+    ) + center
+    weight = jnp.maximum(0.0, 1.0 - jnp.abs(place - pixel))
+    weight = jnp.where(tilt < TILTS, weight, 0.0) / TILTS
+    return weight.reshape(count * BOX, xs.shape[0]).astype(jnp.bfloat16)
+
+
+def sample_points(xs, zs):
+    center = (BOX - 1) / 2.0
+    angle = jnp.arange(ROTS, dtype=jnp.float32)[None, :, None] * (2.0 * jnp.pi / ROTS)
+    radius = (jnp.arange(CYCLES, dtype=jnp.float32)[None, None, :] + 0.5) * (BOX / (2.0 * CYCLES))
+    wx = jnp.maximum(0.0, 1.0 - jnp.abs(xs[:, None, None] - center - radius * jnp.cos(angle)))
+    wz = jnp.maximum(0.0, 1.0 - jnp.abs(zs[:, None, None] - center - radius * jnp.sin(angle)))
+    return (wx * wz).reshape(xs.shape[0], ROTS * CYCLES).astype(jnp.bfloat16)
 
 
 def shift_table():
@@ -100,6 +124,11 @@
             grid=(1,),
             in_specs=[pl.BlockSpec(tiles.shape, lambda i, q: (0, 0, 0))],
             out_specs=pl.BlockSpec((count, BOX, BOX), lambda i, q: (0, 0, 0)),
+        ),
+        cost_estimate=pl.CostEstimate(
+            flops=count * 2 * BOX * WIN * (tiles.shape[1] + BOX),
+            transcendentals=0,
+            bytes_accessed=tiles.size * 2 + count * BOX * BOX * 2,
         ),
     )(flat, tiles)
 
@@ -129,26 +158,26 @@
     pmat = jnp.pad(pmat, ((0, 0), (0, 0), (0, padded - TILTS), (0, 0))).reshape(
         count * BOX, padded * BOX
     )
-    high, low = folded_matrix(padded)
-    cyl = jnp.dot(pmat, jnp.asarray(high), preferred_element_type=jnp.float32) + jnp.dot(
-        pmat, jnp.asarray(low), preferred_element_type=jnp.float32
-    )
+    xs_np, zs_np = touched_points()
+    xs, zs = jnp.asarray(xs_np), jnp.asarray(zs_np)
+    volume = jnp.dot(pmat, back_points(padded, xs, zs), preferred_element_type=jnp.float32)
+    volume = volume.astype(jnp.bfloat16)
+    cyl = jnp.dot(volume, sample_points(xs, zs), preferred_element_type=jnp.float32)
     cyl = cyl.astype(jnp.bfloat16).reshape(count, BOX, ROTS * CYCLES)
-    whole_refs = lax.all_gather(references, "dev", axis=0, tiled=True)
-    ref_three = (
-        whole_refs.reshape(CLASSES, BOX, ROTS, CYCLES)
-        .transpose(0, 2, 1, 3)
-        .reshape(CLASSES, ROTS, BOX * CYCLES)
-    )
-    ref_float = whole_refs.astype(jnp.float32).reshape(CLASSES, BOX * ROTS * CYCLES)
-    ref_power = jnp.mean(ref_float * ref_float, axis=1)
+    owned = references.shape[0]
+    local_t = references.reshape(owned, ROTS, CYCLES).transpose(1, 0, 2).reshape(ROTS, owned * CYCLES)
+    gathered = lax.all_gather(local_t, "dev", axis=1, tiled=True).reshape(
+        ROTS, CLASSES, BOX * CYCLES
+    )
+    ref_float = gathered.astype(jnp.float32)
+    ref_power = jnp.mean(ref_float * ref_float, axis=(0, 2))
     cyl_three = (
         cyl.reshape(count, BOX, ROTS, CYCLES)
         .transpose(0, 2, 1, 3)
         .reshape(count, ROTS, BOX * CYCLES)
     )
-    corr = jnp.einsum("pfm,cgm->pcfg", cyl_three, ref_three, preferred_element_type=jnp.float32)
-    raw = jnp.einsum("pcfg,kfg->pck", corr, shift_table(), precision=lax.Precision.HIGHEST)
+    corr = jnp.einsum("pfm,gcm->pfgc", cyl_three, gathered, preferred_element_type=jnp.float32)
+    raw = jnp.einsum("pfgc,kfg->pck", corr, shift_table(), precision=lax.Precision.HIGHEST)
     cyl_float = cyl.astype(jnp.float32)
     power = jnp.mean(cyl_float.reshape(count, -1) ** 2, axis=1)
     total = BOX * ROTS * CYCLES
@@ -162,7 +191,6 @@
     member = (classes[:, None] == jnp.arange(CLASSES, dtype=jnp.int32)[None, :]).astype(
         jnp.bfloat16
     )
-    owned = CLASSES * BOX // ndev
     placed = member[:, :, None, None] * turned[:, None, :, :]
     placed = placed.reshape(count, ndev, owned, ROTS * CYCLES)
     landed = lax.all_to_all(placed, "dev", split_axis=1, concat_axis=0, tiled=True)

time: 137 us -> 121 us (0.88)
  waiting for transfers between devices: 49.4 us -> 33.5 us
  blocking collectives: 14.3 us -> 0 us
  starting transfers between devices: 6.02 us -> 13.5 us
  other arithmetic: 5.32 us -> 12 us
  matrix products: 4.9 us -> 8.53 us
  local copies, waits for them, and re-layouts: 19.5 us -> 16 us
    all_gather x1, waiting for transfers between devices: 35.5 us -> 3.91 us  [per_device(): lax.all_gather(local_t, 'dev', axis=1, tiled=True)]
    all_to_all x1 -> x0, blocking collectives: 14.3 us -> none  [per_device(): lax.all_to_all(wanted, 'dev', split_axis=0, concat_axis=0, tiled=True)]
    all_to_all x1, waiting for transfers between devices: 0.01 us -> 13.1 us  [per_device(): lax.all_to_all(placed, 'dev', split_axis=1, concat_axis=0, tiled=True)]
    all_to_all x0 -> x1, starting transfers between devices: none -> 7.3 us  [per_device(): lax.all_to_all(wanted, 'dev', split_axis=0, concat_axis=0, tiled=True)]
    convert_element_type x0 -> x1, other arithmetic: none -> 4.47 us  [back_points(): return weight.reshape(count * BOX, xs.shape[0]).astype(jnp.bfloat16)]
    transpose x1, local copies, waits for them, and re-layouts: 4.9 us -> 0.84 us  [per_device(): references.reshape(owned, ROTS, CYCLES).transpose(1, 0, 2)]
    dot_general x4 -> x3, matrix products: 4.9 us -> 8.53 us  [the longest x1 4.98 us: per_device(): jnp.dot(volume, sample_points(xs, zs), preferred_element_type=jnp.float32)]
    all_to_all x0 -> x1, waiting for transfers between devices: none -> 3.4 us  [per_device(): lax.all_to_all(wanted, 'dev', split_axis=0, concat_axis=0, tiled=True)]
  transfers between devices with their start and end apart: 3 -> 4, of which waited for: 2 -> 4; matrix products, arithmetic and copies ran while one was open for 15% -> 25% of each run, Pallas kernels for 0% -> 17%
where the time goes in v2:
time: 121 us; the launch traced here: 120 us
  waiting for transfers between devices  33.5 us (28%)
  Pallas kernels  20.7 us (17%)
  between operations  16.2 us (13%)
  local copies, waits for them, and re-layouts  16 us (13%)
  starting transfers between devices  13.5 us (11%)
  other arithmetic  12 us (10%)
  matrix products  8.53 us (7%)
    pallas_call x1, Pallas kernels, cut_patches(): pl.pallas_call(cut_kernel, out_shape=jax.ShapeDtypeStruct((count, BOX, BO...  20.7 us
    all_to_all x1, waiting for transfers between devices, per_device(): lax.all_to_all(placed, 'dev', split_axis=1, concat_axis=0, tiled=True)  13.1 us
    all_to_all x1, waiting for transfers between devices, per_device(): lax.all_to_all(patches_cut, 'dev', split_axis=0, concat_axis=0, tiled=True)  13.1 us
    all_to_all x1, starting transfers between devices, per_device(): lax.all_to_all(wanted, 'dev', split_axis=0, concat_axis=0, tiled=True)  7.3 us
    unnamed x9, local copies, waits for them, and re-layouts  5.49 us
    dot_general x1, matrix products, per_device(): jnp.dot(volume, sample_points(xs, zs), preferred_element_type=jnp.float32)  4.98 us
    convert_element_type x1, other arithmetic, back_points(): return weight.reshape(count * BOX, xs.shape[0]).astype(jnp.bfloat16)  4.47 us
    reduce_sum x2, other arithmetic, per_device(): ref_power = jnp.mean(ref_float * ref_float, axis=(0, 2))  4.04 us
  transfers between devices with their start and end apart: 4, of which 4 were waited for; matrix products, arithmetic and copies ran while one was open for 25% of the time, Pallas kernels for 17%

profile of v2, /device:TPU:0, one launch (start us, length us, event | category | flops | bytes accessed | tf_op | source)
XLA Modules:
  0.0 120.4 jit_solution(4212594700814050197)
XLA Ops:
  7.2 0.7 copy.73
  7.9 0.1 fusion.9
  8.0 0.2 select_reduce_fusion
  8.2 0.1 copy.52
  8.3 0.6 broadcast_in_dim.14
  8.9 4.0 %scatter_fusion = s32[32,2,3]{2,1,0:T(2,128)} fusion(s32[32,2,3]{2,1,0:T(2,128)} %broadcast_in_dim.14, s32[21]{0:T(128)S(1)} %get-tuple-element.4, s32[21,3]{1,0:T(8,128)S(1)} %copy.52), kind=kCustom, calls=%fused_computation.2 | custom fusion | bytes 924 | tf_op jit(solution)/shard_map/scatter | solution.py:150
  12.9 7.3 %all-to-all-start = ((s32[32,2,3]{2,1,0:T(2,128)}), s32[32,2,3]{2,1,0:T(2,128)S(1)}, u32[]{:S(2)}, u32[]{:S(2)}) async-start(s32[32,2,3]{2,1,0:T(2,128)} %scatter_fusion), calls=%async_computation | async-start | bytes 65536 | tf_op jit(solution)/shard_map/all_to_all | solution.py:152
  20.2 0.0 all-gather.2.cloned.1.call-start
  20.3 0.9 copy.56
  21.1 0.8 copy.57
  22.0 0.0 all-gather.2.cloned.1.call-update
  22.2 0.1 mul.199
  22.2 0.1 mul.202
  22.3 0.1 mul.203
  22.4 0.1 mul.205
  22.5 0.1 mul.206
  22.6 0.8 add_add_fusion
  24.1 3.4 %all-to-all-done = s32[32,2,3]{2,1,0:T(2,128)S(1)} async-done(((s32[32,2,3]{2,1,0:T(2,128)}), s32[32,2,3]{2,1,0:T(2,128)S(1)}, u32[]{:S(2)}, u32[]{:S(2)}) %all-to-all-start) | async-done | bytes 800 | tf_op jit(solution)/shard_map/all_to_all | solution.py:152
  27.5 0.7 reshape_reshape.6.req_ref
  28.2 20.7 %shard_map.86 = bf16[64,64,64]{2,1,0:T(8,128)(2,1)} custom-call(s32[192]{0:T(256)} %reshape_reshape.6.req_ref, bf16[2,128,4096]{2,1,0:T(8,128)(2,1)} %tiles_ref.1), custom_call_target="tpu_custom_call" | custom-call | flops 402653184 | bytes 2621440 | tf_op jit(solution)/shard_map/pallas_call | solution.py:119
  48.9 3.0 %reshape.550 = bf16[32,2,4096]{2,1,0:T(2,128)(2,1)} reshape(bf16[32,2,64,64]{3,2,1,0:T(8,128)(2,1)} %bitcast.53) | data formatting | bytes 1048576
  51.9 2.6 %all-to-all-start.1 = ((bf16[32,2,4096]{2,1,0:T(2,128)(2,1)}), bf16[32,2,4096]{2,1,0:T(2,128)(2,1)S(1)}, u32[]{:S(2)}, u32[]{:S(2)}) async-start(bf16[32,2,4096]{2,1,0:T(2,128)(2,1)} %reshape.550), calls=%async_computation.1 | async-start | bytes 1048576 | tf_op jit(solution)/shard_map/all_to_all | solution.py:154
  55.2 0.0 copy-start
  55.3 0.0 copy-start.1
  55.3 4.5 %multiply_convert_fusion = bf16[22,64,1664]{2,1,0:T(8,128)(2,1)} fusion(f32[22,1664]{1,0:T(8,128)S(1)} %add_add_fusion, pred[22]{0:T(512)(128)(4,1)S(1)} %iota_compare_fusion.3), kind=kLoop, calls=%fused_computation.3 | loop fusion | flops 16400384 | bytes 4832278 | tf_op jit(solution)/shard_map/convert_element_type | solution.py:72
  59.7 0.1 mul.213
  59.8 0.1 mul.214
  59.9 13.1 %all-to-all-done.1 = bf16[32,2,4096]{2,1,0:T(2,128)(2,1)S(1)} async-done(((bf16[32,2,4096]{2,1,0:T(2,128)(2,1)}), bf16[32,2,4096]{2,1,0:T(2,128)(2,1)S(1)}, u32[]{:S(2)}, u32[]{:S(2)}) %all-to-all-start.1) | async-done | bytes 524320 | tf_op jit(solution)/shard_map/all_to_all | solution.py:154
  73.0 0.7 reshape.551
  73.7 0.7 gather_fusion
  74.4 0.2 copy.69
  74.6 0.1 pad.4.clone
  74.7 0.3 reshape.517
  75.0 0.0 copy-done
  75.0 0.0 copy-done.1
  75.0 5.0 %multiply_reduce_fusion.1 = (f32[]{:T(128)}, bf16[64,512]{1,0:T(8,128)(2,1)S(1)}) fusion(f32[512]{0:T(512)S(1)} %get-tuple-element.7, f32[1664]{0:T(1024)S(1)} %copy-done.1, f32[512]{0:T(512)S(1)} %get-tuple-element.6, f32[1664]{0:T(1024)S(1)} %copy-done, bf16[64,1408]{1,0:T(8,128)(2,1)S(1)} %reshape.517, bf16[1408,1664]{1,0:T(8,128)(2,1)} %bitcast.51), kind=kOutput, calls=%fused_computation.18 | convolution fusion | flops 417701888 | bytes 4948996 | tf_op jit(solution)/shard_map/dot_general | solution.py:165
  80.0 0.1 copy.54
  80.1 1.3 %gather_fusion.1 = bf16[512,64]{1,0:T(8,128)(2,1)S(1)} fusion(bf16[64,512]{0,1:T(8,128)(2,1)S(1)} %copy.54, s32[1024]{0:T(1024)S(1)} %pad_clamp_fusion), kind=kCustom, calls=%fused_computation.1 | custom fusion | bytes 133120 | tf_op jit(solution)/shard_map/jit(take_along_axis)/gather | solution.py:190
  81.5 0.1 select_bitcast_fusion
  81.6 0.1 copy.63
  81.7 0.1 mul.217
  81.8 1.1 broadcast_multiply_fusion
  83.0 3.5 %all-to-all-start.2 = ((bf16[1,32,32,512]{3,2,0,1:T(8,128)(2,1)}), bf16[1,32,32,512]{3,2,0,1:T(8,128)(2,1)S(1)}, u32[]{:S(2)}, u32[]{:S(2)}) async-start(bf16[1,32,32,512]{3,2,0,1:T(8,128)(2,1)} %broadcast_multiply_fusion), calls=%async_computation.2 | async-start | bytes 2097152 | tf_op jit(solution)/shard_map/all_to_all | solution.py:196
  86.5 0.3 copy.55
  87.4 3.9 %all-gather.2.cloned.1.call-done = bf16[32,16384]{0,1:T(8,128)(2,1)} async-done(((bf16[32,512]{0,1:T(8,128)(2,1)}), bf16[32,16384]{0,1:T(8,128)(2,1)}) %all-gather.2.cloned.1.call-update) | async-done | bytes 1048592 | tf_op jit(solution)/shard_map/all_gather | solution.py:169
  91.4 3.9 %multiply_reduce_fusion = f32[16384]{0:T(1024)S(1)} fusion(bf16[32,16384]{0,1:T(8,128)(2,1)} %all-gather.2.cloned.1.call-done), kind=kLoop, calls=%fused_computation.4 | loop fusion | flops 1556480 | bytes 1114112 | tf_op jit(solution)/shard_map/reduce_sum | solution.py:173
  95.3 0.1 reduce_sum.50
  95.4 3.0 %fusion.22 = f32[32,32,16]{1,0,2:T(8,128)S(1)} fusion(bf16[32,1024,1]{0,1,2:T(8,128)(2,1)S(1)} %bitcast.55, bf16[32,16,1024]{0,2,1:T(8,128)(2,1)} %bitcast.49), kind=kOutput, calls=%fused_computation.68 | convolution fusion | flops 33554432 | bytes 1179648 | tf_op jit(solution)/shard_map/pfm,gcm->pfgc/dot_general | solution.py:179
  98.5 0.5 fusion.2
  99.0 0.7 reshape.522
  99.7 13.1 %all-to-all-done.2 = bf16[1,32,32,512]{3,2,0,1:T(8,128)(2,1)S(1)} async-done(((bf16[1,32,32,512]{3,2,0,1:T(8,128)(2,1)}), bf16[1,32,32,512]{3,2,0,1:T(8,128)(2,1)S(1)}, u32[]{:S(2)}, u32[]{:S(2)}) %all-to-all-start.2) | async-done | bytes 1048608 | tf_op jit(solution)/shard_map/all_to_all | solution.py:196
  112.8 0.8 convert_reduce_fusion
  (19 shorter events, 0.3 us)
Async XLA Ops:
  12.9 14.6 %all-to-all-start = ((s32[32,2,3]{2,1,0:T(2,128)}), s32[32,2,3]{2,1,0:T(2,128)S(1)}, u32[]{:S(2)}, u32[]{:S(2)}) async-start(s32[32,2,3]{2,1,0:T(2,128)} %scatter_fusion), calls=%async_computation | async-start | bytes 65536 | tf_op jit(solution)/shard_map/all_to_all | solution.py:152
  20.2 71.2 %all-gather.2.cloned.1.call-start = ((), (), s32[]{:S(2)}) async-start(), calls=%async_computation.3 | async-start | bytes 4325376 | tf_op jit(solution)/shard_map/all_gather | solution.py:169
  51.9 21.1 %all-to-all-start.1 = ((bf16[32,2,4096]{2,1,0:T(2,128)(2,1)}), bf16[32,2,4096]{2,1,0:T(2,128)(2,1)S(1)}, u32[]{:S(2)}, u32[]{:S(2)}) async-start(bf16[32,2,4096]{2,1,0:T(2,128)(2,1)} %reshape.550), calls=%async_computation.1 | async-start | bytes 1048576 | tf_op jit(solution)/shard_map/all_to_all | solution.py:154
  55.2 19.8 %copy-start = (f32[1664]{0:T(1024)S(1)}, f32[1664]{0:T(1024)}, u32[]{:S(2)}) copy-start(f32[1664]{0:T(1024)} %constant.136) | copy-start | bytes 19972
  55.3 19.8 %copy-start.1 = (f32[1664]{0:T(1024)S(1)}, f32[1664]{0:T(1024)}, u32[]{:S(2)}) copy-start(f32[1664]{0:T(1024)} %constant.137) | copy-start | bytes 19972
  83.0 29.8 %all-to-all-start.2 = ((bf16[1,32,32,512]{3,2,0,1:T(8,128)(2,1)}), bf16[1,32,32,512]{3,2,0,1:T(8,128)(2,1)S(1)}, u32[]{:S(2)}, u32[]{:S(2)}) async-start(bf16[1,32,32,512]{3,2,0,1:T(8,128)(2,1)} %broadcast_multiply_fusion), calls=%async_computation.2 | async-start | bytes 2097152 | tf_op jit(solution)/shard_map/all_to_all | solution.py:196
Sparse Core Ops, SparseCore 0:
  23.9 67.4 all-gather.1

commit v3 on v2

--- a/solution.py
+++ b/solution.py
@@ -91,23 +91,18 @@
     count = out_ref.shape[0]
     width = tiles_ref.shape[2]
     rows = tiles_ref.shape[1]
-    row_i = lax.broadcasted_iota(jnp.int32, (BOX, rows), 0)
-    row_j = lax.broadcasted_iota(jnp.int32, (BOX, rows), 1)
-    col_v = lax.broadcasted_iota(jnp.int32, (WIN, BOX), 0)
-    col_u = lax.broadcasted_iota(jnp.int32, (WIN, BOX), 1)
+    span = BOX + 16
 
     def body(k, carry):
         t = req_ref[3 * k]
         r = req_ref[3 * k + 1]
         c = req_ref[3 * k + 2]
-        c0 = jnp.minimum((c // 128) * 128, width - WIN)
-        c0 = pl.multiple_of(c0, 128)
-        win = tiles_ref[t, :, pl.ds(c0, WIN)]
-        pick_rows = (row_j == row_i + r).astype(jnp.bfloat16)
-        part = jnp.dot(pick_rows, win, preferred_element_type=jnp.float32)
-        pick_cols = (col_v == col_u + (c - c0)).astype(jnp.bfloat16)
-        cut = jnp.dot(part.astype(jnp.bfloat16), pick_cols, preferred_element_type=jnp.float32)
-        out_ref[k] = cut.astype(out_ref.dtype)
+        r0 = pl.multiple_of(jnp.minimum((r // 16) * 16, rows - span), 16)
+        c0 = pl.multiple_of(jnp.minimum((c // 128) * 128, width - WIN), 128)
+        win = tiles_ref[t, pl.ds(r0, span), pl.ds(c0, WIN)].astype(jnp.float32)
+        win = pltpu.roll(win, (span - (r - r0)) % span, 0)
+        win = pltpu.roll(win, (WIN - (c - c0)) % WIN, 1)
+        out_ref[k] = win[:BOX, :BOX].astype(out_ref.dtype)
         return carry
 
     lax.fori_loop(0, count, body, 0)
@@ -126,7 +121,7 @@
             out_specs=pl.BlockSpec((count, BOX, BOX), lambda i, q: (0, 0, 0)),
         ),
         cost_estimate=pl.CostEstimate(
-            flops=count * 2 * BOX * WIN * (tiles.shape[1] + BOX),
+            flops=count * BOX * WIN * 64,
             transcendentals=0,
             bytes_accessed=tiles.size * 2 + count * BOX * BOX * 2,
         ),
@@ -144,14 +139,15 @@
     local = flat[:, 0] - owner * held
     hits = (owner[:, None] == jnp.arange(ndev, dtype=jnp.int32)[None, :]).astype(jnp.int32)
     slot = jnp.sum((jnp.cumsum(hits, axis=0) - hits) * hits, axis=1)
-    wanted = (
-        jnp.zeros((ndev, cap, 3), jnp.int32)
-        .at[owner, slot]
-        .set(jnp.stack([local, flat[:, 1], flat[:, 2]], axis=-1))
-    )
+    values = jnp.stack([local, flat[:, 1], flat[:, 2]], axis=-1)
+    spot = (owner[None, None, :] == jnp.arange(ndev, dtype=jnp.int32)[:, None, None]) & (
+        slot[None, None, :] == jnp.arange(cap, dtype=jnp.int32)[None, :, None]
+    )
+    wanted = jnp.sum(jnp.where(spot[..., None], values[None, None], 0), axis=2)
     asked = lax.all_to_all(wanted, "dev", split_axis=0, concat_axis=0, tiled=True)
-    patches_cut = cut_patches(tiles, asked.reshape(ndev * cap, 3)).reshape(ndev, cap, BOX, BOX)
+    patches_cut = cut_patches(tiles, asked.reshape(ndev * cap, 3)).reshape(ndev, cap * BOX, BOX)
     arrived = lax.all_to_all(patches_cut, "dev", split_axis=0, concat_axis=0, tiled=True)
+    arrived = arrived.reshape(ndev, cap, BOX, BOX)
     patch = arrived[owner, slot].reshape(count, TILTS, BOX, BOX)
     padded = TILTS + TILTS % 2
     pmat = patch.transpose(0, 2, 1, 3)

time: 121 us -> 113 us (0.934)
  Pallas kernels: 20.7 us -> 10.6 us
  waiting for transfers between devices: 33.5 us -> 41 us
  local copies, waits for them, and re-layouts: 16 us -> 11.3 us
    all_gather x1, waiting for transfers between devices: 3.91 us -> 17.8 us  [per_device(): lax.all_gather(local_t, 'dev', axis=1, tiled=True)]
    pallas_call x1, Pallas kernels: 20.7 us -> 10.6 us  [cut_patches(): pl.pallas_call(cut_kernel, out_shape=jax.ShapeDtypeStruct((count, BOX, BO...]
    all_to_all x1, waiting for transfers between devices: 13.1 us -> 4.59 us  [per_device(): lax.all_to_all(placed, 'dev', split_axis=1, concat_axis=0, tiled=True)]
    scatter x1 -> x0, local copies, waits for them, and re-layouts: 3.98 us -> none  [per_device(): wanted = jnp.zeros((ndev, cap, 3), jnp.int32).at[owner, slot].set(jnp.sta...]
    unnamed x9 -> x7, local copies, waits for them, and re-layouts: 5.49 us -> 1.81 us
    reshape x0 -> x1, local copies, waits for them, and re-layouts: none -> 2.42 us  [per_device(): cut_patches(tiles, asked.reshape(ndev * cap, 3))]
    all_to_all x1, waiting for transfers between devices: 13.1 us -> 15.1 us  [per_device(): lax.all_to_all(patches_cut, 'dev', split_axis=0, concat_axis=0, tiled=True)]
  transfers between devices with their start and end apart: 4 -> 4, of which waited for: 4 -> 4; matrix products, arithmetic and copies ran while one was open for 25% -> 26% of each run, Pallas kernels for 17% -> 9%
where the time goes in v3:
time: 113 us
  waiting for transfers between devices  41 us (36%)
  between operations  16.2 us (14%)
  starting transfers between devices  12.7 us (11%)
  other arithmetic  12.3 us (11%)
  local copies, waits for them, and re-layouts  11.3 us (10%)
  Pallas kernels  10.6 us (9%)
  matrix products  8.51 us (8%)
    all_gather x1, waiting for transfers between devices, per_device(): lax.all_gather(local_t, 'dev', axis=1, tiled=True)  17.8 us
    all_to_all x1, waiting for transfers between devices, per_device(): lax.all_to_all(patches_cut, 'dev', split_axis=0, concat_axis=0, tiled=True)  15.1 us
    pallas_call x1, Pallas kernels, cut_patches(): pl.pallas_call(cut_kernel, out_shape=jax.ShapeDtypeStruct((count, BOX, BO...  10.6 us
    all_to_all x1, starting transfers between devices, per_device(): lax.all_to_all(wanted, 'dev', split_axis=0, concat_axis=0, tiled=True)  7.3 us
    dot_general x1, matrix products, per_device(): jnp.dot(volume, sample_points(xs, zs), preferred_element_type=jnp.float32)  4.97 us
    all_to_all x1, waiting for transfers between devices, per_device(): lax.all_to_all(placed, 'dev', split_axis=1, concat_axis=0, tiled=True)  4.59 us
    convert_element_type x1, other arithmetic, back_points(): return weight.reshape(count * BOX, xs.shape[0]).astype(jnp.bfloat16)  4.47 us
    reduce_sum x2, other arithmetic, per_device(): ref_power = jnp.mean(ref_float * ref_float, axis=(0, 2))  4.04 us
  transfers between devices with their start and end apart: 4, of which 4 were waited for; matrix products, arithmetic and copies ran while one was open for 26% of the time, Pallas kernels for 9%

profile of v3, /device:TPU:0, one launch (start us, length us, event | category | flops | bytes accessed | tf_op | source)
XLA Modules:
  0.0 112.7 jit_solution(4402055360075923797)
XLA Ops:
  7.2 0.7 copy.110
  7.9 0.1 fusion.9
  8.0 0.2 select_reduce_fusion.1
  8.2 0.1 iota_compare_fusion.2
  8.3 0.1 iota_compare_fusion.4
  8.4 0.1 copy.86
  8.5 0.1 broadcast_and_fusion
  8.5 0.1 select_reduce_fusion
  8.7 0.7 copy.87
  9.4 7.3 %all-to-all-start = ((s32[32,2,3]{2,1,0:T(2,128)}), s32[32,2,3]{2,1,0:T(2,128)S(1)}, u32[]{:S(2)}, u32[]{:S(2)}) async-start(s32[32,2,3]{2,1,0:T(2,128)} %copy.87), calls=%async_computation | async-start | bytes 65536 | tf_op jit(solution)/shard_map/all_to_all | solution.py:147
  16.7 0.0 all-gather.2.cloned.1.call-start
  16.8 0.9 copy.93
  17.6 0.8 copy.94
  18.5 0.0 all-gather.2.cloned.1.call-update
  18.7 0.1 mul.199
  18.8 0.1 mul.202
  18.8 0.1 mul.203
  18.9 0.1 mul.205
  19.0 0.1 mul.206
  19.1 0.8 add_add_fusion
  20.6 3.4 %all-to-all-done = s32[32,2,3]{2,1,0:T(2,128)S(1)} async-done(((s32[32,2,3]{2,1,0:T(2,128)}), s32[32,2,3]{2,1,0:T(2,128)S(1)}, u32[]{:S(2)}, u32[]{:S(2)}) %all-to-all-start) | async-done | bytes 800 | tf_op jit(solution)/shard_map/all_to_all | solution.py:147
  24.0 0.7 reshape_reshape.6.req_ref
  24.7 10.6 %shard_map.86 = bf16[64,64,64]{2,1,0:T(8,128)(2,1)} custom-call(s32[192]{0:T(256)} %reshape_reshape.6.req_ref, bf16[2,128,4096]{2,1,0:T(8,128)(2,1)} %tiles_ref.1), custom_call_target="tpu_custom_call" | custom-call | flops 67108864 | bytes 2621440 | tf_op jit(solution)/shard_map/pallas_call | solution.py:114
  35.3 2.4 %copy.88 = bf16[32,128,64]{1,2,0:T(8,128)(2,1)} copy(bf16[32,128,64]{2,1,0:T(8,128)(2,1)} %bitcast.58) | data formatting | bytes 1048576 | tf_op jit(solution)/shard_map/reshape | solution.py:148
  37.7 2.6 %all-to-all-start.1 = ((bf16[32,128,64]{1,2,0:T(8,128)(2,1)}), bf16[32,128,64]{1,2,0:T(8,128)(2,1)S(1)}, u32[]{:S(2)}, u32[]{:S(2)}) async-start(bf16[32,128,64]{1,2,0:T(8,128)(2,1)} %copy.88), calls=%async_computation.1 | async-start | bytes 1048576 | tf_op jit(solution)/shard_map/all_to_all | solution.py:149
  41.0 0.0 copy-start
  41.0 0.0 copy-start.1
  41.0 4.5 %multiply_convert_fusion = bf16[22,64,1664]{2,1,0:T(8,128)(2,1)} fusion(f32[22,1664]{1,0:T(8,128)S(1)} %add_add_fusion, pred[22]{0:T(512)(128)(4,1)S(1)} %iota_compare_fusion.5), kind=kLoop, calls=%fused_computation.2 | loop fusion | flops 16400384 | bytes 4832278 | tf_op jit(solution)/shard_map/convert_element_type | solution.py:72
  45.5 0.1 mul.213
  45.6 0.1 mul.214
  45.7 15.1 %all-to-all-done.1 = bf16[32,128,64]{1,2,0:T(8,128)(2,1)S(1)} async-done(((bf16[32,128,64]{1,2,0:T(8,128)(2,1)}), bf16[32,128,64]{1,2,0:T(8,128)(2,1)S(1)}, u32[]{:S(2)}, u32[]{:S(2)}) %all-to-all-start.1) | async-done | bytes 524320 | tf_op jit(solution)/shard_map/all_to_all | solution.py:149
  60.8 0.5 copy.89
  61.3 0.7 gather_fusion
  62.0 0.2 copy.106
  62.3 0.1 pad.4.clone
  62.4 0.3 reshape.598
  62.6 0.0 copy-done
  62.7 0.0 copy-done.1
  62.7 5.0 %multiply_reduce_fusion.1 = (f32[]{:T(128)}, bf16[64,512]{1,0:T(8,128)(2,1)S(1)}) fusion(f32[512]{0:T(512)S(1)} %get-tuple-element.5, f32[1664]{0:T(1024)S(1)} %copy-done.1, f32[512]{0:T(512)S(1)} %get-tuple-element.4, f32[1664]{0:T(1024)S(1)} %copy-done, bf16[64,1408]{1,0:T(8,128)(2,1)S(1)} %reshape.598, bf16[1408,1664]{1,0:T(8,128)(2,1)} %bitcast.56), kind=kOutput, calls=%fused_computation.17 | convolution fusion | flops 417701888 | bytes 4948996 | tf_op jit(solution)/shard_map/dot_general | solution.py:161
  67.6 0.1 copy.91
  67.8 1.3 %gather_fusion.1 = bf16[512,64]{1,0:T(8,128)(2,1)S(1)} fusion(bf16[64,512]{0,1:T(8,128)(2,1)S(1)} %copy.91, s32[1024]{0:T(1024)S(1)} %pad_clamp_fusion), kind=kCustom, calls=%fused_computation.1 | custom fusion | bytes 133120 | tf_op jit(solution)/shard_map/jit(take_along_axis)/gather | solution.py:186
  69.1 0.1 select_bitcast_fusion
  69.3 0.1 copy.100
  69.4 0.1 mul.217
  69.5 1.1 %broadcast_multiply_fusion = bf16[1,32,32,512]{3,2,0,1:T(8,128)(2,1)} fusion(bf16[1,32,32,512]{3,2,0,1:T(8,128)(2,1)S(1)} %bitcast.57, bf16[32]{0:T(256)(128)(2,1)S(1)} %mul.214), kind=kLoop, calls=%fused_computation.11 | loop fusion | flops 524288 | bytes 2097216 | tf_op jit(solution)/shard_map/mul | solution.py:190
  70.6 2.8 %all-to-all-start.2 = ((bf16[1,32,32,512]{3,2,0,1:T(8,128)(2,1)}), bf16[1,32,32,512]{3,2,0,1:T(8,128)(2,1)S(1)}, u32[]{:S(2)}, u32[]{:S(2)}) async-start(bf16[1,32,32,512]{3,2,0,1:T(8,128)(2,1)} %broadcast_multiply_fusion), calls=%async_computation.2 | async-start | bytes 2097152 | tf_op jit(solution)/shard_map/all_to_all | solution.py:192
  73.4 0.3 copy.92
  74.3 17.8 %all-gather.2.cloned.1.call-done = bf16[32,16384]{0,1:T(8,128)(2,1)} async-done(((bf16[32,512]{0,1:T(8,128)(2,1)}), bf16[32,16384]{0,1:T(8,128)(2,1)}) %all-gather.2.cloned.1.call-update) | async-done | bytes 1048592 | tf_op jit(solution)/shard_map/all_gather | solution.py:165
  92.1 3.9 %multiply_reduce_fusion = f32[16384]{0:T(1024)S(1)} fusion(bf16[32,16384]{0,1:T(8,128)(2,1)} %all-gather.2.cloned.1.call-done), kind=kLoop, calls=%fused_computation.3 | loop fusion | flops 1556480 | bytes 1114112 | tf_op jit(solution)/shard_map/reduce_sum | solution.py:169
  96.1 0.1 reduce_sum.60
  96.2 3.0 %fusion.25 = f32[32,32,16]{1,0,2:T(8,128)S(1)} fusion(bf16[32,1024,1]{0,1,2:T(8,128)(2,1)S(1)} %bitcast.61, bf16[32,16,1024]{0,2,1:T(8,128)(2,1)} %bitcast.54), kind=kOutput, calls=%fused_computation.77 | convolution fusion | flops 33554432 | bytes 1179648 | tf_op jit(solution)/shard_map/pfm,gcm->pfgc/dot_general | solution.py:175
  99.2 0.5 fusion.2
  99.8 0.7 reshape.603
  100.4 4.6 %all-to-all-done.2 = bf16[1,32,32,512]{3,2,0,1:T(8,128)(2,1)S(1)} async-done(((bf16[1,32,32,512]{3,2,0,1:T(8,128)(2,1)}), bf16[1,32,32,512]{3,2,0,1:T(8,128)(2,1)S(1)}, u32[]{:S(2)}, u32[]{:S(2)}) %all-to-all-start.2) | async-done | bytes 1048608 | tf_op jit(solution)/shard_map/all_to_all | solution.py:192
  105.0 0.8 convert_reduce_fusion
  (20 shorter events, 0.3 us)
Async XLA Ops:
  9.4 14.6 %all-to-all-start = ((s32[32,2,3]{2,1,0:T(2,128)}), s32[32,2,3]{2,1,0:T(2,128)S(1)}, u32[]{:S(2)}, u32[]{:S(2)}) async-start(s32[32,2,3]{2,1,0:T(2,128)} %copy.87), calls=%async_computation | async-start | bytes 65536 | tf_op jit(solution)/shard_map/all_to_all | solution.py:147
  16.7 75.4 %all-gather.2.cloned.1.call-start = ((), (), s32[]{:S(2)}) async-start(), calls=%async_computation.3 | async-start | bytes 4325376 | tf_op jit(solution)/shard_map/all_gather | solution.py:165
  37.7 23.1 %all-to-all-start.1 = ((bf16[32,128,64]{1,2,0:T(8,128)(2,1)}), bf16[32,128,64]{1,2,0:T(8,128)(2,1)S(1)}, u32[]{:S(2)}, u32[]{:S(2)}) async-start(bf16[32,128,64]{1,2,0:T(8,128)(2,1)} %copy.88), calls=%async_computation.1 | async-start | bytes 1048576 | tf_op jit(solution)/shard_map/all_to_all | solution.py:149
  41.0 21.7 %copy-start = (f32[1664]{0:T(1024)S(1)}, f32[1664]{0:T(1024)}, u32[]{:S(2)}) copy-start(f32[1664]{0:T(1024)} %constant.135) | copy-start | bytes 19972
  41.0 21.7 %copy-start.1 = (f32[1664]{0:T(1024)S(1)}, f32[1664]{0:T(1024)}, u32[]{:S(2)}) copy-start(f32[1664]{0:T(1024)} %constant.136) | copy-start | bytes 19972
  70.6 34.4 %all-to-all-start.2 = ((bf16[1,32,32,512]{3,2,0,1:T(8,128)(2,1)}), bf16[1,32,32,512]{3,2,0,1:T(8,128)(2,1)S(1)}, u32[]{:S(2)}, u32[]{:S(2)}) async-start(bf16[1,32,32,512]{3,2,0,1:T(8,128)(2,1)} %broadcast_multiply_fusion), calls=%async_computation.2 | async-start | bytes 2097152 | tf_op jit(solution)/shard_map/all_to_all | solution.py:192
Sparse Core Ops, SparseCore 0:
  20.4 71.6 all-gather.1

commit v4 on v3

--- a/solution.py
+++ b/solution.py
@@ -161,18 +161,23 @@
     cyl = jnp.dot(volume, sample_points(xs, zs), preferred_element_type=jnp.float32)
     cyl = cyl.astype(jnp.bfloat16).reshape(count, BOX, ROTS * CYCLES)
     owned = references.shape[0]
+    parts = BOX // owned
     local_t = references.reshape(owned, ROTS, CYCLES).transpose(1, 0, 2).reshape(ROTS, owned * CYCLES)
-    gathered = lax.all_gather(local_t, "dev", axis=1, tiled=True).reshape(
-        ROTS, CLASSES, BOX * CYCLES
-    )
+    gathered = lax.all_gather(local_t[None], "dev", axis=0, tiled=True)
+    gathered = gathered.reshape(CLASSES, parts, ROTS, owned * CYCLES)
     ref_float = gathered.astype(jnp.float32)
-    ref_power = jnp.mean(ref_float * ref_float, axis=(0, 2))
+    ref_power = jnp.mean(ref_float * ref_float, axis=(1, 2, 3))
     cyl_three = (
         cyl.reshape(count, BOX, ROTS, CYCLES)
         .transpose(0, 2, 1, 3)
-        .reshape(count, ROTS, BOX * CYCLES)
-    )
-    corr = jnp.einsum("pfm,gcm->pfgc", cyl_three, gathered, preferred_element_type=jnp.float32)
+        .reshape(count, ROTS, parts, owned * CYCLES)
+    )
+    corr = sum(
+        jnp.einsum(
+            "pfm,cgm->pfgc", cyl_three[:, :, q], gathered[:, q], preferred_element_type=jnp.float32
+        )
+        for q in range(parts)
+    )
     raw = jnp.einsum("pfgc,kfg->pck", corr, shift_table(), precision=lax.Precision.HIGHEST)
     cyl_float = cyl.astype(jnp.float32)
     power = jnp.mean(cyl_float.reshape(count, -1) ** 2, axis=1)

time: 113 us -> 105 us (0.929)
  waiting for transfers between devices: 41 us -> 33.9 us
  other arithmetic: 12.3 us -> 10 us
    all_gather x1, waiting for transfers between devices: 17.8 us -> 6.13 us  [per_device(): gathered = lax.all_gather(local_t[None], 'dev', axis=0, tiled=True)]
    all_to_all x1, waiting for transfers between devices: 4.59 us -> 13.3 us  [per_device(): lax.all_to_all(placed, 'dev', split_axis=1, concat_axis=0, tiled=True)]
    all_to_all x1, waiting for transfers between devices: 15.1 us -> 11.4 us  [per_device(): lax.all_to_all(patches_cut, 'dev', split_axis=0, concat_axis=0, tiled=True)]
    reduce_sum x2, other arithmetic: 4.04 us -> 1.71 us  [per_device(): ref_power = jnp.mean(ref_float * ref_float, axis=(1, 2, 3))]
    dot_general x1 -> x2, matrix products: 3.04 us -> 3.2 us  [per_device(): jnp.einsum('pfm,cgm->pfgc', cyl_three[:, :, q], gathered[:, q], preferred...]
  transfers between devices with their start and end apart: 4 -> 4, of which waited for: 4 -> 4; matrix products, arithmetic and copies ran while one was open for 26% -> 26% of each run, Pallas kernels for 9% -> 10%
where the time goes in v4:
time: 105 us; the launch traced here: 104 us
  waiting for transfers between devices  33.9 us (32%)
  between operations  16.2 us (15%)
  starting transfers between devices  13.3 us (13%)
  local copies, waits for them, and re-layouts  11.4 us (11%)
  Pallas kernels  10.6 us (10%)
  other arithmetic  10 us (10%)
  matrix products  8.68 us (8%)
    all_to_all x1, waiting for transfers between devices, per_device(): lax.all_to_all(placed, 'dev', split_axis=1, concat_axis=0, tiled=True)  13.3 us
    all_to_all x1, waiting for transfers between devices, per_device(): lax.all_to_all(patches_cut, 'dev', split_axis=0, concat_axis=0, tiled=True)  11.4 us
    pallas_call x1, Pallas kernels, cut_patches(): pl.pallas_call(cut_kernel, out_shape=jax.ShapeDtypeStruct((count, BOX, BO...  10.6 us
    all_to_all x1, starting transfers between devices, per_device(): lax.all_to_all(wanted, 'dev', split_axis=0, concat_axis=0, tiled=True)  7.3 us
    all_gather x1, waiting for transfers between devices, per_device(): gathered = lax.all_gather(local_t[None], 'dev', axis=0, tiled=True)  6.13 us
    dot_general x1, matrix products, per_device(): jnp.dot(volume, sample_points(xs, zs), preferred_element_type=jnp.float32)  4.96 us
    convert_element_type x1, other arithmetic, back_points(): return weight.reshape(count * BOX, xs.shape[0]).astype(jnp.bfloat16)  4.47 us
    dot_general x2, matrix products, per_device(): jnp.einsum('pfm,cgm->pfgc', cyl_three[:, :, q], gathered[:, q], preferred...  3.2 us
  transfers between devices with their start and end apart: 4, of which 4 were waited for; matrix products, arithmetic and copies ran while one was open for 26% of the time, Pallas kernels for 10%

profile of v4, /device:TPU:0, one launch (start us, length us, event | category | flops | bytes accessed | tf_op | source)
XLA Modules:
  0.0 104.1 jit_solution(5021636170059714479)
XLA Ops:
  7.2 0.7 copy.117
  7.9 0.1 fusion.11
  8.0 0.2 select_reduce_fusion.1
  8.2 0.1 iota_compare_fusion.2
  8.3 0.1 iota_compare_fusion.4
  8.4 0.1 copy.91
  8.5 0.1 broadcast_and_fusion
  8.5 0.1 select_reduce_fusion
  8.7 0.7 copy.92
  9.4 7.3 %all-to-all-start = ((s32[32,2,3]{2,1,0:T(2,128)}), s32[32,2,3]{2,1,0:T(2,128)S(1)}, u32[]{:S(2)}, u32[]{:S(2)}) async-start(s32[32,2,3]{2,1,0:T(2,128)} %copy.92), calls=%async_computation | async-start | bytes 65536 | tf_op jit(solution)/shard_map/all_to_all | solution.py:147
  16.7 0.0 all-gather.2.cloned.1.call-start
  16.7 0.9 copy.99
  17.6 0.2 copy.100
  17.8 0.7 copy.101
  18.5 0.0 all-gather.2.cloned.1.call-update
  19.4 0.8 add_add_fusion
  20.9 3.0 %all-to-all-done = s32[32,2,3]{2,1,0:T(2,128)S(1)} async-done(((s32[32,2,3]{2,1,0:T(2,128)}), s32[32,2,3]{2,1,0:T(2,128)S(1)}, u32[]{:S(2)}, u32[]{:S(2)}) %all-to-all-start) | async-done | bytes 800 | tf_op jit(solution)/shard_map/all_to_all | solution.py:147
  23.9 0.7 reshape_reshape.6.req_ref
  24.7 10.6 %shard_map.86 = bf16[64,64,64]{2,1,0:T(8,128)(2,1)} custom-call(s32[192]{0:T(256)} %reshape_reshape.6.req_ref, bf16[2,128,4096]{2,1,0:T(8,128)(2,1)} %tiles_ref.1), custom_call_target="tpu_custom_call" | custom-call | flops 67108864 | bytes 2621440 | tf_op jit(solution)/shard_map/pallas_call | solution.py:114
  35.2 2.4 %copy.93 = bf16[32,128,64]{1,2,0:T(8,128)(2,1)} copy(bf16[32,128,64]{2,1,0:T(8,128)(2,1)} %bitcast.85) | data formatting | bytes 1048576 | tf_op jit(solution)/shard_map/reshape | solution.py:148
  37.6 2.8 %all-to-all-start.1 = ((bf16[32,128,64]{1,2,0:T(8,128)(2,1)}), bf16[32,128,64]{1,2,0:T(8,128)(2,1)S(1)}, u32[]{:S(2)}, u32[]{:S(2)}) async-start(bf16[32,128,64]{1,2,0:T(8,128)(2,1)} %copy.93), calls=%async_computation.1 | async-start | bytes 1048576 | tf_op jit(solution)/shard_map/all_to_all | solution.py:149
  40.4 0.1 mul.199
  40.5 0.1 mul.202
  40.6 0.1 mul.203
  40.7 0.1 mul.205
  40.7 0.1 mul.206
  40.8 0.1 mul.213
  40.9 0.1 mul.214
  41.0 0.0 copy-start
  41.0 0.0 copy-start.1
  41.0 4.5 %multiply_convert_fusion = bf16[22,64,1664]{2,1,0:T(8,128)(2,1)} fusion(f32[22,1664]{1,0:T(8,128)S(1)} %add_add_fusion, pred[22]{0:T(512)(128)(4,1)S(1)} %iota_compare_fusion.5), kind=kLoop, calls=%fused_computation.2 | loop fusion | flops 16400384 | bytes 4832278 | tf_op jit(solution)/shard_map/convert_element_type | solution.py:72
  45.5 11.4 %all-to-all-done.1 = bf16[32,128,64]{1,2,0:T(8,128)(2,1)S(1)} async-done(((bf16[32,128,64]{1,2,0:T(8,128)(2,1)}), bf16[32,128,64]{1,2,0:T(8,128)(2,1)S(1)}, u32[]{:S(2)}, u32[]{:S(2)}) %all-to-all-start.1) | async-done | bytes 524320 | tf_op jit(solution)/shard_map/all_to_all | solution.py:149
  57.0 0.5 copy.94
  57.4 0.7 gather_fusion
  58.2 0.2 copy.113
  58.4 0.1 pad.4.clone
  58.5 0.3 reshape.604
  58.8 0.0 copy-done
  58.8 0.0 copy-done.1
  58.8 5.0 %multiply_reduce_fusion.1 = (f32[]{:T(128)}, bf16[64,512]{1,0:T(8,128)(2,1)S(1)}) fusion(f32[512]{0:T(512)S(1)} %get-tuple-element.5, f32[1664]{0:T(1024)S(1)} %copy-done.1, f32[512]{0:T(512)S(1)} %get-tuple-element.4, f32[1664]{0:T(1024)S(1)} %copy-done, bf16[64,1408]{1,0:T(8,128)(2,1)S(1)} %reshape.604, bf16[1408,1664]{1,0:T(8,128)(2,1)} %bitcast.81), kind=kOutput, calls=%fused_computation.24 | convolution fusion | flops 417701888 | bytes 4948996 | tf_op jit(solution)/shard_map/dot_general | solution.py:161
  63.8 0.1 copy.96
  63.9 1.3 %gather_fusion.1 = bf16[512,64]{1,0:T(8,128)(2,1)S(1)} fusion(bf16[64,512]{0,1:T(8,128)(2,1)S(1)} %copy.96, s32[1024]{0:T(1024)S(1)} %pad_clamp_fusion), kind=kCustom, calls=%fused_computation.1 | custom fusion | bytes 133120 | tf_op jit(solution)/shard_map/jit(take_along_axis)/gather | solution.py:191
  65.2 0.1 select_bitcast_fusion
  65.4 0.1 copy.107
  65.5 0.1 mul.217
  65.6 1.1 %broadcast_multiply_fusion = bf16[1,32,32,512]{3,2,0,1:T(8,128)(2,1)} fusion(bf16[1,32,32,512]{3,2,0,1:T(8,128)(2,1)S(1)} %bitcast.82, bf16[32]{0:T(256)(128)(2,1)S(1)} %mul.214), kind=kLoop, calls=%fused_computation.16 | loop fusion | flops 524288 | bytes 2097216 | tf_op jit(solution)/shard_map/mul | solution.py:195
  66.7 3.1 %all-to-all-start.2 = ((bf16[1,32,32,512]{3,2,0,1:T(8,128)(2,1)}), bf16[1,32,32,512]{3,2,0,1:T(8,128)(2,1)S(1)}, u32[]{:S(2)}, u32[]{:S(2)}) async-start(bf16[1,32,32,512]{3,2,0,1:T(8,128)(2,1)} %broadcast_multiply_fusion), calls=%async_computation.2 | async-start | bytes 2097152 | tf_op jit(solution)/shard_map/all_to_all | solution.py:197
  69.9 0.3 copy.97
  70.8 6.1 %all-gather.2.cloned.1.call-done = bf16[32,32,512]{2,1,0:T(8,128)(2,1)} async-done(((bf16[1,32,512]{2,1,0:T(8,128)(2,1)}), bf16[32,32,512]{2,1,0:T(8,128)(2,1)}) %all-gather.2.cloned.1.call-update) | async-done | bytes 1048592 | tf_op jit(solution)/shard_map/all_gather | solution.py:166
  76.9 1.6 %multiply_reduce_fusion = f32[32]{0:T(128)S(1)} fusion(bf16[32,32,512]{2,1,0:T(8,128)(2,1)} %all-gather.2.cloned.1.call-done), kind=kLoop, calls=%fused_computation.6 | loop fusion | flops 1572832 | bytes 1048704 | tf_op jit(solution)/shard_map/reduce_sum | solution.py:169
  78.5 0.1 reduce_sum.59
  78.6 0.1 reduce_sum.60
  78.8 1.6 %fusion.4 = f32[32,16,32]{2,0,1:T(8,128)S(1)} fusion(bf16[16,2,32,512]{3,2,1,0:T(8,128)(2,1)} %bitcast.83, bf16[1,32,2,512]{1,3,2,0:T(8,128)(2,1)S(1)} %bitcast.88), kind=kOutput, calls=%fused_computation.15 | convolution fusion | flops 16777216 | bytes 720896 | tf_op jit(solution)/shard_map/pfm,cgm->pfgc/dot_general | solution.py:176
  80.3 1.6 %fusion.1 = f32[32,32,16]{1,0,2:T(8,128)S(1)} fusion(f32[32,16,32]{2,0,1:T(8,128)S(1)} %fusion.4, bf16[16,2,32,512]{3,2,1,0:T(8,128)(2,1)} %bitcast.84, bf16[1,32,2,512]{1,3,2,0:T(8,128)(2,1)S(1)} %bitcast.89), kind=kOutput, calls=%fused_computation.9 | convolution fusion | flops 16793600 | bytes 983040 | tf_op jit(solution)/shard_map/pfm,cgm->pfgc/dot_general | solution.py:176
  82.0 0.5 fusion.3
  82.5 0.7 reshape.611
  83.2 13.3 %all-to-all-done.2 = bf16[1,32,32,512]{3,2,0,1:T(8,128)(2,1)S(1)} async-done(((bf16[1,32,32,512]{3,2,0,1:T(8,128)(2,1)}), bf16[1,32,32,512]{3,2,0,1:T(8,128)(2,1)S(1)}, u32[]{:S(2)}, u32[]{:S(2)}) %all-to-all-start.2) | async-done | bytes 1048608 | tf_op jit(solution)/shard_map/all_to_all | solution.py:197
  96.5 0.8 convert_reduce_fusion
  (19 shorter events, 0.3 us)
Async XLA Ops:
  9.4 14.6 %all-to-all-start = ((s32[32,2,3]{2,1,0:T(2,128)}), s32[32,2,3]{2,1,0:T(2,128)S(1)}, u32[]{:S(2)}, u32[]{:S(2)}) async-start(s32[32,2,3]{2,1,0:T(2,128)} %copy.92), calls=%async_computation | async-start | bytes 65536 | tf_op jit(solution)/shard_map/all_to_all | solution.py:147
  16.7 60.2 %all-gather.2.cloned.1.call-start = ((), (), s32[]{:S(2)}) async-start(), calls=%async_computation.3 | async-start | bytes 1081344 | tf_op jit(solution)/shard_map/all_gather | solution.py:166
  37.6 19.4 %all-to-all-start.1 = ((bf16[32,128,64]{1,2,0:T(8,128)(2,1)}), bf16[32,128,64]{1,2,0:T(8,128)(2,1)S(1)}, u32[]{:S(2)}, u32[]{:S(2)}) async-start(bf16[32,128,64]{1,2,0:T(8,128)(2,1)} %copy.93), calls=%async_computation.1 | async-start | bytes 1048576 | tf_op jit(solution)/shard_map/all_to_all | solution.py:149
  41.0 17.8 %copy-start = (f32[1664]{0:T(1024)S(1)}, f32[1664]{0:T(1024)}, u32[]{:S(2)}) copy-start(f32[1664]{0:T(1024)} %constant.135) | copy-start | bytes 19972
  41.0 17.8 %copy-start.1 = (f32[1664]{0:T(1024)S(1)}, f32[1664]{0:T(1024)}, u32[]{:S(2)}) copy-start(f32[1664]{0:T(1024)} %constant.136) | copy-start | bytes 19972
  66.7 29.8 %all-to-all-start.2 = ((bf16[1,32,32,512]{3,2,0,1:T(8,128)(2,1)}), bf16[1,32,32,512]{3,2,0,1:T(8,128)(2,1)S(1)}, u32[]{:S(2)}, u32[]{:S(2)}) async-start(bf16[1,32,32,512]{3,2,0,1:T(8,128)(2,1)} %broadcast_multiply_fusion), calls=%async_computation.2 | async-start | bytes 2097152 | tf_op jit(solution)/shard_map/all_to_all | solution.py:197
Sparse Core Ops, SparseCore 0:
  21.0 55.9 all-gather.1

commit v5 on v4

--- a/solution.py
+++ b/solution.py
@@ -100,12 +100,12 @@
         r0 = pl.multiple_of(jnp.minimum((r // 16) * 16, rows - span), 16)
         c0 = pl.multiple_of(jnp.minimum((c // 128) * 128, width - WIN), 128)
         win = tiles_ref[t, pl.ds(r0, span), pl.ds(c0, WIN)].astype(jnp.float32)
+        win = pltpu.roll(win, (WIN - (c - c0)) % WIN, 1)[:, :128]
         win = pltpu.roll(win, (span - (r - r0)) % span, 0)
-        win = pltpu.roll(win, (WIN - (c - c0)) % WIN, 1)
         out_ref[k] = win[:BOX, :BOX].astype(out_ref.dtype)
         return carry
 
-    lax.fori_loop(0, count, body, 0)
+    lax.fori_loop(0, count, body, 0, unroll=2)
 
 
 def cut_patches(tiles, req):
@@ -158,7 +158,8 @@
     xs, zs = jnp.asarray(xs_np), jnp.asarray(zs_np)
     volume = jnp.dot(pmat, back_points(padded, xs, zs), preferred_element_type=jnp.float32)
     volume = volume.astype(jnp.bfloat16)
-    cyl = jnp.dot(volume, sample_points(xs, zs), preferred_element_type=jnp.float32)
+    sample = lax.optimization_barrier(sample_points(xs, zs))
+    cyl = jnp.dot(volume, sample, preferred_element_type=jnp.float32)
     cyl = cyl.astype(jnp.bfloat16).reshape(count, BOX, ROTS * CYCLES)
     owned = references.shape[0]
     parts = BOX // owned

time: 105 us -> 104 us (level)
  Pallas kernels: 10.6 us -> 7.37 us
  starting transfers between devices: 13.3 us -> 15.7 us
  other arithmetic: 10 us -> 12 us
  waiting for transfers between devices: 33.9 us -> 32.5 us
    pallas_call x1, Pallas kernels: 10.6 us -> 7.37 us  [cut_patches(): pl.pallas_call(cut_kernel, out_shape=jax.ShapeDtypeStruct((count, BOX, BO...]
    all_to_all x1, starting transfers between devices: 2.8 us -> 5.19 us  [per_device(): lax.all_to_all(patches_cut, 'dev', split_axis=0, concat_axis=0, tiled=True)]
    all_to_all x1, waiting for transfers between devices: 3.04 us -> 0.65 us  [per_device(): lax.all_to_all(wanted, 'dev', split_axis=0, concat_axis=0, tiled=True)]
    all_gather x1, waiting for transfers between devices: 6.13 us -> 8.21 us  [per_device(): gathered = lax.all_gather(local_t[None], 'dev', axis=0, tiled=True)]
    convert_element_type x0 -> x1, other arithmetic: none -> 1.98 us  [sample_points(): return (wx * wz).reshape(xs.shape[0], ROTS * CYCLES).astype(jnp.bfloat16)]
    all_to_all x1, waiting for transfers between devices: 13.3 us -> 11.9 us  [per_device(): lax.all_to_all(placed, 'dev', split_axis=1, concat_axis=0, tiled=True)]
  transfers between devices with their start and end apart: 4 -> 4, of which waited for: 4 -> 4; matrix products, arithmetic and copies ran while one was open for 26% -> 27% of each run, Pallas kernels for 10% -> 7%
where the time goes in v5:
time: 104 us; the launch traced here: 103 us
  waiting for transfers between devices  32.5 us (31%)
  between operations  16.2 us (16%)
  starting transfers between devices  15.7 us (15%)
  other arithmetic  12 us (12%)
  local copies, waits for them, and re-layouts  11.4 us (11%)
  matrix products  7.9 us (8%)
  Pallas kernels  7.37 us (7%)
    all_to_all x1, waiting for transfers between devices, per_device(): lax.all_to_all(placed, 'dev', split_axis=1, concat_axis=0, tiled=True)  11.9 us
    all_to_all x1, waiting for transfers between devices, per_device(): lax.all_to_all(patches_cut, 'dev', split_axis=0, concat_axis=0, tiled=True)  11.8 us
    all_gather x1, waiting for transfers between devices, per_device(): gathered = lax.all_gather(local_t[None], 'dev', axis=0, tiled=True)  8.21 us
    pallas_call x1, Pallas kernels, cut_patches(): pl.pallas_call(cut_kernel, out_shape=jax.ShapeDtypeStruct((count, BOX, BO...  7.37 us
    all_to_all x1, starting transfers between devices, per_device(): lax.all_to_all(wanted, 'dev', split_axis=0, concat_axis=0, tiled=True)  7.3 us
    all_to_all x1, starting transfers between devices, per_device(): lax.all_to_all(patches_cut, 'dev', split_axis=0, concat_axis=0, tiled=True)  5.19 us
    convert_element_type x1, other arithmetic, back_points(): return weight.reshape(count * BOX, xs.shape[0]).astype(jnp.bfloat16)  4.47 us
    dot_general x1, matrix products, per_device(): cyl = jnp.dot(volume, sample, preferred_element_type=jnp.float32)  4.18 us
  transfers between devices with their start and end apart: 4, of which 4 were waited for; matrix products, arithmetic and copies ran while one was open for 27% of the time, Pallas kernels for 7%

profile of v5, /device:TPU:0, one launch (start us, length us, event | category | flops | bytes accessed | tf_op | source)
XLA Modules:
  0.0 103.0 jit_solution(2019287612901107554)
XLA Ops:
  7.2 0.7 copy.117
  7.9 0.1 fusion.11
  8.0 0.2 select_reduce_fusion.1
  8.2 0.1 iota_compare_fusion.2
  8.3 0.1 iota_compare_fusion.4
  8.4 0.1 copy.91
  8.5 0.1 broadcast_and_fusion
  8.5 0.1 select_reduce_fusion
  8.7 0.7 copy.92
  9.4 7.3 %all-to-all-start = ((s32[32,2,3]{2,1,0:T(2,128)}), s32[32,2,3]{2,1,0:T(2,128)S(1)}, u32[]{:S(2)}, u32[]{:S(2)}) async-start(s32[32,2,3]{2,1,0:T(2,128)} %copy.92), calls=%async_computation | async-start | bytes 65536 | tf_op jit(solution)/shard_map/all_to_all | solution.py:147
  16.7 0.0 all-gather.2.cloned.1.call-start
  16.7 0.9 copy.99
  17.6 0.2 copy.100
  17.8 0.7 copy.101
  18.5 0.0 all-gather.2.cloned.1.call-update
  18.7 0.1 mul.199
  18.8 0.1 mul.202
  18.9 0.1 mul.203
  19.0 0.1 mul.205
  19.0 0.1 mul.206
  19.8 0.8 add_add_fusion
  20.6 2.0 %multiply_convert_fusion.1 = bf16[1664,512]{1,0:T(8,128)(2,1)S(1)} fusion(f32[512]{0:T(512)S(1)} %get-tuple-element.5, f32[1664]{0:T(1024)} %constant.136, f32[512]{0:T(512)S(1)} %get-tuple-element.4, f32[1664]{0:T(1024)} %constant.135), kind=kLoop, calls=%fused_computation.3 | loop fusion | flops 8519680 | bytes 1721344 | tf_op jit(solution)/shard_map/convert_element_type | solution.py:81
  23.3 0.6 all-to-all-done
  23.9 0.7 reshape_reshape.6.req_ref
  24.7 7.4 %shard_map.86 = bf16[64,64,64]{2,1,0:T(8,128)(2,1)} custom-call(s32[192]{0:T(256)} %reshape_reshape.6.req_ref, bf16[2,128,4096]{2,1,0:T(8,128)(2,1)} %tiles_ref.1), custom_call_target="tpu_custom_call" | custom-call | flops 67108864 | bytes 2621440 | tf_op jit(solution)/shard_map/pallas_call | solution.py:114
  32.0 2.4 %copy.93 = bf16[32,128,64]{1,2,0:T(8,128)(2,1)} copy(bf16[32,128,64]{2,1,0:T(8,128)(2,1)} %bitcast.86) | data formatting | bytes 1048576 | tf_op jit(solution)/shard_map/reshape | solution.py:148
  34.4 5.2 %all-to-all-start.1 = ((bf16[32,128,64]{1,2,0:T(8,128)(2,1)}), bf16[32,128,64]{1,2,0:T(8,128)(2,1)S(1)}, u32[]{:S(2)}, u32[]{:S(2)}) async-start(bf16[32,128,64]{1,2,0:T(8,128)(2,1)} %copy.93), calls=%async_computation.1 | async-start | bytes 1048576 | tf_op jit(solution)/shard_map/all_to_all | solution.py:149
  39.6 0.1 mul.213
  39.7 0.1 mul.214
  39.8 4.5 %multiply_convert_fusion = bf16[22,64,1664]{2,1,0:T(8,128)(2,1)} fusion(f32[22,1664]{1,0:T(8,128)S(1)} %add_add_fusion, pred[22]{0:T(512)(128)(4,1)S(1)} %iota_compare_fusion.5), kind=kLoop, calls=%fused_computation.2 | loop fusion | flops 16400384 | bytes 4832278 | tf_op jit(solution)/shard_map/convert_element_type | solution.py:72
  44.3 11.8 %all-to-all-done.1 = bf16[32,128,64]{1,2,0:T(8,128)(2,1)S(1)} async-done(((bf16[32,128,64]{1,2,0:T(8,128)(2,1)}), bf16[32,128,64]{1,2,0:T(8,128)(2,1)S(1)}, u32[]{:S(2)}, u32[]{:S(2)}) %all-to-all-start.1) | async-done | bytes 524320 | tf_op jit(solution)/shard_map/all_to_all | solution.py:149
  56.0 0.5 copy.94
  56.5 0.7 gather_fusion
  57.2 0.2 copy.113
  57.5 0.1 pad.4.clone
  57.6 0.3 reshape.604
  57.8 4.2 %multiply_reduce_fusion.1 = (f32[]{:T(128)}, bf16[64,512]{1,0:T(8,128)(2,1)S(1)}) fusion(bf16[1664,512]{1,0:T(8,128)(2,1)S(1)} %multiply_convert_fusion.1, bf16[64,1408]{1,0:T(8,128)(2,1)S(1)} %reshape.604, bf16[1408,1664]{1,0:T(8,128)(2,1)} %bitcast.81), kind=kOutput, calls=%fused_computation.24 | convolution fusion | flops 409182208 | bytes 6635524 | tf_op jit(solution)/shard_map/dot_general | solution.py:162
  62.0 0.1 copy.96
  62.1 1.3 %gather_fusion.1 = bf16[512,64]{1,0:T(8,128)(2,1)S(1)} fusion(bf16[64,512]{0,1:T(8,128)(2,1)S(1)} %copy.96, s32[1024]{0:T(1024)S(1)} %pad_clamp_fusion), kind=kCustom, calls=%fused_computation.1 | custom fusion | bytes 133120 | tf_op jit(solution)/shard_map/jit(take_along_axis)/gather | solution.py:192
  63.5 0.1 select_bitcast_fusion
  63.6 0.1 copy.107
  63.7 0.1 mul.217
  63.8 1.1 %broadcast_multiply_fusion = bf16[1,32,32,512]{3,2,0,1:T(8,128)(2,1)} fusion(bf16[1,32,32,512]{3,2,0,1:T(8,128)(2,1)S(1)} %bitcast.83, bf16[32]{0:T(256)(128)(2,1)S(1)} %mul.214), kind=kLoop, calls=%fused_computation.16 | loop fusion | flops 524288 | bytes 2097216 | tf_op jit(solution)/shard_map/mul | solution.py:196
  65.0 3.1 %all-to-all-start.2 = ((bf16[1,32,32,512]{3,2,0,1:T(8,128)(2,1)}), bf16[1,32,32,512]{3,2,0,1:T(8,128)(2,1)S(1)}, u32[]{:S(2)}, u32[]{:S(2)}) async-start(bf16[1,32,32,512]{3,2,0,1:T(8,128)(2,1)} %broadcast_multiply_fusion), calls=%async_computation.2 | async-start | bytes 2097152 | tf_op jit(solution)/shard_map/all_to_all | solution.py:198
  68.1 0.3 copy.97
  69.1 8.2 %all-gather.2.cloned.1.call-done = bf16[32,32,512]{2,1,0:T(8,128)(2,1)} async-done(((bf16[1,32,512]{2,1,0:T(8,128)(2,1)}), bf16[32,32,512]{2,1,0:T(8,128)(2,1)}) %all-gather.2.cloned.1.call-update) | async-done | bytes 1048592 | tf_op jit(solution)/shard_map/all_gather | solution.py:167
  77.3 1.6 %multiply_reduce_fusion = f32[32]{0:T(128)S(1)} fusion(bf16[32,32,512]{2,1,0:T(8,128)(2,1)} %all-gather.2.cloned.1.call-done), kind=kLoop, calls=%fused_computation.6 | loop fusion | flops 1572832 | bytes 1048704 | tf_op jit(solution)/shard_map/reduce_sum | solution.py:170
  78.9 0.1 reduce_sum.59
  79.0 0.1 reduce_sum.60
  79.1 1.6 %fusion.4 = f32[32,16,32]{2,0,1:T(8,128)S(1)} fusion(bf16[16,2,32,512]{3,2,1,0:T(8,128)(2,1)} %bitcast.84, bf16[1,32,2,512]{1,3,2,0:T(8,128)(2,1)S(1)} %bitcast.89), kind=kOutput, calls=%fused_computation.15 | convolution fusion | flops 16777216 | bytes 720896 | tf_op jit(solution)/shard_map/pfm,cgm->pfgc/dot_general | solution.py:177
  80.7 1.6 %fusion = f32[32,32,16]{1,0,2:T(8,128)S(1)} fusion(f32[32,16,32]{2,0,1:T(8,128)S(1)} %fusion.4, bf16[16,2,32,512]{3,2,1,0:T(8,128)(2,1)} %bitcast.85, bf16[1,32,2,512]{1,3,2,0:T(8,128)(2,1)S(1)} %bitcast.90), kind=kOutput, calls=%fused_computation.8 | convolution fusion | flops 16793600 | bytes 983040 | tf_op jit(solution)/shard_map/pfm,cgm->pfgc/dot_general | solution.py:177
  82.3 0.5 fusion.3
  82.8 0.7 reshape.611
  83.5 11.9 %all-to-all-done.2 = bf16[1,32,32,512]{3,2,0,1:T(8,128)(2,1)S(1)} async-done(((bf16[1,32,32,512]{3,2,0,1:T(8,128)(2,1)}), bf16[1,32,32,512]{3,2,0,1:T(8,128)(2,1)S(1)}, u32[]{:S(2)}, u32[]{:S(2)}) %all-to-all-start.2) | async-done | bytes 1048608 | tf_op jit(solution)/shard_map/all_to_all | solution.py:198
  95.4 0.8 convert_reduce_fusion
  (19 shorter events, 0.3 us)
Async XLA Ops:
  9.4 14.6 %all-to-all-start = ((s32[32,2,3]{2,1,0:T(2,128)}), s32[32,2,3]{2,1,0:T(2,128)S(1)}, u32[]{:S(2)}, u32[]{:S(2)}) async-start(s32[32,2,3]{2,1,0:T(2,128)} %copy.92), calls=%async_computation | async-start | bytes 65536 | tf_op jit(solution)/shard_map/all_to_all | solution.py:147
  16.7 60.6 %all-gather.2.cloned.1.call-start = ((), (), s32[]{:S(2)}) async-start(), calls=%async_computation.3 | async-start | bytes 1081344 | tf_op jit(solution)/shard_map/all_gather | solution.py:167
  34.4 21.6 %all-to-all-start.1 = ((bf16[32,128,64]{1,2,0:T(8,128)(2,1)}), bf16[32,128,64]{1,2,0:T(8,128)(2,1)S(1)}, u32[]{:S(2)}, u32[]{:S(2)}) async-start(bf16[32,128,64]{1,2,0:T(8,128)(2,1)} %copy.93), calls=%async_computation.1 | async-start | bytes 1048576 | tf_op jit(solution)/shard_map/all_to_all | solution.py:149
  65.0 30.4 %all-to-all-start.2 = ((bf16[1,32,32,512]{3,2,0,1:T(8,128)(2,1)}), bf16[1,32,32,512]{3,2,0,1:T(8,128)(2,1)S(1)}, u32[]{:S(2)}, u32[]{:S(2)}) async-start(bf16[1,32,32,512]{3,2,0,1:T(8,128)(2,1)} %broadcast_multiply_fusion), calls=%async_computation.2 | async-start | bytes 2097152 | tf_op jit(solution)/shard_map/all_to_all | solution.py:198
Sparse Core Ops, SparseCore 0:
  21.0 56.2 all-gather.1

commit v6 on v5

--- a/solution.py
+++ b/solution.py
@@ -87,43 +87,45 @@
     return (steps[None, None, :] == want).astype(jnp.float32)
 
 
-def cut_kernel(req_ref, tiles_ref, out_ref):
-    count = out_ref.shape[0]
+def cut_kernel(cap, req_ref, tiles_ref, out_ref):
+    ends = out_ref.shape[0]
     width = tiles_ref.shape[2]
     rows = tiles_ref.shape[1]
     span = BOX + 16
 
-    def body(k, carry):
-        t = req_ref[3 * k]
-        r = req_ref[3 * k + 1]
-        c = req_ref[3 * k + 2]
-        r0 = pl.multiple_of(jnp.minimum((r // 16) * 16, rows - span), 16)
-        c0 = pl.multiple_of(jnp.minimum((c // 128) * 128, width - WIN), 128)
-        win = tiles_ref[t, pl.ds(r0, span), pl.ds(c0, WIN)].astype(jnp.float32)
-        win = pltpu.roll(win, (WIN - (c - c0)) % WIN, 1)[:, :128]
-        win = pltpu.roll(win, (span - (r - r0)) % span, 0)
-        out_ref[k] = win[:BOX, :BOX].astype(out_ref.dtype)
+    def body(d, carry):
+        for s in range(cap):
+            k = d * cap + s
+            t = req_ref[3 * k]
+            r = req_ref[3 * k + 1]
+            c = req_ref[3 * k + 2]
+            r0 = pl.multiple_of(jnp.minimum((r // 16) * 16, rows - span), 16)
+            c0 = pl.multiple_of(jnp.minimum((c // 128) * 128, width - WIN), 128)
+            win = tiles_ref[t, pl.ds(r0, span), pl.ds(c0, WIN)].astype(jnp.float32)
+            win = pltpu.roll(win, (WIN - (c - c0)) % WIN, 1)[:, :128]
+            win = pltpu.roll(win, (span - (r - r0)) % span, 0)
+            flip = win[:BOX, :].T
+            out_ref[d, :, s * BOX : (s + 1) * BOX] = flip[:BOX, :BOX].astype(out_ref.dtype)
         return carry
 
-    lax.fori_loop(0, count, body, 0, unroll=2)
-
-
-def cut_patches(tiles, req):
-    count = req.shape[0]
+    lax.fori_loop(0, ends, body, 0)
+
+
+def cut_patches(tiles, req, ends, cap):
     flat = req.reshape(-1)
     return pl.pallas_call(
-        cut_kernel,
-        out_shape=jax.ShapeDtypeStruct((count, BOX, BOX), tiles.dtype),
+        functools.partial(cut_kernel, cap),
+        out_shape=jax.ShapeDtypeStruct((ends, BOX, cap * BOX), tiles.dtype),
         grid_spec=pltpu.PrefetchScalarGridSpec(
             num_scalar_prefetch=1,
             grid=(1,),
             in_specs=[pl.BlockSpec(tiles.shape, lambda i, q: (0, 0, 0))],
-            out_specs=pl.BlockSpec((count, BOX, BOX), lambda i, q: (0, 0, 0)),
+            out_specs=pl.BlockSpec((ends, BOX, cap * BOX), lambda i, q: (0, 0, 0)),
         ),
         cost_estimate=pl.CostEstimate(
-            flops=count * BOX * WIN * 64,
+            flops=ends * cap * BOX * WIN * 64,
             transcendentals=0,
-            bytes_accessed=tiles.size * 2 + count * BOX * BOX * 2,
+            bytes_accessed=tiles.size * 2 + ends * cap * BOX * BOX * 2,
         ),
     )(flat, tiles)
 
@@ -145,19 +147,22 @@
     )
     wanted = jnp.sum(jnp.where(spot[..., None], values[None, None], 0), axis=2)
     asked = lax.all_to_all(wanted, "dev", split_axis=0, concat_axis=0, tiled=True)
-    patches_cut = cut_patches(tiles, asked.reshape(ndev * cap, 3)).reshape(ndev, cap * BOX, BOX)
+    patches_cut = cut_patches(tiles, asked.reshape(ndev * cap, 3), ndev, cap)
     arrived = lax.all_to_all(patches_cut, "dev", split_axis=0, concat_axis=0, tiled=True)
-    arrived = arrived.reshape(ndev, cap, BOX, BOX)
-    patch = arrived[owner, slot].reshape(count, TILTS, BOX, BOX)
+    rows_of = arrived[owner]
+    flipped = sum(
+        jnp.where(slot[:, None, None] == s, rows_of[:, :, s * BOX : (s + 1) * BOX], 0)
+        for s in range(cap)
+    ).reshape(count, TILTS, BOX, BOX)
     padded = TILTS + TILTS % 2
-    pmat = patch.transpose(0, 2, 1, 3)
-    pmat = jnp.pad(pmat, ((0, 0), (0, 0), (0, padded - TILTS), (0, 0))).reshape(
-        count * BOX, padded * BOX
-    )
+    flipped = jnp.pad(flipped, ((0, 0), (0, padded - TILTS), (0, 0), (0, 0)))
+    flipped = flipped.reshape(count, padded * BOX, BOX)
     xs_np, zs_np = touched_points()
     xs, zs = jnp.asarray(xs_np), jnp.asarray(zs_np)
-    volume = jnp.dot(pmat, back_points(padded, xs, zs), preferred_element_type=jnp.float32)
-    volume = volume.astype(jnp.bfloat16)
+    volume = jnp.einsum(
+        "pky,kn->pyn", flipped, back_points(padded, xs, zs), preferred_element_type=jnp.float32
+    )
+    volume = volume.astype(jnp.bfloat16).reshape(count * BOX, xs.shape[0])
     sample = lax.optimization_barrier(sample_points(xs, zs))
     cyl = jnp.dot(volume, sample, preferred_element_type=jnp.float32)
     cyl = cyl.astype(jnp.bfloat16).reshape(count, BOX, ROTS * CYCLES)

time: 104 us -> 103 us (level)
  local copies, waits for them, and re-layouts: 11.4 us -> 7.93 us
  Pallas kernels: 7.37 us -> 10.7 us
    pallas_call x1, Pallas kernels: 7.37 us -> 10.7 us  [cut_patches(): pl.pallas_call(functools.partial(cut_kernel, cap), out_shape=jax.ShapeDty...]
    reshape x2 -> x0, local copies, waits for them, and re-layouts: 2.62 us -> none  [the longest x1 2.35 us: per_device(): cut_patches(tiles, asked.reshape(ndev * cap, 3))]
    all_gather x1, waiting for transfers between devices: 8.21 us -> 9.41 us  [per_device(): gathered = lax.all_gather(local_t[None], 'dev', axis=0, tiled=True)]
  transfers between devices with their start and end apart: 4 -> 4, of which waited for: 4 -> 4; matrix products, arithmetic and copies ran while one was open for 27% -> 24% of each run, Pallas kernels for 7% -> 10%
where the time goes in v6:
time: 103 us
  waiting for transfers between devices  33.5 us (33%)
  between operations  16.3 us (16%)
  starting transfers between devices  15 us (15%)
  other arithmetic  11.5 us (11%)
  Pallas kernels  10.7 us (10%)
  local copies, waits for them, and re-layouts  7.93 us (8%)
  matrix products  7.89 us (8%)
    all_to_all x1, waiting for transfers between devices, per_device(): lax.all_to_all(patches_cut, 'dev', split_axis=0, concat_axis=0, tiled=True)  12 us
    all_to_all x1, waiting for transfers between devices, per_device(): lax.all_to_all(placed, 'dev', split_axis=1, concat_axis=0, tiled=True)  10.9 us
    pallas_call x1, Pallas kernels, cut_patches(): pl.pallas_call(functools.partial(cut_kernel, cap), out_shape=jax.ShapeDty...  10.7 us
    all_gather x1, waiting for transfers between devices, per_device(): gathered = lax.all_gather(local_t[None], 'dev', axis=0, tiled=True)  9.41 us
    all_to_all x1, starting transfers between devices, per_device(): lax.all_to_all(wanted, 'dev', split_axis=0, concat_axis=0, tiled=True)  7.3 us
    all_to_all x1, starting transfers between devices, per_device(): lax.all_to_all(patches_cut, 'dev', split_axis=0, concat_axis=0, tiled=True)  4.6 us
    convert_element_type x1, other arithmetic, back_points(): return weight.reshape(count * BOX, xs.shape[0]).astype(jnp.bfloat16)  4.47 us
    dot_general x1, matrix products, per_device(): cyl = jnp.dot(volume, sample, preferred_element_type=jnp.float32)  4.17 us
  transfers between devices with their start and end apart: 4, of which 4 were waited for; matrix products, arithmetic and copies ran while one was open for 24% of the time, Pallas kernels for 10%

profile of v6, /device:TPU:0, one launch (start us, length us, event | category | flops | bytes accessed | tf_op | source)
XLA Modules:
  0.0 102.8 jit_solution(1148468827535910519)
XLA Ops:
  7.2 0.0 copy-start
  7.2 0.0 copy-start.1
  7.2 0.7 copy.90
  7.9 0.1 fusion.13
  8.0 0.2 select_reduce_fusion.1
  8.2 0.1 iota_compare_fusion.2
  8.3 0.1 iota_compare_fusion.3
  8.4 0.1 copy.68
  8.5 0.1 broadcast_and_fusion
  8.6 0.1 select_reduce_fusion
  8.7 0.7 copy.69
  9.4 7.3 %all-to-all-start = ((s32[32,2,3]{2,1,0:T(2,128)}), s32[32,2,3]{2,1,0:T(2,128)S(1)}, u32[]{:S(2)}, u32[]{:S(2)}) async-start(s32[32,2,3]{2,1,0:T(2,128)} %copy.69), calls=%async_computation | async-start | bytes 65536 | tf_op jit(solution)/shard_map/all_to_all | solution.py:149
  16.7 0.0 all-gather.2.cloned.1.call-start
  16.8 0.9 copy.73
  17.7 0.2 copy.74
  17.9 0.7 copy.75
  18.6 0.0 all-gather.2.cloned.1.call-update
  19.5 0.1 mul.199
  19.6 0.1 mul.202
  19.7 0.1 mul.203
  19.8 0.1 mul.205
  19.8 0.1 mul.206
  20.6 2.0 %multiply_convert_fusion.1 = bf16[1664,512]{1,0:T(8,128)(2,1)S(1)} fusion(f32[512]{0:T(512)S(1)} %get-tuple-element.5, f32[1664]{0:T(1024)} %constant.138, f32[512]{0:T(512)S(1)} %get-tuple-element.4, f32[1664]{0:T(1024)} %constant.137), kind=kLoop, calls=%fused_computation.3 | loop fusion | flops 8519680 | bytes 1721344 | tf_op jit(solution)/shard_map/convert_element_type | solution.py:81
  22.6 0.1 mul.213
  22.7 0.1 mul.214
  22.8 1.2 %all-to-all-done = s32[32,2,3]{2,1,0:T(2,128)S(1)} async-done(((s32[32,2,3]{2,1,0:T(2,128)}), s32[32,2,3]{2,1,0:T(2,128)S(1)}, u32[]{:S(2)}, u32[]{:S(2)}) %all-to-all-start) | async-done | bytes 800 | tf_op jit(solution)/shard_map/all_to_all | solution.py:149
  24.0 0.7 reshape_reshape.6.req_ref
  24.7 10.7 %shard_map.86 = bf16[32,64,128]{2,1,0:T(8,128)(2,1)} custom-call(s32[192]{0:T(256)} %reshape_reshape.6.req_ref, bf16[2,128,4096]{2,1,0:T(8,128)(2,1)} %tiles_ref.1), custom_call_target="tpu_custom_call" | custom-call | flops 67108864 | bytes 2621440 | tf_op jit(solution)/shard_map/pallas_call | solution.py:116
  35.4 4.6 %all-to-all-start.1 = ((bf16[32,64,128]{2,1,0:T(8,128)(2,1)}), bf16[32,64,128]{2,1,0:T(8,128)(2,1)S(1)}, u32[]{:S(2)}, u32[]{:S(2)}) async-start(bf16[32,64,128]{2,1,0:T(8,128)(2,1)} %shard_map.86), calls=%async_computation.1 | async-start | bytes 1048576 | tf_op jit(solution)/shard_map/all_to_all | solution.py:151
  40.1 0.0 copy-done
  40.1 0.0 copy-done.1
  40.1 0.1 add_add_fusion
  40.2 4.5 %multiply_convert_fusion = bf16[22,64,1664]{2,1,0:T(8,128)(2,1)} fusion(f32[22,1664]{1,0:T(8,128)S(1)} %add_add_fusion, pred[22]{0:T(512)(128)(4,1)S(1)} %iota_compare_fusion.5), kind=kLoop, calls=%fused_computation.2 | loop fusion | flops 16400384 | bytes 4832278 | tf_op jit(solution)/shard_map/convert_element_type | solution.py:72
  44.6 12.0 %all-to-all-done.1 = bf16[32,64,128]{2,1,0:T(8,128)(2,1)S(1)} async-done(((bf16[32,64,128]{2,1,0:T(8,128)(2,1)}), bf16[32,64,128]{2,1,0:T(8,128)(2,1)S(1)}, u32[]{:S(2)}, u32[]{:S(2)}) %all-to-all-start.1) | async-done | bytes 524320 | tf_op jit(solution)/shard_map/all_to_all | solution.py:151
  56.6 0.6 gather_fusion
  57.2 0.2 fusion.6
  57.4 0.1 pad.4
  57.5 4.2 %multiply_reduce_fusion.1 = (f32[]{:T(128)}, bf16[64,512]{1,0:T(8,128)(2,1)S(1)}) fusion(bf16[1664,512]{1,0:T(8,128)(2,1)S(1)} %multiply_convert_fusion.1, bf16[1408,64]{1,0:T(8,128)(2,1)S(1)} %bitcast.80, bf16[1408,1664]{1,0:T(8,128)(2,1)} %bitcast.75), kind=kOutput, calls=%fused_computation.28 | convolution fusion | flops 409182208 | bytes 6635524 | tf_op jit(solution)/shard_map/dot_general | solution.py:167
  61.7 0.1 copy.70
  61.8 1.3 %gather_fusion.1 = bf16[512,64]{1,0:T(8,128)(2,1)S(1)} fusion(bf16[64,512]{0,1:T(8,128)(2,1)S(1)} %copy.70, s32[1024]{0:T(1024)S(1)} %pad_clamp_fusion), kind=kCustom, calls=%fused_computation.1 | custom fusion | bytes 133120 | tf_op jit(solution)/shard_map/jit(take_along_axis)/gather | solution.py:197
  63.2 0.1 select_bitcast_fusion
  63.3 0.1 copy.81
  63.4 0.1 mul.217
  63.5 1.1 %broadcast_multiply_fusion = bf16[1,32,32,512]{3,2,0,1:T(8,128)(2,1)} fusion(bf16[1,32,32,512]{3,2,0,1:T(8,128)(2,1)S(1)} %bitcast.77, bf16[32]{0:T(256)(128)(2,1)S(1)} %mul.214), kind=kLoop, calls=%fused_computation.16 | loop fusion | flops 524288 | bytes 2097216 | tf_op jit(solution)/shard_map/mul | solution.py:201
  64.6 3.0 %all-to-all-start.2 = ((bf16[1,32,32,512]{3,2,0,1:T(8,128)(2,1)}), bf16[1,32,32,512]{3,2,0,1:T(8,128)(2,1)S(1)}, u32[]{:S(2)}, u32[]{:S(2)}) async-start(bf16[1,32,32,512]{3,2,0,1:T(8,128)(2,1)} %broadcast_multiply_fusion), calls=%async_computation.2 | async-start | bytes 2097152 | tf_op jit(solution)/shard_map/all_to_all | solution.py:203
  67.7 0.3 copy.71
  68.6 9.4 %all-gather.2.cloned.1.call-done = bf16[32,32,512]{2,1,0:T(8,128)(2,1)} async-done(((bf16[1,32,512]{2,1,0:T(8,128)(2,1)}), bf16[32,32,512]{2,1,0:T(8,128)(2,1)}) %all-gather.2.cloned.1.call-update) | async-done | bytes 1048592 | tf_op jit(solution)/shard_map/all_gather | solution.py:172
  78.1 1.6 %multiply_reduce_fusion = f32[32]{0:T(128)S(1)} fusion(bf16[32,32,512]{2,1,0:T(8,128)(2,1)} %all-gather.2.cloned.1.call-done), kind=kLoop, calls=%fused_computation.6 | loop fusion | flops 1572832 | bytes 1048704 | tf_op jit(solution)/shard_map/reduce_sum | solution.py:175
  79.7 0.1 reduce_sum.56
  79.7 0.1 reduce_sum.57
  79.9 1.6 %fusion.4 = f32[32,16,32]{2,0,1:T(8,128)S(1)} fusion(bf16[16,2,32,512]{3,2,1,0:T(8,128)(2,1)} %bitcast.78, bf16[1,32,2,512]{1,3,2,0:T(8,128)(2,1)S(1)} %bitcast.81), kind=kOutput, calls=%fused_computation.15 | convolution fusion | flops 16777216 | bytes 720896 | tf_op jit(solution)/shard_map/pfm,cgm->pfgc/dot_general | solution.py:182
  81.5 1.6 %fusion = f32[32,32,16]{1,0,2:T(8,128)S(1)} fusion(f32[32,16,32]{2,0,1:T(8,128)S(1)} %fusion.4, bf16[16,2,32,512]{3,2,1,0:T(8,128)(2,1)} %bitcast.79, bf16[1,32,2,512]{1,3,2,0:T(8,128)(2,1)S(1)} %bitcast.82), kind=kOutput, calls=%fused_computation.8 | convolution fusion | flops 16793600 | bytes 983040 | tf_op jit(solution)/shard_map/pfm,cgm->pfgc/dot_general | solution.py:182
  83.1 0.5 fusion.3
  83.6 0.7 reshape.604
  84.3 10.9 %all-to-all-done.2 = bf16[1,32,32,512]{3,2,0,1:T(8,128)(2,1)S(1)} async-done(((bf16[1,32,32,512]{3,2,0,1:T(8,128)(2,1)}), bf16[1,32,32,512]{3,2,0,1:T(8,128)(2,1)S(1)}, u32[]{:S(2)}, u32[]{:S(2)}) %all-to-all-start.2) | async-done | bytes 1048608 | tf_op jit(solution)/shard_map/all_to_all | solution.py:203
  95.1 0.8 convert_reduce_fusion
  (21 shorter events, 0.3 us)
Async XLA Ops:
  7.2 32.9 %copy-start = (f32[1664]{0:T(1024)S(1)}, f32[1664]{0:T(1024)}, u32[]{:S(2)}) copy-start(f32[1664]{0:T(1024)} %constant.137) | copy-start | bytes 19972
  7.2 32.9 %copy-start.1 = (f32[1664]{0:T(1024)S(1)}, f32[1664]{0:T(1024)}, u32[]{:S(2)}) copy-start(f32[1664]{0:T(1024)} %constant.138) | copy-start | bytes 19972
  9.4 14.6 %all-to-all-start = ((s32[32,2,3]{2,1,0:T(2,128)}), s32[32,2,3]{2,1,0:T(2,128)S(1)}, u32[]{:S(2)}, u32[]{:S(2)}) async-start(s32[32,2,3]{2,1,0:T(2,128)} %copy.69), calls=%async_computation | async-start | bytes 65536 | tf_op jit(solution)/shard_map/all_to_all | solution.py:149
  16.7 61.3 %all-gather.2.cloned.1.call-start = ((), (), s32[]{:S(2)}) async-start(), calls=%async_computation.3 | async-start | bytes 1081344 | tf_op jit(solution)/shard_map/all_gather | solution.py:172
  35.4 21.2 %all-to-all-start.1 = ((bf16[32,64,128]{2,1,0:T(8,128)(2,1)}), bf16[32,64,128]{2,1,0:T(8,128)(2,1)S(1)}, u32[]{:S(2)}, u32[]{:S(2)}) async-start(bf16[32,64,128]{2,1,0:T(8,128)(2,1)} %shard_map.86), calls=%async_computation.1 | async-start | bytes 1048576 | tf_op jit(solution)/shard_map/all_to_all | solution.py:151
  64.6 30.5 %all-to-all-start.2 = ((bf16[1,32,32,512]{3,2,0,1:T(8,128)(2,1)}), bf16[1,32,32,512]{3,2,0,1:T(8,128)(2,1)S(1)}, u32[]{:S(2)}, u32[]{:S(2)}) async-start(bf16[1,32,32,512]{3,2,0,1:T(8,128)(2,1)} %broadcast_multiply_fusion), calls=%async_computation.2 | async-start | bytes 2097152 | tf_op jit(solution)/shard_map/all_to_all | solution.py:203
Sparse Core Ops, SparseCore 0:
  21.0 56.9 all-gather.1

commit v7 on v6

--- a/solution.py
+++ b/solution.py
@@ -130,6 +130,19 @@
     )(flat, tiles)
 
 
+def double_gather(block, ndev):
+    me = lax.axis_index("dev")
+    step = 1
+    while step < ndev:
+        other = lax.ppermute(block, "dev", perm=[(i, i ^ step) for i in range(ndev)])
+        low = (me // step) % 2 == 0
+        block = jnp.where(
+            low, jnp.concatenate([block, other], axis=0), jnp.concatenate([other, block], axis=0)
+        )
+        step *= 2
+    return block
+
+
 def per_device(tiles, footprint, classes, rotations, references):
     ndev = lax.axis_size("dev")
     count = footprint.shape[0]
@@ -169,7 +182,7 @@
     owned = references.shape[0]
     parts = BOX // owned
     local_t = references.reshape(owned, ROTS, CYCLES).transpose(1, 0, 2).reshape(ROTS, owned * CYCLES)
-    gathered = lax.all_gather(local_t[None], "dev", axis=0, tiled=True)
+    gathered = double_gather(local_t[None], ndev)
     gathered = gathered.reshape(CLASSES, parts, ROTS, owned * CYCLES)
     ref_float = gathered.astype(jnp.float32)
     ref_power = jnp.mean(ref_float * ref_float, axis=(1, 2, 3))

time: 103 us -> 119 us (1.16)
  waiting for transfers between devices: 33.5 us -> 55.5 us
  between operations: 16.3 us -> 3.02 us
  starting transfers between devices: 15 us -> 25.4 us
  matrix products: 7.89 us -> 5.22 us
    ppermute x0 -> x5, waiting for transfers between devices: none -> 49.9 us  [double_gather(): lax.ppermute(block, 'dev', perm=[(i, i ^ step) for i in range(ndev)])]
    all_to_all x1, waiting for transfers between devices: 10.9 us -> 0.01 us  [per_device(): lax.all_to_all(placed, 'dev', split_axis=1, concat_axis=0, tiled=True)]
    ppermute x0 -> x5, starting transfers between devices: none -> 9.51 us  [double_gather(): lax.ppermute(block, 'dev', perm=[(i, i ^ step) for i in range(ndev)])]
    all_gather x1 -> x0, waiting for transfers between devices: 9.41 us -> none  [per_device(): gathered = lax.all_gather(local_t[None], 'dev', axis=0, tiled=True)]
    all_to_all x1, waiting for transfers between devices: 12 us -> 5.55 us  [per_device(): lax.all_to_all(patches_cut, 'dev', split_axis=0, concat_axis=0, tiled=True)]
    dot_general x2, matrix products: 3.2 us -> 0.59 us  [per_device(): jnp.einsum('pfm,cgm->pfgc', cyl_three[:, :, q], gathered[:, q], preferred...]
    all_to_all x1, waiting for transfers between devices: 1.24 us -> 0.01 us  [per_device(): lax.all_to_all(wanted, 'dev', split_axis=0, concat_axis=0, tiled=True)]
    all_to_all x1, starting transfers between devices: 4.6 us -> 5.83 us  [per_device(): lax.all_to_all(patches_cut, 'dev', split_axis=0, concat_axis=0, tiled=True)]
  transfers between devices with their start and end apart: 4 -> 8, of which waited for: 4 -> 4; matrix products, arithmetic and copies ran while one was open for 24% -> 18% of each run, Pallas kernels for 10% -> 9%
where the time goes in v7:
time: 119 us; the launch traced here: 118 us
  waiting for transfers between devices  55.5 us (47%)
  starting transfers between devices  25.4 us (21%)
  other arithmetic  10.7 us (9%)
  Pallas kernels  10.7 us (9%)
  local copies, waits for them, and re-layouts  7.55 us (6%)
  matrix products  5.22 us (4%)
  between operations  3.02 us (3%)
    ppermute x5, waiting for transfers between devices, double_gather(): lax.ppermute(block, 'dev', perm=[(i, i ^ step) for i in range(ndev)])  49.9 us
    pallas_call x1, Pallas kernels, cut_patches(): pl.pallas_call(functools.partial(cut_kernel, cap), out_shape=jax.ShapeDty...  10.7 us
    ppermute x5, starting transfers between devices, double_gather(): lax.ppermute(block, 'dev', perm=[(i, i ^ step) for i in range(ndev)])  9.51 us
    all_to_all x1, starting transfers between devices, per_device(): lax.all_to_all(wanted, 'dev', split_axis=0, concat_axis=0, tiled=True)  6.96 us
    all_to_all x1, starting transfers between devices, per_device(): lax.all_to_all(patches_cut, 'dev', split_axis=0, concat_axis=0, tiled=True)  5.83 us
    all_to_all x1, waiting for transfers between devices, per_device(): lax.all_to_all(patches_cut, 'dev', split_axis=0, concat_axis=0, tiled=True)  5.55 us
    convert_element_type x1, other arithmetic, back_points(): return weight.reshape(count * BOX, xs.shape[0]).astype(jnp.bfloat16)  4.49 us
    dot_general x1, matrix products, per_device(): cyl = jnp.dot(volume, sample, preferred_element_type=jnp.float32)  4.17 us
  transfers between devices with their start and end apart: 8, of which 4 were waited for; matrix products, arithmetic and copies ran while one was open for 18% of the time, Pallas kernels for 9%

profile of v7, /device:TPU:0, one launch (start us, length us, event | category | flops | bytes accessed | tf_op | source)
XLA Modules:
  0.0 118.1 jit_solution(8734457267485138971)
XLA Ops:
  0.6 0.9 copy.77
  1.5 0.2 copy.78
  1.7 0.5 collective-permute-start
  2.2 0.7 copy.100
  3.0 0.1 fusion.12
  3.1 0.2 select_reduce_fusion.1
  3.3 0.1 iota_compare_fusion.2
  3.3 0.1 iota_compare_fusion.3
  3.4 0.1 copy.84
  3.5 0.1 broadcast_and_fusion
  3.6 0.1 select_reduce_fusion
  3.8 0.7 copy.85
  4.5 7.0 %all-to-all-start = ((s32[32,2,3]{2,1,0:T(2,128)}), s32[32,2,3]{2,1,0:T(2,128)S(1)}, u32[]{:S(2)}, u32[]{:S(2)}) async-start(s32[32,2,3]{2,1,0:T(2,128)} %copy.85), calls=%async_computation | async-start | bytes 65536 | tf_op jit(solution)/shard_map/all_to_all | solution.py:162
  11.7 0.1 mul.199
  11.7 0.1 mul.202
  11.8 0.1 mul.203
  11.9 0.1 mul.205
  12.0 0.1 mul.206
  12.7 0.8 add_add_fusion
  13.5 0.0 copy-start
  13.5 0.0 copy-start.1
  13.6 4.5 %multiply_convert_fusion = bf16[22,64,1664]{2,1,0:T(8,128)(2,1)} fusion(f32[22,1664]{1,0:T(8,128)S(1)} %add_add_fusion, pred[22]{0:T(512)(128)(4,1)S(1)} %iota_compare_fusion.5), kind=kLoop, calls=%fused_computation.2 | loop fusion | flops 16400384 | bytes 4832278 | tf_op jit(solution)/shard_map/convert_element_type | solution.py:72
  18.7 0.0 all-to-all-done
  18.7 0.7 reshape_reshape.6.req_ref
  19.4 10.7 %shard_map.86 = bf16[32,64,128]{2,1,0:T(8,128)(2,1)} custom-call(s32[192]{0:T(256)} %reshape_reshape.6.req_ref, bf16[2,128,4096]{2,1,0:T(8,128)(2,1)} %tiles_ref.1), custom_call_target="tpu_custom_call" | custom-call | flops 67108864 | bytes 2621440 | tf_op jit(solution)/shard_map/pallas_call | solution.py:116
  30.2 5.8 %all-to-all-start.1 = ((bf16[32,64,128]{2,1,0:T(8,128)(2,1)}), bf16[32,64,128]{2,1,0:T(8,128)(2,1)S(1)}, u32[]{:S(2)}, u32[]{:S(2)}) async-start(bf16[32,64,128]{2,1,0:T(8,128)(2,1)} %shard_map.86), calls=%async_computation.1 | async-start | bytes 1048576 | tf_op jit(solution)/shard_map/all_to_all | solution.py:164
  36.1 1.3 %multiply_convert_fusion.1 = bf16[1664,512]{1,0:T(8,128)(2,1)S(1)} fusion(f32[512]{0:T(512)S(1)} %get-tuple-element.7, f32[1664]{0:T(1024)S(1)} %copy-done.1, f32[512]{0:T(512)S(1)} %get-tuple-element.6, f32[1664]{0:T(1024)S(1)} %copy-done), kind=kLoop, calls=%fused_computation.3 | loop fusion | flops 8519680 | bytes 1721344 | tf_op jit(solution)/shard_map/convert_element_type | solution.py:81
  37.4 0.1 copy.79
  37.5 0.1 mul.213
  37.6 0.1 mul.214
  37.7 0.0 collective-permute-done
  37.7 0.1 copy.80
  37.8 1.8 %collective-permute-start.1 = (bf16[2,32,512]{2,1,0:T(8,128)(2,1)S(1)}, bf16[2,32,512]{2,1,0:T(8,128)(2,1)S(1)}, u32[]{:S(2)}, u32[]{:S(2)}) collective-permute-start(bf16[2,32,512]{2,1,0:T(8,128)(2,1)S(1)} %maximum_select_fusion.4), channel_id=1, source_target_pairs={{0,2},{1,3},{2,0},{3,1},{4,6},{5,7},{6,4},{7,5},{8,10},{9,11},{10,... | collective-permute-start | bytes 196616 | tf_op jit(solution)/shard_map/ppermute | solution.py:137
  39.6 4.9 %collective-permute-done.1 = bf16[2,32,512]{2,1,0:T(8,128)(2,1)S(1)} collective-permute-done((bf16[2,32,512]{2,1,0:T(8,128)(2,1)S(1)}, bf16[2,32,512]{2,1,0:T(8,128)(2,1)S(1)}, u32[]{:S(2)}, u32[]{:S(2)}) %collective-permute-start.1) | collective-permute-done | bytes 65568 | tf_op jit(solution)/shard_map/ppermute | solution.py:137
  44.6 1.4 %collective-permute-start.2 = (bf16[4,32,512]{2,1,0:T(8,128)(2,1)S(1)}, bf16[4,32,512]{2,1,0:T(8,128)(2,1)S(1)}, u32[]{:S(2)}, u32[]{:S(2)}) collective-permute-start(bf16[4,32,512]{2,1,0:T(8,128)(2,1)S(1)} %maximum_select_fusion.3), channel_id=1, source_target_pairs={{0,4},{1,5},{2,6},{3,7},{4,0},{5,1},{6,2},{7,3},{8,12},{9,13},{10,... | collective-permute-start | bytes 393224 | tf_op jit(solution)/shard_map/ppermute | solution.py:137
  46.0 5.5 %all-to-all-done.1 = bf16[32,64,128]{2,1,0:T(8,128)(2,1)S(1)} async-done(((bf16[32,64,128]{2,1,0:T(8,128)(2,1)}), bf16[32,64,128]{2,1,0:T(8,128)(2,1)S(1)}, u32[]{:S(2)}, u32[]{:S(2)}) %all-to-all-start.1) | async-done | bytes 524320 | tf_op jit(solution)/shard_map/all_to_all | solution.py:164
  51.6 0.6 gather_fusion
  52.2 0.2 fusion.6
  52.4 0.1 pad.4
  52.5 4.2 %multiply_reduce_fusion.1 = (f32[]{:T(128)}, bf16[64,512]{1,0:T(8,128)(2,1)S(1)}) fusion(bf16[1664,512]{1,0:T(8,128)(2,1)S(1)} %multiply_convert_fusion.1, bf16[1408,64]{1,0:T(8,128)(2,1)S(1)} %bitcast.79, bf16[1408,1664]{1,0:T(8,128)(2,1)} %bitcast.74), kind=kOutput, calls=%fused_computation.31 | convolution fusion | flops 409182208 | bytes 6635524 | tf_op jit(solution)/shard_map/dot_general | solution.py:180
  56.7 0.1 copy.86
  56.8 1.3 %gather_fusion.1 = bf16[512,64]{1,0:T(8,128)(2,1)S(1)} fusion(bf16[64,512]{0,1:T(8,128)(2,1)S(1)} %copy.86, s32[1024]{0:T(1024)S(1)} %pad_clamp_fusion), kind=kCustom, calls=%fused_computation.1 | custom fusion | bytes 133120 | tf_op jit(solution)/shard_map/jit(take_along_axis)/gather | solution.py:210
  58.1 0.1 select_bitcast_fusion
  58.3 0.1 copy.93
  58.4 0.1 mul.217
  58.5 1.1 broadcast_multiply_fusion
  59.6 3.1 %all-to-all-start.2 = ((bf16[1,32,32,512]{3,2,0,1:T(8,128)(2,1)}), bf16[1,32,32,512]{3,2,0,1:T(8,128)(2,1)S(1)}, u32[]{:S(2)}, u32[]{:S(2)}) async-start(bf16[1,32,32,512]{3,2,0,1:T(8,128)(2,1)} %broadcast_multiply_fusion), calls=%async_computation.2 | async-start | bytes 2097152 | tf_op jit(solution)/shard_map/all_to_all | solution.py:216
  62.7 0.0 collective-permute-done.2
  62.7 1.8 %collective-permute-start.3 = (bf16[8,32,512]{2,1,0:T(8,128)(2,1)S(1)}, bf16[8,32,512]{2,1,0:T(8,128)(2,1)S(1)}, u32[]{:S(2)}, u32[]{:S(2)}) collective-permute-start(bf16[8,32,512]{2,1,0:T(8,128)(2,1)S(1)} %maximum_select_fusion.2), channel_id=1, source_target_pairs={{0,8},{1,9},{2,10},{3,11},{4,12},{5,13},{6,14},{7,15},{8,0},{9,1},... | collective-permute-start | bytes 786440 | tf_op jit(solution)/shard_map/ppermute | solution.py:137
  64.6 22.0 %collective-permute-done.3 = bf16[8,32,512]{2,1,0:T(8,128)(2,1)S(1)} collective-permute-done((bf16[8,32,512]{2,1,0:T(8,128)(2,1)S(1)}, bf16[8,32,512]{2,1,0:T(8,128)(2,1)S(1)}, u32[]{:S(2)}, u32[]{:S(2)}) %collective-permute-start.3) | collective-permute-done | bytes 262176 | tf_op jit(solution)/shard_map/ppermute | solution.py:137
  86.6 0.1 maximum_select_fusion.1
  86.7 3.9 %collective-permute-start.4 = (bf16[16,32,512]{2,1,0:T(8,128)(2,1)S(1)}, bf16[16,32,512]{2,1,0:T(8,128)(2,1)S(1)}, u32[]{:S(2)}, u32[]{:S(2)}) collective-permute-start(bf16[16,32,512]{2,1,0:T(8,128)(2,1)S(1)} %maximum_select_fusion.1), channel_id=1, source_target_pairs={{0,16},{1,17},{2,18},{3,19},{4,20},{5,21},{6,22},{7,23},{8,24},{9,... | collective-permute-start | bytes 1572872 | tf_op jit(solution)/shard_map/ppermute | solution.py:137
  90.6 22.9 %collective-permute-done.4 = bf16[16,32,512]{2,1,0:T(8,128)(2,1)S(1)} collective-permute-done((bf16[16,32,512]{2,1,0:T(8,128)(2,1)S(1)}, bf16[16,32,512]{2,1,0:T(8,128)(2,1)S(1)}, u32[]{:S(2)}, u32[]{:S(2)}) %collective-permute-start.4) | collective-permute-done | bytes 524320 | tf_op jit(solution)/shard_map/ppermute | solution.py:137
  113.5 0.7 multiply_reduce_fusion
  114.3 0.1 reduce_sum.56
  114.3 0.1 reduce_sum.57
  114.5 0.3 copy.87
  114.8 0.3 fusion.4
  115.1 0.3 fusion
  115.4 0.2 copy.91
  116.2 0.5 fusion.3
  116.7 0.7 reshape.605
  117.3 0.0 all-to-all-done.2
  117.3 0.8 convert_reduce_fusion
  (26 shorter events, 0.4 us)
Async XLA Ops:
  1.7 35.9 %collective-permute-start = (bf16[1,32,512]{1,2,0:T(8,128)(2,1)S(1)}, bf16[1,32,512]{1,2,0:T(8,128)(2,1)S(1)}, u32[]{:S(2)}, u32[]{:S(2)}) collective-permute-start(bf16[1,32,512]{1,2,0:T(8,128)(2,1)S(1)} %bitcast.82), channel_id=1, source_target_pairs={{0,1},{1,0},{2,3},{3,2},{4,5},{5,4},{6,7},{7,6},{8,9},{9,8},{10,11... | collective-permute-start | bytes 98312 | tf_op jit(solution)/shard_map/ppermute | solution.py:137
  4.5 14.2 %all-to-all-start = ((s32[32,2,3]{2,1,0:T(2,128)}), s32[32,2,3]{2,1,0:T(2,128)S(1)}, u32[]{:S(2)}, u32[]{:S(2)}) async-start(s32[32,2,3]{2,1,0:T(2,128)} %copy.85), calls=%async_computation | async-start | bytes 65536 | tf_op jit(solution)/shard_map/all_to_all | solution.py:162
  13.5 22.5 %copy-start = (f32[1664]{0:T(1024)S(1)}, f32[1664]{0:T(1024)}, u32[]{:S(2)}) copy-start(f32[1664]{0:T(1024)} %constant.215) | copy-start | bytes 19972
  13.5 22.5 %copy-start.1 = (f32[1664]{0:T(1024)S(1)}, f32[1664]{0:T(1024)}, u32[]{:S(2)}) copy-start(f32[1664]{0:T(1024)} %constant.216) | copy-start | bytes 19972
  30.2 21.4 %all-to-all-start.1 = ((bf16[32,64,128]{2,1,0:T(8,128)(2,1)}), bf16[32,64,128]{2,1,0:T(8,128)(2,1)S(1)}, u32[]{:S(2)}, u32[]{:S(2)}) async-start(bf16[32,64,128]{2,1,0:T(8,128)(2,1)} %shard_map.86), calls=%async_computation.1 | async-start | bytes 1048576 | tf_op jit(solution)/shard_map/all_to_all | solution.py:164
  37.8 6.8 %collective-permute-start.1 = (bf16[2,32,512]{2,1,0:T(8,128)(2,1)S(1)}, bf16[2,32,512]{2,1,0:T(8,128)(2,1)S(1)}, u32[]{:S(2)}, u32[]{:S(2)}) collective-permute-start(bf16[2,32,512]{2,1,0:T(8,128)(2,1)S(1)} %maximum_select_fusion.4), channel_id=1, source_target_pairs={{0,2},{1,3},{2,0},{3,1},{4,6},{5,7},{6,4},{7,5},{8,10},{9,11},{10,... | collective-permute-start | bytes 196616 | tf_op jit(solution)/shard_map/ppermute | solution.py:137
  44.6 18.1 %collective-permute-start.2 = (bf16[4,32,512]{2,1,0:T(8,128)(2,1)S(1)}, bf16[4,32,512]{2,1,0:T(8,128)(2,1)S(1)}, u32[]{:S(2)}, u32[]{:S(2)}) collective-permute-start(bf16[4,32,512]{2,1,0:T(8,128)(2,1)S(1)} %maximum_select_fusion.3), channel_id=1, source_target_pairs={{0,4},{1,5},{2,6},{3,7},{4,0},{5,1},{6,2},{7,3},{8,12},{9,13},{10,... | collective-permute-start | bytes 393224 | tf_op jit(solution)/shard_map/ppermute | solution.py:137
  59.6 57.7 %all-to-all-start.2 = ((bf16[1,32,32,512]{3,2,0,1:T(8,128)(2,1)}), bf16[1,32,32,512]{3,2,0,1:T(8,128)(2,1)S(1)}, u32[]{:S(2)}, u32[]{:S(2)}) async-start(bf16[1,32,32,512]{3,2,0,1:T(8,128)(2,1)} %broadcast_multiply_fusion), calls=%async_computation.2 | async-start | bytes 2097152 | tf_op jit(solution)/shard_map/all_to_all | solution.py:216
  62.7 23.9 %collective-permute-start.3 = (bf16[8,32,512]{2,1,0:T(8,128)(2,1)S(1)}, bf16[8,32,512]{2,1,0:T(8,128)(2,1)S(1)}, u32[]{:S(2)}, u32[]{:S(2)}) collective-permute-start(bf16[8,32,512]{2,1,0:T(8,128)(2,1)S(1)} %maximum_select_fusion.2), channel_id=1, source_target_pairs={{0,8},{1,9},{2,10},{3,11},{4,12},{5,13},{6,14},{7,15},{8,0},{9,1},... | collective-permute-start | bytes 786440 | tf_op jit(solution)/shard_map/ppermute | solution.py:137
  86.7 26.8 %collective-permute-start.4 = (bf16[16,32,512]{2,1,0:T(8,128)(2,1)S(1)}, bf16[16,32,512]{2,1,0:T(8,128)(2,1)S(1)}, u32[]{:S(2)}, u32[]{:S(2)}) collective-permute-start(bf16[16,32,512]{2,1,0:T(8,128)(2,1)S(1)} %maximum_select_fusion.1), channel_id=1, source_target_pairs={{0,16},{1,17},{2,18},{3,19},{4,20},{5,21},{6,22},{7,23},{8,24},{9,... | collective-permute-start | bytes 1572872 | tf_op jit(solution)/shard_map/ppermute | solution.py:137

commit v8 on v7

--- a/solution.py
+++ b/solution.py
@@ -132,15 +132,18 @@
 
 def double_gather(block, ndev):
     me = lax.axis_index("dev")
-    step = 1
-    while step < ndev:
+    bits = ndev.bit_length() - 1
+    for level in range(bits):
+        step = ndev >> (level + 1)
         other = lax.ppermute(block, "dev", perm=[(i, i ^ step) for i in range(ndev)])
         low = (me // step) % 2 == 0
         block = jnp.where(
             low, jnp.concatenate([block, other], axis=0), jnp.concatenate([other, block], axis=0)
         )
-        step *= 2
-    return block
+    rest = block.shape[1:]
+    block = block.reshape((2,) * bits + rest)
+    block = block.transpose(tuple(range(bits))[::-1] + tuple(range(bits, block.ndim)))
+    return block.reshape((ndev,) + rest)
 
 
 def per_device(tiles, footprint, classes, rotations, references):

time: 119 us -> 96.5 us (0.81)
  waiting for transfers between devices: 55.5 us -> 33.9 us
  starting transfers between devices: 25.4 us -> 24.2 us
    ppermute x5, waiting for transfers between devices: 49.9 us -> 13.5 us  [double_gather(): lax.ppermute(block, 'dev', perm=[(i, i ^ step) for i in range(ndev)])]
    all_to_all x1, waiting for transfers between devices: 0.01 us -> 20.5 us  [per_device(): lax.all_to_all(placed, 'dev', split_axis=1, concat_axis=0, tiled=True)]
    all_to_all x1, waiting for transfers between devices: 5.55 us -> 0.01 us  [per_device(): lax.all_to_all(patches_cut, 'dev', split_axis=0, concat_axis=0, tiled=True)]
    all_to_all x1, starting transfers between devices: 5.83 us -> 3.72 us  [per_device(): lax.all_to_all(patches_cut, 'dev', split_axis=0, concat_axis=0, tiled=True)]
    all_to_all x1, starting transfers between devices: 3.07 us -> 5.03 us  [per_device(): lax.all_to_all(placed, 'dev', split_axis=1, concat_axis=0, tiled=True)]
    ppermute x5, starting transfers between devices: 9.51 us -> 8.11 us  [double_gather(): lax.ppermute(block, 'dev', perm=[(i, i ^ step) for i in range(ndev)])]
  transfers between devices with their start and end apart: 8 -> 8, of which waited for: 4 -> 4; matrix products, arithmetic and copies ran while one was open for 18% -> 22% of each run, Pallas kernels for 9% -> 11%
where the time goes in v8:
time: 96.5 us; the launch traced here: 95.9 us
  waiting for transfers between devices  33.9 us (35%)
  starting transfers between devices  24.2 us (25%)
  other arithmetic  11.1 us (12%)
  Pallas kernels  10.7 us (11%)
  local copies, waits for them, and re-layouts  7.76 us (8%)
  matrix products  5.21 us (5%)
  between operations  2.99 us (3%)
    all_to_all x1, waiting for transfers between devices, per_device(): lax.all_to_all(placed, 'dev', split_axis=1, concat_axis=0, tiled=True)  20.5 us
    ppermute x5, waiting for transfers between devices, double_gather(): lax.ppermute(block, 'dev', perm=[(i, i ^ step) for i in range(ndev)])  13.5 us
    pallas_call x1, Pallas kernels, cut_patches(): pl.pallas_call(functools.partial(cut_kernel, cap), out_shape=jax.ShapeDty...  10.7 us
    ppermute x5, starting transfers between devices, double_gather(): lax.ppermute(block, 'dev', perm=[(i, i ^ step) for i in range(ndev)])  8.11 us
    all_to_all x1, starting transfers between devices, per_device(): lax.all_to_all(wanted, 'dev', split_axis=0, concat_axis=0, tiled=True)  7.3 us
    all_to_all x1, starting transfers between devices, per_device(): lax.all_to_all(placed, 'dev', split_axis=1, concat_axis=0, tiled=True)  5.03 us
    convert_element_type x1, other arithmetic, back_points(): return weight.reshape(count * BOX, xs.shape[0]).astype(jnp.bfloat16)  4.49 us
    dot_general x1, matrix products, per_device(): cyl = jnp.dot(volume, sample, preferred_element_type=jnp.float32)  4.17 us
  transfers between devices with their start and end apart: 8, of which 4 were waited for; matrix products, arithmetic and copies ran while one was open for 22% of the time, Pallas kernels for 11%

profile of v8, /device:TPU:0, one launch (start us, length us, event | category | flops | bytes accessed | tf_op | source)
XLA Modules:
  0.0 95.9 jit_solution(5060217693341241098)
XLA Ops:
  0.6 0.7 copy.97
  1.4 0.1 iota_compare_fusion.3
  1.4 0.1 copy.83
  1.5 0.1 fusion.12
  1.7 0.2 select_reduce_fusion.1
  1.8 0.1 iota_compare_fusion.2
  1.9 0.1 broadcast_and_fusion
  2.0 0.1 select_reduce_fusion
  2.2 0.7 copy.84
  2.9 7.3 %all-to-all-start = ((s32[32,2,3]{2,1,0:T(2,128)}), s32[32,2,3]{2,1,0:T(2,128)S(1)}, u32[]{:S(2)}, u32[]{:S(2)}) async-start(s32[32,2,3]{2,1,0:T(2,128)} %copy.84), calls=%async_computation | async-start | bytes 65536 | tf_op jit(solution)/shard_map/all_to_all | solution.py:165
  10.2 0.9 copy.76
  11.1 0.2 copy.77
  11.3 2.7 %collective-permute-start = (bf16[1,32,512]{1,2,0:T(8,128)(2,1)S(1)}, bf16[1,32,512]{1,2,0:T(8,128)(2,1)S(1)}, u32[]{:S(2)}, u32[]{:S(2)}) collective-permute-start(bf16[1,32,512]{1,2,0:T(8,128)(2,1)S(1)} %bitcast.83), channel_id=1, source_target_pairs={{0,16},{1,17},{2,18},{3,19},{4,20},{5,21},{6,22},{7,23},{8,24},{9,... | collective-permute-start | bytes 98312 | tf_op jit(solution)/shard_map/ppermute | solution.py:138
  14.8 0.1 mul.206
  14.9 0.1 mul.207
  15.0 0.1 mul.203
  15.1 0.1 mul.204
  15.2 0.1 mul.200
  15.2 0.8 add_add_fusion
  16.1 2.0 %multiply_convert_fusion.1 = bf16[1664,512]{1,0:T(8,128)(2,1)S(1)} fusion(f32[512]{0:T(512)S(1)} %get-tuple-element.5, f32[1664]{0:T(1024)} %constant.216, f32[512]{0:T(512)S(1)} %get-tuple-element.4, f32[1664]{0:T(1024)} %constant.215), kind=kLoop, calls=%fused_computation.3 | loop fusion | flops 8519680 | bytes 1721344 | tf_op jit(solution)/shard_map/convert_element_type | solution.py:81
  18.1 4.5 %multiply_convert_fusion = bf16[22,64,1664]{2,1,0:T(8,128)(2,1)} fusion(f32[22,1664]{1,0:T(8,128)S(1)} %add_add_fusion, pred[22]{0:T(512)(128)(4,1)S(1)} %iota_compare_fusion.5), kind=kLoop, calls=%fused_computation.2 | loop fusion | flops 16400384 | bytes 4832278 | tf_op jit(solution)/shard_map/convert_element_type | solution.py:72
  22.6 0.0 all-to-all-done
  22.6 0.7 reshape_reshape.10.req_ref
  23.3 10.7 %shard_map.86 = bf16[32,64,128]{2,1,0:T(8,128)(2,1)} custom-call(s32[192]{0:T(256)} %reshape_reshape.10.req_ref, bf16[2,128,4096]{2,1,0:T(8,128)(2,1)} %tiles_ref.1), custom_call_target="tpu_custom_call" | custom-call | flops 67108864 | bytes 2621440 | tf_op jit(solution)/shard_map/pallas_call | solution.py:116
  34.0 3.7 %all-to-all-start.1 = ((bf16[32,64,128]{2,1,0:T(8,128)(2,1)}), bf16[32,64,128]{2,1,0:T(8,128)(2,1)S(1)}, u32[]{:S(2)}, u32[]{:S(2)}) async-start(bf16[32,64,128]{2,1,0:T(8,128)(2,1)} %shard_map.86), calls=%async_computation.1 | async-start | bytes 1048576 | tf_op jit(solution)/shard_map/all_to_all | solution.py:167
  37.8 0.1 copy.78
  38.6 0.0 collective-permute-done
  38.6 0.1 copy.79
  38.7 1.8 %collective-permute-start.1 = (bf16[2,32,512]{2,1,0:T(8,128)(2,1)S(1)}, bf16[2,32,512]{2,1,0:T(8,128)(2,1)S(1)}, u32[]{:S(2)}, u32[]{:S(2)}) collective-permute-start(bf16[2,32,512]{2,1,0:T(8,128)(2,1)S(1)} %maximum_select_fusion.4), channel_id=1, source_target_pairs={{0,8},{1,9},{2,10},{3,11},{4,12},{5,13},{6,14},{7,15},{8,0},{9,1},... | collective-permute-start | bytes 196616 | tf_op jit(solution)/shard_map/ppermute | solution.py:138
  40.6 7.8 %collective-permute-done.1 = bf16[2,32,512]{2,1,0:T(8,128)(2,1)S(1)} collective-permute-done((bf16[2,32,512]{2,1,0:T(8,128)(2,1)S(1)}, bf16[2,32,512]{2,1,0:T(8,128)(2,1)S(1)}, u32[]{:S(2)}, u32[]{:S(2)}) %collective-permute-start.1) | collective-permute-done | bytes 65568 | tf_op jit(solution)/shard_map/ppermute | solution.py:138
  48.3 1.7 %collective-permute-start.2 = (bf16[4,32,512]{2,1,0:T(8,128)(2,1)S(1)}, bf16[4,32,512]{2,1,0:T(8,128)(2,1)S(1)}, u32[]{:S(2)}, u32[]{:S(2)}) collective-permute-start(bf16[4,32,512]{2,1,0:T(8,128)(2,1)S(1)} %maximum_select_fusion.3), channel_id=1, source_target_pairs={{0,4},{1,5},{2,6},{3,7},{4,0},{5,1},{6,2},{7,3},{8,12},{9,13},{10,... | collective-permute-start | bytes 393224 | tf_op jit(solution)/shard_map/ppermute | solution.py:138
  50.1 0.1 mul.214
  50.2 0.1 mul.215
  50.3 4.0 %collective-permute-done.2 = bf16[4,32,512]{2,1,0:T(8,128)(2,1)S(1)} collective-permute-done((bf16[4,32,512]{2,1,0:T(8,128)(2,1)S(1)}, bf16[4,32,512]{2,1,0:T(8,128)(2,1)S(1)}, u32[]{:S(2)}, u32[]{:S(2)}) %collective-permute-start.2) | collective-permute-done | bytes 131104 | tf_op jit(solution)/shard_map/ppermute | solution.py:138
  54.3 1.5 %collective-permute-start.3 = (bf16[8,32,512]{2,1,0:T(8,128)(2,1)S(1)}, bf16[8,32,512]{2,1,0:T(8,128)(2,1)S(1)}, u32[]{:S(2)}, u32[]{:S(2)}) collective-permute-start(bf16[8,32,512]{2,1,0:T(8,128)(2,1)S(1)} %maximum_select_fusion.2), channel_id=1, source_target_pairs={{0,2},{1,3},{2,0},{3,1},{4,6},{5,7},{6,4},{7,5},{8,10},{9,11},{10,... | collective-permute-start | bytes 786440 | tf_op jit(solution)/shard_map/ppermute | solution.py:138
  55.8 0.0 all-to-all-done.1
  55.8 0.6 gather_fusion
  56.4 0.2 fusion.6
  56.7 0.1 pad.4
  56.7 4.2 %multiply_reduce_fusion.1 = (f32[]{:T(128)}, bf16[64,512]{1,0:T(8,128)(2,1)S(1)}) fusion(bf16[1664,512]{1,0:T(8,128)(2,1)S(1)} %multiply_convert_fusion.1, bf16[1408,64]{1,0:T(8,128)(2,1)S(1)} %bitcast.80, bf16[1408,1664]{1,0:T(8,128)(2,1)} %bitcast.73), kind=kOutput, calls=%fused_computation.31 | convolution fusion | flops 409182208 | bytes 6635524 | tf_op jit(solution)/shard_map/dot_general | solution.py:183
  60.9 0.1 copy.85
  61.0 1.3 %gather_fusion.1 = bf16[512,64]{1,0:T(8,128)(2,1)S(1)} fusion(bf16[64,512]{0,1:T(8,128)(2,1)S(1)} %copy.85, s32[1024]{0:T(1024)S(1)} %pad_clamp_fusion), kind=kCustom, calls=%fused_computation.1 | custom fusion | bytes 133120 | tf_op jit(solution)/shard_map/jit(take_along_axis)/gather | solution.py:213
  62.4 0.1 select_bitcast_fusion
  62.5 0.1 copy.92
  62.6 0.1 mul.218
  62.7 1.1 %broadcast_multiply_fusion = bf16[1,32,32,512]{3,2,0,1:T(8,128)(2,1)} fusion(bf16[1,32,32,512]{3,2,0,1:T(8,128)(2,1)S(1)} %bitcast.77, bf16[32]{0:T(256)(128)(2,1)S(1)} %mul.215), kind=kLoop, calls=%fused_computation.18 | loop fusion | flops 524288 | bytes 2097216 | tf_op jit(solution)/shard_map/mul | solution.py:217
  63.9 5.0 %all-to-all-start.2 = ((bf16[1,32,32,512]{3,2,0,1:T(8,128)(2,1)}), bf16[1,32,32,512]{3,2,0,1:T(8,128)(2,1)S(1)}, u32[]{:S(2)}, u32[]{:S(2)}) async-start(bf16[1,32,32,512]{3,2,0,1:T(8,128)(2,1)} %broadcast_multiply_fusion), calls=%async_computation.2 | async-start | bytes 2097152 | tf_op jit(solution)/shard_map/all_to_all | solution.py:219
  68.9 0.0 collective-permute-done.3
  68.9 0.1 maximum_select_fusion.1
  69.0 0.3 collective-permute-start.4
  69.4 1.6 %collective-permute-done.4 = bf16[16,32,512]{2,1,0:T(8,128)(2,1)S(1)} collective-permute-done((bf16[16,32,512]{2,1,0:T(8,128)(2,1)S(1)}, bf16[16,32,512]{2,1,0:T(8,128)(2,1)S(1)}, u32[]{:S(2)}, u32[]{:S(2)}) %collective-permute-start.4) | collective-permute-done | bytes 524320 | tf_op jit(solution)/shard_map/ppermute | solution.py:138
  71.0 0.2 maximum_select_fusion
  71.2 0.1 copy.82
  71.3 0.3 multiply_reduce_fusion
  72.3 0.1 copy.90
  72.4 0.1 sqrt.12
  72.5 0.3 copy.86
  72.8 0.3 fusion.4
  73.1 0.3 fusion
  73.4 0.2 copy.89
  73.5 0.5 fusion.3
  74.0 0.7 reshape.615
  74.7 20.5 %all-to-all-done.2 = bf16[1,32,32,512]{3,2,0,1:T(8,128)(2,1)S(1)} async-done(((bf16[1,32,32,512]{3,2,0,1:T(8,128)(2,1)}), bf16[1,32,32,512]{3,2,0,1:T(8,128)(2,1)S(1)}, u32[]{:S(2)}, u32[]{:S(2)}) %all-to-all-start.2) | async-done | bytes 1048608 | tf_op jit(solution)/shard_map/all_to_all | solution.py:219
  95.1 0.8 convert_reduce_fusion
  (24 shorter events, 0.4 us)
Async XLA Ops:
  2.9 19.7 %all-to-all-start = ((s32[32,2,3]{2,1,0:T(2,128)}), s32[32,2,3]{2,1,0:T(2,128)S(1)}, u32[]{:S(2)}, u32[]{:S(2)}) async-start(s32[32,2,3]{2,1,0:T(2,128)} %copy.84), calls=%async_computation | async-start | bytes 65536 | tf_op jit(solution)/shard_map/all_to_all | solution.py:165
  11.3 27.3 %collective-permute-start = (bf16[1,32,512]{1,2,0:T(8,128)(2,1)S(1)}, bf16[1,32,512]{1,2,0:T(8,128)(2,1)S(1)}, u32[]{:S(2)}, u32[]{:S(2)}) collective-permute-start(bf16[1,32,512]{1,2,0:T(8,128)(2,1)S(1)} %bitcast.83), channel_id=1, source_target_pairs={{0,16},{1,17},{2,18},{3,19},{4,20},{5,21},{6,22},{7,23},{8,24},{9,... | collective-permute-start | bytes 98312 | tf_op jit(solution)/shard_map/ppermute | solution.py:138
  34.0 21.8 %all-to-all-start.1 = ((bf16[32,64,128]{2,1,0:T(8,128)(2,1)}), bf16[32,64,128]{2,1,0:T(8,128)(2,1)S(1)}, u32[]{:S(2)}, u32[]{:S(2)}) async-start(bf16[32,64,128]{2,1,0:T(8,128)(2,1)} %shard_map.86), calls=%async_computation.1 | async-start | bytes 1048576 | tf_op jit(solution)/shard_map/all_to_all | solution.py:167
  38.7 9.6 %collective-permute-start.1 = (bf16[2,32,512]{2,1,0:T(8,128)(2,1)S(1)}, bf16[2,32,512]{2,1,0:T(8,128)(2,1)S(1)}, u32[]{:S(2)}, u32[]{:S(2)}) collective-permute-start(bf16[2,32,512]{2,1,0:T(8,128)(2,1)S(1)} %maximum_select_fusion.4), channel_id=1, source_target_pairs={{0,8},{1,9},{2,10},{3,11},{4,12},{5,13},{6,14},{7,15},{8,0},{9,1},... | collective-permute-start | bytes 196616 | tf_op jit(solution)/shard_map/ppermute | solution.py:138
  48.3 6.0 %collective-permute-start.2 = (bf16[4,32,512]{2,1,0:T(8,128)(2,1)S(1)}, bf16[4,32,512]{2,1,0:T(8,128)(2,1)S(1)}, u32[]{:S(2)}, u32[]{:S(2)}) collective-permute-start(bf16[4,32,512]{2,1,0:T(8,128)(2,1)S(1)} %maximum_select_fusion.3), channel_id=1, source_target_pairs={{0,4},{1,5},{2,6},{3,7},{4,0},{5,1},{6,2},{7,3},{8,12},{9,13},{10,... | collective-permute-start | bytes 393224 | tf_op jit(solution)/shard_map/ppermute | solution.py:138
  54.3 14.6 %collective-permute-start.3 = (bf16[8,32,512]{2,1,0:T(8,128)(2,1)S(1)}, bf16[8,32,512]{2,1,0:T(8,128)(2,1)S(1)}, u32[]{:S(2)}, u32[]{:S(2)}) collective-permute-start(bf16[8,32,512]{2,1,0:T(8,128)(2,1)S(1)} %maximum_select_fusion.2), channel_id=1, source_target_pairs={{0,2},{1,3},{2,0},{3,1},{4,6},{5,7},{6,4},{7,5},{8,10},{9,11},{10,... | collective-permute-start | bytes 786440 | tf_op jit(solution)/shard_map/ppermute | solution.py:138
  63.9 31.3 %all-to-all-start.2 = ((bf16[1,32,32,512]{3,2,0,1:T(8,128)(2,1)}), bf16[1,32,32,512]{3,2,0,1:T(8,128)(2,1)S(1)}, u32[]{:S(2)}, u32[]{:S(2)}) async-start(bf16[1,32,32,512]{3,2,0,1:T(8,128)(2,1)} %broadcast_multiply_fusion), calls=%async_computation.2 | async-start | bytes 2097152 | tf_op jit(solution)/shard_map/all_to_all | solution.py:219
  69.0 2.0 %collective-permute-start.4 = (bf16[16,32,512]{2,1,0:T(8,128)(2,1)S(1)}, bf16[16,32,512]{2,1,0:T(8,128)(2,1)S(1)}, u32[]{:S(2)}, u32[]{:S(2)}) collective-permute-start(bf16[16,32,512]{2,1,0:T(8,128)(2,1)S(1)} %maximum_select_fusion.1), channel_id=1, source_target_pairs={{0,1},{1,0},{2,3},{3,2},{4,5},{5,4},{6,7},{7,6},{8,9},{9,8},{10,11... | collective-permute-start | bytes 1572872 | tf_op jit(solution)/shard_map/ppermute | solution.py:138

commit v9 on v8

--- a/solution.py
+++ b/solution.py
@@ -164,6 +164,10 @@
     wanted = jnp.sum(jnp.where(spot[..., None], values[None, None], 0), axis=2)
     asked = lax.all_to_all(wanted, "dev", split_axis=0, concat_axis=0, tiled=True)
     patches_cut = cut_patches(tiles, asked.reshape(ndev * cap, 3), ndev, cap)
+    xs_np, zs_np = touched_points()
+    xs, zs, patches_cut = lax.optimization_barrier(
+        (jnp.asarray(xs_np), jnp.asarray(zs_np), patches_cut)
+    )
     arrived = lax.all_to_all(patches_cut, "dev", split_axis=0, concat_axis=0, tiled=True)
     rows_of = arrived[owner]
     flipped = sum(
@@ -173,8 +177,6 @@
     padded = TILTS + TILTS % 2
     flipped = jnp.pad(flipped, ((0, 0), (0, padded - TILTS), (0, 0), (0, 0)))
     flipped = flipped.reshape(count, padded * BOX, BOX)
-    xs_np, zs_np = touched_points()
-    xs, zs = jnp.asarray(xs_np), jnp.asarray(zs_np)
     volume = jnp.einsum(
         "pky,kn->pyn", flipped, back_points(padded, xs, zs), preferred_element_type=jnp.float32
     )

time: 96.5 us -> 90.3 us (0.936)
  waiting for transfers between devices: 33.9 us -> 30.2 us
  other arithmetic: 11.1 us -> 9.63 us
  starting transfers between devices: 24.2 us -> 23.1 us
    ppermute x5, waiting for transfers between devices: 13.5 us -> 8.65 us  [double_gather(): lax.ppermute(block, 'dev', perm=[(i, i ^ step) for i in range(ndev)])]
    all_to_all x1, waiting for transfers between devices: 0.01 us -> 1.12 us  [per_device(): lax.all_to_all(wanted, 'dev', split_axis=0, concat_axis=0, tiled=True)]
    all_to_all x1, starting transfers between devices: 3.72 us -> 2.62 us  [per_device(): lax.all_to_all(patches_cut, 'dev', split_axis=0, concat_axis=0, tiled=True)]
  transfers between devices with their start and end apart: 8 -> 8, of which waited for: 4 -> 5; matrix products, arithmetic and copies ran while one was open for 22% -> 22% of each run, Pallas kernels for 11% -> 12%
where the time goes in v9:
time: 90.3 us; the launch traced here: 89.8 us
  waiting for transfers between devices  30.2 us (33%)
  starting transfers between devices  23.1 us (26%)
  Pallas kernels  10.8 us (12%)
  other arithmetic  9.63 us (11%)
  local copies, waits for them, and re-layouts  7.79 us (9%)
  matrix products  5.21 us (6%)
  between operations  3.09 us (3%)
    all_to_all x1, waiting for transfers between devices, per_device(): lax.all_to_all(placed, 'dev', split_axis=1, concat_axis=0, tiled=True)  20.5 us
    pallas_call x1, Pallas kernels, cut_patches(): pl.pallas_call(functools.partial(cut_kernel, cap), out_shape=jax.ShapeDty...  10.8 us
    ppermute x5, waiting for transfers between devices, double_gather(): lax.ppermute(block, 'dev', perm=[(i, i ^ step) for i in range(ndev)])  8.65 us
    ppermute x5, starting transfers between devices, double_gather(): lax.ppermute(block, 'dev', perm=[(i, i ^ step) for i in range(ndev)])  8.11 us
    all_to_all x1, starting transfers between devices, per_device(): lax.all_to_all(wanted, 'dev', split_axis=0, concat_axis=0, tiled=True)  7.3 us
    all_to_all x1, starting transfers between devices, per_device(): lax.all_to_all(placed, 'dev', split_axis=1, concat_axis=0, tiled=True)  5.03 us
    convert_element_type x1, other arithmetic, back_points(): return weight.reshape(count * BOX, xs.shape[0]).astype(jnp.bfloat16)  4.48 us
    dot_general x1, matrix products, per_device(): cyl = jnp.dot(volume, sample, preferred_element_type=jnp.float32)  4.17 us
  transfers between devices with their start and end apart: 8, of which 5 were waited for; matrix products, arithmetic and copies ran while one was open for 22% of the time, Pallas kernels for 12%

profile of v9, /device:TPU:0, one launch (start us, length us, event | category | flops | bytes accessed | tf_op | source)
XLA Modules:
  0.0 89.8 jit_solution(18437958410476916292)
XLA Ops:
  0.6 0.0 copy-start
  0.6 0.0 copy-start.1
  0.7 0.7 copy.97
  1.4 0.1 fusion.12
  1.5 0.2 select_reduce_fusion.1
  1.7 0.1 iota_compare_fusion.2
  1.8 0.1 iota_compare_fusion.3
  1.9 0.1 copy.83
  2.0 0.1 broadcast_and_fusion
  2.1 0.1 select_reduce_fusion
  2.2 0.7 copy.84
  2.9 7.3 %all-to-all-start = ((s32[32,2,3]{2,1,0:T(2,128)}), s32[32,2,3]{2,1,0:T(2,128)S(1)}, u32[]{:S(2)}, u32[]{:S(2)}) async-start(s32[32,2,3]{2,1,0:T(2,128)} %copy.84), calls=%async_computation | async-start | bytes 65536 | tf_op jit(solution)/shard_map/all_to_all | solution.py:165
  10.2 0.9 copy.76
  11.1 0.2 copy.77
  11.3 2.7 %collective-permute-start = (bf16[1,32,512]{1,2,0:T(8,128)(2,1)S(1)}, bf16[1,32,512]{1,2,0:T(8,128)(2,1)S(1)}, u32[]{:S(2)}, u32[]{:S(2)}) collective-permute-start(bf16[1,32,512]{1,2,0:T(8,128)(2,1)S(1)} %bitcast.83), channel_id=1, source_target_pairs={{0,16},{1,17},{2,18},{3,19},{4,20},{5,21},{6,22},{7,23},{8,24},{9,... | collective-permute-start | bytes 98312 | tf_op jit(solution)/shard_map/ppermute | solution.py:138
  15.0 0.1 mul.200
  15.1 0.1 mul.203
  15.1 0.1 mul.204
  15.2 0.1 mul.206
  15.3 0.1 mul.207
  16.1 0.1 copy.78
  16.2 0.1 mul.214
  16.3 0.1 mul.215
  16.4 1.1 %all-to-all-done = s32[32,2,3]{2,1,0:T(2,128)S(1)} async-done(((s32[32,2,3]{2,1,0:T(2,128)}), s32[32,2,3]{2,1,0:T(2,128)S(1)}, u32[]{:S(2)}, u32[]{:S(2)}) %all-to-all-start) | async-done | bytes 800 | tf_op jit(solution)/shard_map/all_to_all | solution.py:165
  17.5 0.7 reshape_reshape.10.req_ref
  18.2 10.8 %shard_map.86 = bf16[32,64,128]{2,1,0:T(8,128)(2,1)} custom-call(s32[192]{0:T(256)} %reshape_reshape.10.req_ref, bf16[2,128,4096]{2,1,0:T(8,128)(2,1)} %tiles_ref.1), custom_call_target="tpu_custom_call" | custom-call | flops 67108864 | bytes 2621440 | tf_op jit(solution)/shard_map/pallas_call | solution.py:116
  29.0 2.6 %all-to-all-start.1 = ((bf16[32,64,128]{2,1,0:T(8,128)(2,1)}), bf16[32,64,128]{2,1,0:T(8,128)(2,1)S(1)}, u32[]{:S(2)}, u32[]{:S(2)}) async-start(bf16[32,64,128]{2,1,0:T(8,128)(2,1)} %shard_map.86), calls=%async_computation.1 | async-start | bytes 1048576 | tf_op jit(solution)/shard_map/all_to_all | solution.py:171
  31.6 0.1 add_add_fusion
  31.7 0.0 collective-permute-done
  31.8 0.1 copy.79
  31.9 1.8 %collective-permute-start.1 = (bf16[2,32,512]{2,1,0:T(8,128)(2,1)S(1)}, bf16[2,32,512]{2,1,0:T(8,128)(2,1)S(1)}, u32[]{:S(2)}, u32[]{:S(2)}) collective-permute-start(bf16[2,32,512]{2,1,0:T(8,128)(2,1)S(1)} %maximum_select_fusion.4), channel_id=1, source_target_pairs={{0,8},{1,9},{2,10},{3,11},{4,12},{5,13},{6,14},{7,15},{8,0},{9,1},... | collective-permute-start | bytes 196616 | tf_op jit(solution)/shard_map/ppermute | solution.py:138
  33.7 4.5 %multiply_convert_fusion = bf16[22,64,1664]{2,1,0:T(8,128)(2,1)} fusion(f32[22,1664]{1,0:T(8,128)S(1)} %add_add_fusion, pred[22]{0:T(512)(128)(4,1)S(1)} %iota_compare_fusion.5), kind=kLoop, calls=%fused_computation.2 | loop fusion | flops 16400384 | bytes 4832278 | tf_op jit(solution)/shard_map/convert_element_type | solution.py:72
  38.2 4.0 %collective-permute-done.1 = bf16[2,32,512]{2,1,0:T(8,128)(2,1)S(1)} collective-permute-done((bf16[2,32,512]{2,1,0:T(8,128)(2,1)S(1)}, bf16[2,32,512]{2,1,0:T(8,128)(2,1)S(1)}, u32[]{:S(2)}, u32[]{:S(2)}) %collective-permute-start.1) | collective-permute-done | bytes 65568 | tf_op jit(solution)/shard_map/ppermute | solution.py:138
  42.2 1.7 %collective-permute-start.2 = (bf16[4,32,512]{2,1,0:T(8,128)(2,1)S(1)}, bf16[4,32,512]{2,1,0:T(8,128)(2,1)S(1)}, u32[]{:S(2)}, u32[]{:S(2)}) collective-permute-start(bf16[4,32,512]{2,1,0:T(8,128)(2,1)S(1)} %maximum_select_fusion.3), channel_id=1, source_target_pairs={{0,4},{1,5},{2,6},{3,7},{4,0},{5,1},{6,2},{7,3},{8,12},{9,13},{10,... | collective-permute-start | bytes 393224 | tf_op jit(solution)/shard_map/ppermute | solution.py:138
  43.9 1.2 %multiply_convert_fusion.1 = bf16[1664,512]{1,0:T(8,128)(2,1)S(1)} fusion(f32[512]{0:T(512)S(1)} %get-tuple-element.11, f32[1664]{0:T(1024)S(1)} %get-tuple-element.16, f32[512]{0:T(512)S(1)} %get-tuple-element.10, f32[1664]{0:T(1024)S(1)} %get-tuple-element.17), kind=kLoop, calls=%fused_computation.3 | loop fusion | flops 8519680 | bytes 1721344 | tf_op jit(solution)/shard_map/convert_element_type | solution.py:81
  45.2 3.0 %collective-permute-done.2 = bf16[4,32,512]{2,1,0:T(8,128)(2,1)S(1)} collective-permute-done((bf16[4,32,512]{2,1,0:T(8,128)(2,1)S(1)}, bf16[4,32,512]{2,1,0:T(8,128)(2,1)S(1)}, u32[]{:S(2)}, u32[]{:S(2)}) %collective-permute-start.2) | collective-permute-done | bytes 131104 | tf_op jit(solution)/shard_map/ppermute | solution.py:138
  48.2 1.5 %collective-permute-start.3 = (bf16[8,32,512]{2,1,0:T(8,128)(2,1)S(1)}, bf16[8,32,512]{2,1,0:T(8,128)(2,1)S(1)}, u32[]{:S(2)}, u32[]{:S(2)}) collective-permute-start(bf16[8,32,512]{2,1,0:T(8,128)(2,1)S(1)} %maximum_select_fusion.2), channel_id=1, source_target_pairs={{0,2},{1,3},{2,0},{3,1},{4,6},{5,7},{6,4},{7,5},{8,10},{9,11},{10,... | collective-permute-start | bytes 786440 | tf_op jit(solution)/shard_map/ppermute | solution.py:138
  49.7 0.6 gather_fusion
  50.3 0.2 fusion.6
  50.5 0.1 pad.4
  50.6 4.2 %multiply_reduce_fusion.1 = (f32[]{:T(128)}, bf16[64,512]{1,0:T(8,128)(2,1)S(1)}) fusion(bf16[1664,512]{1,0:T(8,128)(2,1)S(1)} %multiply_convert_fusion.1, bf16[1408,64]{1,0:T(8,128)(2,1)S(1)} %bitcast.80, bf16[1408,1664]{1,0:T(8,128)(2,1)} %bitcast.73), kind=kOutput, calls=%fused_computation.31 | convolution fusion | flops 409182208 | bytes 6635524 | tf_op jit(solution)/shard_map/dot_general | solution.py:185
  54.8 0.1 copy.85
  54.9 1.3 %gather_fusion.1 = bf16[512,64]{1,0:T(8,128)(2,1)S(1)} fusion(bf16[64,512]{0,1:T(8,128)(2,1)S(1)} %copy.85, s32[1024]{0:T(1024)S(1)} %pad_clamp_fusion), kind=kCustom, calls=%fused_computation.1 | custom fusion | bytes 133120 | tf_op jit(solution)/shard_map/jit(take_along_axis)/gather | solution.py:215
  56.2 0.1 select_bitcast_fusion
  56.4 0.1 copy.92
  56.5 0.1 mul.218
  56.6 1.1 %broadcast_multiply_fusion = bf16[1,32,32,512]{3,2,0,1:T(8,128)(2,1)} fusion(bf16[1,32,32,512]{3,2,0,1:T(8,128)(2,1)S(1)} %bitcast.77, bf16[32]{0:T(256)(128)(2,1)S(1)} %mul.215), kind=kLoop, calls=%fused_computation.18 | loop fusion | flops 524288 | bytes 2097216 | tf_op jit(solution)/shard_map/mul | solution.py:219
  57.7 5.0 %all-to-all-start.2 = ((bf16[1,32,32,512]{3,2,0,1:T(8,128)(2,1)}), bf16[1,32,32,512]{3,2,0,1:T(8,128)(2,1)S(1)}, u32[]{:S(2)}, u32[]{:S(2)}) async-start(bf16[1,32,32,512]{3,2,0,1:T(8,128)(2,1)} %broadcast_multiply_fusion), calls=%async_computation.2 | async-start | bytes 2097152 | tf_op jit(solution)/shard_map/all_to_all | solution.py:221
  62.8 0.1 maximum_select_fusion.1
  62.9 0.3 collective-permute-start.4
  63.2 1.6 %collective-permute-done.4 = bf16[16,32,512]{2,1,0:T(8,128)(2,1)S(1)} collective-permute-done((bf16[16,32,512]{2,1,0:T(8,128)(2,1)S(1)}, bf16[16,32,512]{2,1,0:T(8,128)(2,1)S(1)}, u32[]{:S(2)}, u32[]{:S(2)}) %collective-permute-start.4) | collective-permute-done | bytes 524320 | tf_op jit(solution)/shard_map/ppermute | solution.py:138
  64.9 0.2 maximum_select_fusion
  65.0 0.1 copy.82
  65.1 0.3 multiply_reduce_fusion
  66.1 0.1 copy.90
  66.2 0.1 sqrt.12
  66.3 0.3 copy.86
  66.6 0.3 fusion.4
  66.9 0.3 fusion
  67.2 0.2 copy.89
  67.4 0.5 fusion.3
  67.9 0.7 reshape.615
  68.5 20.5 %all-to-all-done.2 = bf16[1,32,32,512]{3,2,0,1:T(8,128)(2,1)S(1)} async-done(((bf16[1,32,32,512]{3,2,0,1:T(8,128)(2,1)}), bf16[1,32,32,512]{3,2,0,1:T(8,128)(2,1)S(1)}, u32[]{:S(2)}, u32[]{:S(2)}) %all-to-all-start.2) | async-done | bytes 1048608 | tf_op jit(solution)/shard_map/all_to_all | solution.py:221
  89.0 0.8 convert_reduce_fusion
  (29 shorter events, 0.4 us)
Async XLA Ops:
  0.6 31.0 %copy-start = (f32[1664]{0:T(1024)S(1)}, f32[1664]{0:T(1024)}, u32[]{:S(2)}) copy-start(f32[1664]{0:T(1024)} %constant.207.clone) | copy-start | bytes 19972
  0.6 31.0 %copy-start.1 = (f32[1664]{0:T(1024)S(1)}, f32[1664]{0:T(1024)}, u32[]{:S(2)}) copy-start(f32[1664]{0:T(1024)} %constant.208.clone) | copy-start | bytes 19972
  2.9 14.6 %all-to-all-start = ((s32[32,2,3]{2,1,0:T(2,128)}), s32[32,2,3]{2,1,0:T(2,128)S(1)}, u32[]{:S(2)}, u32[]{:S(2)}) async-start(s32[32,2,3]{2,1,0:T(2,128)} %copy.84), calls=%async_computation | async-start | bytes 65536 | tf_op jit(solution)/shard_map/all_to_all | solution.py:165
  11.3 20.4 %collective-permute-start = (bf16[1,32,512]{1,2,0:T(8,128)(2,1)S(1)}, bf16[1,32,512]{1,2,0:T(8,128)(2,1)S(1)}, u32[]{:S(2)}, u32[]{:S(2)}) collective-permute-start(bf16[1,32,512]{1,2,0:T(8,128)(2,1)S(1)} %bitcast.83), channel_id=1, source_target_pairs={{0,16},{1,17},{2,18},{3,19},{4,20},{5,21},{6,22},{7,23},{8,24},{9,... | collective-permute-start | bytes 98312 | tf_op jit(solution)/shard_map/ppermute | solution.py:138
  29.0 20.7 %all-to-all-start.1 = ((bf16[32,64,128]{2,1,0:T(8,128)(2,1)}), bf16[32,64,128]{2,1,0:T(8,128)(2,1)S(1)}, u32[]{:S(2)}, u32[]{:S(2)}) async-start(bf16[32,64,128]{2,1,0:T(8,128)(2,1)} %shard_map.86), calls=%async_computation.1 | async-start | bytes 1048576 | tf_op jit(solution)/shard_map/all_to_all | solution.py:171
  31.9 10.3 %collective-permute-start.1 = (bf16[2,32,512]{2,1,0:T(8,128)(2,1)S(1)}, bf16[2,32,512]{2,1,0:T(8,128)(2,1)S(1)}, u32[]{:S(2)}, u32[]{:S(2)}) collective-permute-start(bf16[2,32,512]{2,1,0:T(8,128)(2,1)S(1)} %maximum_select_fusion.4), channel_id=1, source_target_pairs={{0,8},{1,9},{2,10},{3,11},{4,12},{5,13},{6,14},{7,15},{8,0},{9,1},... | collective-permute-start | bytes 196616 | tf_op jit(solution)/shard_map/ppermute | solution.py:138
  42.2 6.0 %collective-permute-start.2 = (bf16[4,32,512]{2,1,0:T(8,128)(2,1)S(1)}, bf16[4,32,512]{2,1,0:T(8,128)(2,1)S(1)}, u32[]{:S(2)}, u32[]{:S(2)}) collective-permute-start(bf16[4,32,512]{2,1,0:T(8,128)(2,1)S(1)} %maximum_select_fusion.3), channel_id=1, source_target_pairs={{0,4},{1,5},{2,6},{3,7},{4,0},{5,1},{6,2},{7,3},{8,12},{9,13},{10,... | collective-permute-start | bytes 393224 | tf_op jit(solution)/shard_map/ppermute | solution.py:138
  48.2 14.6 %collective-permute-start.3 = (bf16[8,32,512]{2,1,0:T(8,128)(2,1)S(1)}, bf16[8,32,512]{2,1,0:T(8,128)(2,1)S(1)}, u32[]{:S(2)}, u32[]{:S(2)}) collective-permute-start(bf16[8,32,512]{2,1,0:T(8,128)(2,1)S(1)} %maximum_select_fusion.2), channel_id=1, source_target_pairs={{0,2},{1,3},{2,0},{3,1},{4,6},{5,7},{6,4},{7,5},{8,10},{9,11},{10,... | collective-permute-start | bytes 786440 | tf_op jit(solution)/shard_map/ppermute | solution.py:138
  57.7 31.3 %all-to-all-start.2 = ((bf16[1,32,32,512]{3,2,0,1:T(8,128)(2,1)}), bf16[1,32,32,512]{3,2,0,1:T(8,128)(2,1)S(1)}, u32[]{:S(2)}, u32[]{:S(2)}) async-start(bf16[1,32,32,512]{3,2,0,1:T(8,128)(2,1)} %broadcast_multiply_fusion), calls=%async_computation.2 | async-start | bytes 2097152 | tf_op jit(solution)/shard_map/all_to_all | solution.py:221
  62.9 2.0 %collective-permute-start.4 = (bf16[16,32,512]{2,1,0:T(8,128)(2,1)S(1)}, bf16[16,32,512]{2,1,0:T(8,128)(2,1)S(1)}, u32[]{:S(2)}, u32[]{:S(2)}) collective-permute-start(bf16[16,32,512]{2,1,0:T(8,128)(2,1)S(1)} %maximum_select_fusion.1), channel_id=1, source_target_pairs={{0,1},{1,0},{2,3},{3,2},{4,5},{5,4},{6,7},{7,6},{8,9},{9,8},{10,11... | collective-permute-start | bytes 1572872 | tf_op jit(solution)/shard_map/ppermute | solution.py:138

commit v10 on v9

--- a/solution.py
+++ b/solution.py
@@ -108,7 +108,7 @@
             out_ref[d, :, s * BOX : (s + 1) * BOX] = flip[:BOX, :BOX].astype(out_ref.dtype)
         return carry
 
-    lax.fori_loop(0, ends, body, 0)
+    lax.fori_loop(0, ends, body, 0, unroll=2)
 
 
 def cut_patches(tiles, req, ends, cap):

time: 90.3 us -> 87.2 us (0.966)
  Pallas kernels: 10.8 us -> 7.65 us
    pallas_call x1, Pallas kernels: 10.8 us -> 7.65 us  [cut_patches(): pl.pallas_call(functools.partial(cut_kernel, cap), out_shape=jax.ShapeDty...]
  transfers between devices with their start and end apart: 8 -> 8, of which waited for: 5 -> 5; matrix products, arithmetic and copies ran while one was open for 22% -> 23% of each run, Pallas kernels for 12% -> 9%
where the time goes in v10:
time: 87.2 us; the launch traced here: 86.7 us
  waiting for transfers between devices  30.2 us (35%)
  starting transfers between devices  23.1 us (26%)
  other arithmetic  9.63 us (11%)
  local copies, waits for them, and re-layouts  7.79 us (9%)
  Pallas kernels  7.65 us (9%)
  matrix products  5.21 us (6%)
  between operations  3.09 us (4%)
    all_to_all x1, waiting for transfers between devices, per_device(): lax.all_to_all(placed, 'dev', split_axis=1, concat_axis=0, tiled=True)  20.5 us
    ppermute x5, waiting for transfers between devices, double_gather(): lax.ppermute(block, 'dev', perm=[(i, i ^ step) for i in range(ndev)])  8.65 us
    ppermute x5, starting transfers between devices, double_gather(): lax.ppermute(block, 'dev', perm=[(i, i ^ step) for i in range(ndev)])  8.11 us
    pallas_call x1, Pallas kernels, cut_patches(): pl.pallas_call(functools.partial(cut_kernel, cap), out_shape=jax.ShapeDty...  7.65 us
    all_to_all x1, starting transfers between devices, per_device(): lax.all_to_all(wanted, 'dev', split_axis=0, concat_axis=0, tiled=True)  7.3 us
    all_to_all x1, starting transfers between devices, per_device(): lax.all_to_all(placed, 'dev', split_axis=1, concat_axis=0, tiled=True)  5.03 us
    convert_element_type x1, other arithmetic, back_points(): return weight.reshape(count * BOX, xs.shape[0]).astype(jnp.bfloat16)  4.48 us
    dot_general x1, matrix products, per_device(): cyl = jnp.dot(volume, sample, preferred_element_type=jnp.float32)  4.17 us
  transfers between devices with their start and end apart: 8, of which 5 were waited for; matrix products, arithmetic and copies ran while one was open for 23% of the time, Pallas kernels for 9%

profile of v10, /device:TPU:0, one launch (start us, length us, event | category | flops | bytes accessed | tf_op | source)
XLA Modules:
  0.0 86.7 jit_solution(9381759907788095156)
XLA Ops:
  0.6 0.0 copy-start
  0.6 0.0 copy-start.1
  0.7 0.7 copy.97
  1.4 0.1 fusion.12
  1.5 0.2 select_reduce_fusion.1
  1.7 0.1 iota_compare_fusion.2
  1.8 0.1 iota_compare_fusion.3
  1.9 0.1 copy.83
  2.0 0.1 broadcast_and_fusion
  2.1 0.1 select_reduce_fusion
  2.2 0.7 copy.84
  2.9 7.3 %all-to-all-start = ((s32[32,2,3]{2,1,0:T(2,128)}), s32[32,2,3]{2,1,0:T(2,128)S(1)}, u32[]{:S(2)}, u32[]{:S(2)}) async-start(s32[32,2,3]{2,1,0:T(2,128)} %copy.84), calls=%async_computation | async-start | bytes 65536 | tf_op jit(solution)/shard_map/all_to_all | solution.py:165
  10.2 0.9 %copy.76 = bf16[32,512]{0,1:T(8,128)(2,1)S(1)} copy(bf16[32,512]{1,0:T(8,128)(2,1)} %param.11) | data formatting | bytes 65536 | tf_op args[4]
  11.1 0.2 copy.77
  11.3 2.7 %collective-permute-start = (bf16[1,32,512]{1,2,0:T(8,128)(2,1)S(1)}, bf16[1,32,512]{1,2,0:T(8,128)(2,1)S(1)}, u32[]{:S(2)}, u32[]{:S(2)}) collective-permute-start(bf16[1,32,512]{1,2,0:T(8,128)(2,1)S(1)} %bitcast.83), channel_id=1, source_target_pairs={{0,16},{1,17},{2,18},{3,19},{4,20},{5,21},{6,22},{7,23},{8,24},{9,... | collective-permute-start | bytes 98312 | tf_op jit(solution)/shard_map/ppermute | solution.py:138
  15.0 0.1 mul.200
  15.1 0.1 mul.203
  15.1 0.1 mul.204
  15.2 0.1 mul.206
  15.3 0.1 mul.207
  16.1 0.1 copy.78
  16.2 0.1 mul.214
  16.3 0.1 mul.215
  16.4 1.1 %all-to-all-done = s32[32,2,3]{2,1,0:T(2,128)S(1)} async-done(((s32[32,2,3]{2,1,0:T(2,128)}), s32[32,2,3]{2,1,0:T(2,128)S(1)}, u32[]{:S(2)}, u32[]{:S(2)}) %all-to-all-start) | async-done | bytes 800 | tf_op jit(solution)/shard_map/all_to_all | solution.py:165
  17.5 0.7 reshape_reshape.10.req_ref
  18.2 7.6 %shard_map.86 = bf16[32,64,128]{2,1,0:T(8,128)(2,1)} custom-call(s32[192]{0:T(256)} %reshape_reshape.10.req_ref, bf16[2,128,4096]{2,1,0:T(8,128)(2,1)} %tiles_ref.1), custom_call_target="tpu_custom_call" | custom-call | flops 67108864 | bytes 2621440 | tf_op jit(solution)/shard_map/pallas_call | solution.py:116
  25.9 2.6 %all-to-all-start.1 = ((bf16[32,64,128]{2,1,0:T(8,128)(2,1)}), bf16[32,64,128]{2,1,0:T(8,128)(2,1)S(1)}, u32[]{:S(2)}, u32[]{:S(2)}) async-start(bf16[32,64,128]{2,1,0:T(8,128)(2,1)} %shard_map.86), calls=%async_computation.1 | async-start | bytes 1048576 | tf_op jit(solution)/shard_map/all_to_all | solution.py:171
  28.5 0.1 add_add_fusion
  28.6 0.0 collective-permute-done
  28.6 0.1 copy.79
  28.8 1.8 %collective-permute-start.1 = (bf16[2,32,512]{2,1,0:T(8,128)(2,1)S(1)}, bf16[2,32,512]{2,1,0:T(8,128)(2,1)S(1)}, u32[]{:S(2)}, u32[]{:S(2)}) collective-permute-start(bf16[2,32,512]{2,1,0:T(8,128)(2,1)S(1)} %maximum_select_fusion.4), channel_id=1, source_target_pairs={{0,8},{1,9},{2,10},{3,11},{4,12},{5,13},{6,14},{7,15},{8,0},{9,1},... | collective-permute-start | bytes 196616 | tf_op jit(solution)/shard_map/ppermute | solution.py:138
  30.6 4.5 %multiply_convert_fusion = bf16[22,64,1664]{2,1,0:T(8,128)(2,1)} fusion(f32[22,1664]{1,0:T(8,128)S(1)} %add_add_fusion, pred[22]{0:T(512)(128)(4,1)S(1)} %iota_compare_fusion.5), kind=kLoop, calls=%fused_computation.2 | loop fusion | flops 16400384 | bytes 4832278 | tf_op jit(solution)/shard_map/convert_element_type | solution.py:72
  35.1 4.0 %collective-permute-done.1 = bf16[2,32,512]{2,1,0:T(8,128)(2,1)S(1)} collective-permute-done((bf16[2,32,512]{2,1,0:T(8,128)(2,1)S(1)}, bf16[2,32,512]{2,1,0:T(8,128)(2,1)S(1)}, u32[]{:S(2)}, u32[]{:S(2)}) %collective-permute-start.1) | collective-permute-done | bytes 65568 | tf_op jit(solution)/shard_map/ppermute | solution.py:138
  39.1 1.7 %collective-permute-start.2 = (bf16[4,32,512]{2,1,0:T(8,128)(2,1)S(1)}, bf16[4,32,512]{2,1,0:T(8,128)(2,1)S(1)}, u32[]{:S(2)}, u32[]{:S(2)}) collective-permute-start(bf16[4,32,512]{2,1,0:T(8,128)(2,1)S(1)} %maximum_select_fusion.3), channel_id=1, source_target_pairs={{0,4},{1,5},{2,6},{3,7},{4,0},{5,1},{6,2},{7,3},{8,12},{9,13},{10,... | collective-permute-start | bytes 393224 | tf_op jit(solution)/shard_map/ppermute | solution.py:138
  40.8 1.2 %multiply_convert_fusion.1 = bf16[1664,512]{1,0:T(8,128)(2,1)S(1)} fusion(f32[512]{0:T(512)S(1)} %get-tuple-element.11, f32[1664]{0:T(1024)S(1)} %get-tuple-element.16, f32[512]{0:T(512)S(1)} %get-tuple-element.10, f32[1664]{0:T(1024)S(1)} %get-tuple-element.17), kind=kLoop, calls=%fused_computation.3 | loop fusion | flops 8519680 | bytes 1721344 | tf_op jit(solution)/shard_map/convert_element_type | solution.py:81
  42.1 3.0 %collective-permute-done.2 = bf16[4,32,512]{2,1,0:T(8,128)(2,1)S(1)} collective-permute-done((bf16[4,32,512]{2,1,0:T(8,128)(2,1)S(1)}, bf16[4,32,512]{2,1,0:T(8,128)(2,1)S(1)}, u32[]{:S(2)}, u32[]{:S(2)}) %collective-permute-start.2) | collective-permute-done | bytes 131104 | tf_op jit(solution)/shard_map/ppermute | solution.py:138
  45.1 1.5 %collective-permute-start.3 = (bf16[8,32,512]{2,1,0:T(8,128)(2,1)S(1)}, bf16[8,32,512]{2,1,0:T(8,128)(2,1)S(1)}, u32[]{:S(2)}, u32[]{:S(2)}) collective-permute-start(bf16[8,32,512]{2,1,0:T(8,128)(2,1)S(1)} %maximum_select_fusion.2), channel_id=1, source_target_pairs={{0,2},{1,3},{2,0},{3,1},{4,6},{5,7},{6,4},{7,5},{8,10},{9,11},{10,... | collective-permute-start | bytes 786440 | tf_op jit(solution)/shard_map/ppermute | solution.py:138
  46.6 0.6 gather_fusion
  47.2 0.2 fusion.6
  47.4 0.1 pad.4
  47.5 4.2 %multiply_reduce_fusion.1 = (f32[]{:T(128)}, bf16[64,512]{1,0:T(8,128)(2,1)S(1)}) fusion(bf16[1664,512]{1,0:T(8,128)(2,1)S(1)} %multiply_convert_fusion.1, bf16[1408,64]{1,0:T(8,128)(2,1)S(1)} %bitcast.80, bf16[1408,1664]{1,0:T(8,128)(2,1)} %bitcast.73), kind=kOutput, calls=%fused_computation.31 | convolution fusion | flops 409182208 | bytes 6635524 | tf_op jit(solution)/shard_map/dot_general | solution.py:185
  51.7 0.1 copy.85
  51.8 1.3 %gather_fusion.1 = bf16[512,64]{1,0:T(8,128)(2,1)S(1)} fusion(bf16[64,512]{0,1:T(8,128)(2,1)S(1)} %copy.85, s32[1024]{0:T(1024)S(1)} %pad_clamp_fusion), kind=kCustom, calls=%fused_computation.1 | custom fusion | bytes 133120 | tf_op jit(solution)/shard_map/jit(take_along_axis)/gather | solution.py:215
  53.1 0.1 select_bitcast_fusion
  53.3 0.1 copy.92
  53.4 0.1 mul.218
  53.5 1.1 %broadcast_multiply_fusion = bf16[1,32,32,512]{3,2,0,1:T(8,128)(2,1)} fusion(bf16[1,32,32,512]{3,2,0,1:T(8,128)(2,1)S(1)} %bitcast.77, bf16[32]{0:T(256)(128)(2,1)S(1)} %mul.215), kind=kLoop, calls=%fused_computation.18 | loop fusion | flops 524288 | bytes 2097216 | tf_op jit(solution)/shard_map/mul | solution.py:219
  54.6 5.0 %all-to-all-start.2 = ((bf16[1,32,32,512]{3,2,0,1:T(8,128)(2,1)}), bf16[1,32,32,512]{3,2,0,1:T(8,128)(2,1)S(1)}, u32[]{:S(2)}, u32[]{:S(2)}) async-start(bf16[1,32,32,512]{3,2,0,1:T(8,128)(2,1)} %broadcast_multiply_fusion), calls=%async_computation.2 | async-start | bytes 2097152 | tf_op jit(solution)/shard_map/all_to_all | solution.py:221
  59.7 0.1 maximum_select_fusion.1
  59.8 0.3 collective-permute-start.4
  60.1 1.6 %collective-permute-done.4 = bf16[16,32,512]{2,1,0:T(8,128)(2,1)S(1)} collective-permute-done((bf16[16,32,512]{2,1,0:T(8,128)(2,1)S(1)}, bf16[16,32,512]{2,1,0:T(8,128)(2,1)S(1)}, u32[]{:S(2)}, u32[]{:S(2)}) %collective-permute-start.4) | collective-permute-done | bytes 524320 | tf_op jit(solution)/shard_map/ppermute | solution.py:138
  61.8 0.2 maximum_select_fusion
  61.9 0.1 copy.82
  62.0 0.3 multiply_reduce_fusion
  63.0 0.1 copy.90
  63.1 0.1 sqrt.12
  63.2 0.3 copy.86
  63.5 0.3 fusion.4
  63.8 0.3 fusion
  64.1 0.2 copy.89
  64.3 0.5 fusion.3
  64.7 0.7 reshape.615
  65.4 20.5 %all-to-all-done.2 = bf16[1,32,32,512]{3,2,0,1:T(8,128)(2,1)S(1)} async-done(((bf16[1,32,32,512]{3,2,0,1:T(8,128)(2,1)}), bf16[1,32,32,512]{3,2,0,1:T(8,128)(2,1)S(1)}, u32[]{:S(2)}, u32[]{:S(2)}) %all-to-all-start.2) | async-done | bytes 1048608 | tf_op jit(solution)/shard_map/all_to_all | solution.py:221
  85.9 0.8 convert_reduce_fusion
  (29 shorter events, 0.4 us)
Async XLA Ops:
  0.6 27.9 %copy-start = (f32[1664]{0:T(1024)S(1)}, f32[1664]{0:T(1024)}, u32[]{:S(2)}) copy-start(f32[1664]{0:T(1024)} %constant.207.clone) | copy-start | bytes 19972
  0.6 27.9 %copy-start.1 = (f32[1664]{0:T(1024)S(1)}, f32[1664]{0:T(1024)}, u32[]{:S(2)}) copy-start(f32[1664]{0:T(1024)} %constant.208.clone) | copy-start | bytes 19972
  2.9 14.6 %all-to-all-start = ((s32[32,2,3]{2,1,0:T(2,128)}), s32[32,2,3]{2,1,0:T(2,128)S(1)}, u32[]{:S(2)}, u32[]{:S(2)}) async-start(s32[32,2,3]{2,1,0:T(2,128)} %copy.84), calls=%async_computation | async-start | bytes 65536 | tf_op jit(solution)/shard_map/all_to_all | solution.py:165
  11.3 17.3 %collective-permute-start = (bf16[1,32,512]{1,2,0:T(8,128)(2,1)S(1)}, bf16[1,32,512]{1,2,0:T(8,128)(2,1)S(1)}, u32[]{:S(2)}, u32[]{:S(2)}) collective-permute-start(bf16[1,32,512]{1,2,0:T(8,128)(2,1)S(1)} %bitcast.83), channel_id=1, source_target_pairs={{0,16},{1,17},{2,18},{3,19},{4,20},{5,21},{6,22},{7,23},{8,24},{9,... | collective-permute-start | bytes 98312 | tf_op jit(solution)/shard_map/ppermute | solution.py:138
  25.9 20.7 %all-to-all-start.1 = ((bf16[32,64,128]{2,1,0:T(8,128)(2,1)}), bf16[32,64,128]{2,1,0:T(8,128)(2,1)S(1)}, u32[]{:S(2)}, u32[]{:S(2)}) async-start(bf16[32,64,128]{2,1,0:T(8,128)(2,1)} %shard_map.86), calls=%async_computation.1 | async-start | bytes 1048576 | tf_op jit(solution)/shard_map/all_to_all | solution.py:171
  28.8 10.3 %collective-permute-start.1 = (bf16[2,32,512]{2,1,0:T(8,128)(2,1)S(1)}, bf16[2,32,512]{2,1,0:T(8,128)(2,1)S(1)}, u32[]{:S(2)}, u32[]{:S(2)}) collective-permute-start(bf16[2,32,512]{2,1,0:T(8,128)(2,1)S(1)} %maximum_select_fusion.4), channel_id=1, source_target_pairs={{0,8},{1,9},{2,10},{3,11},{4,12},{5,13},{6,14},{7,15},{8,0},{9,1},... | collective-permute-start | bytes 196616 | tf_op jit(solution)/shard_map/ppermute | solution.py:138
  39.1 6.0 %collective-permute-start.2 = (bf16[4,32,512]{2,1,0:T(8,128)(2,1)S(1)}, bf16[4,32,512]{2,1,0:T(8,128)(2,1)S(1)}, u32[]{:S(2)}, u32[]{:S(2)}) collective-permute-start(bf16[4,32,512]{2,1,0:T(8,128)(2,1)S(1)} %maximum_select_fusion.3), channel_id=1, source_target_pairs={{0,4},{1,5},{2,6},{3,7},{4,0},{5,1},{6,2},{7,3},{8,12},{9,13},{10,... | collective-permute-start | bytes 393224 | tf_op jit(solution)/shard_map/ppermute | solution.py:138
  45.1 14.6 %collective-permute-start.3 = (bf16[8,32,512]{2,1,0:T(8,128)(2,1)S(1)}, bf16[8,32,512]{2,1,0:T(8,128)(2,1)S(1)}, u32[]{:S(2)}, u32[]{:S(2)}) collective-permute-start(bf16[8,32,512]{2,1,0:T(8,128)(2,1)S(1)} %maximum_select_fusion.2), channel_id=1, source_target_pairs={{0,2},{1,3},{2,0},{3,1},{4,6},{5,7},{6,4},{7,5},{8,10},{9,11},{10,... | collective-permute-start | bytes 786440 | tf_op jit(solution)/shard_map/ppermute | solution.py:138
  54.6 31.3 %all-to-all-start.2 = ((bf16[1,32,32,512]{3,2,0,1:T(8,128)(2,1)}), bf16[1,32,32,512]{3,2,0,1:T(8,128)(2,1)S(1)}, u32[]{:S(2)}, u32[]{:S(2)}) async-start(bf16[1,32,32,512]{3,2,0,1:T(8,128)(2,1)} %broadcast_multiply_fusion), calls=%async_computation.2 | async-start | bytes 2097152 | tf_op jit(solution)/shard_map/all_to_all | solution.py:221
  59.8 2.0 %collective-permute-start.4 = (bf16[16,32,512]{2,1,0:T(8,128)(2,1)S(1)}, bf16[16,32,512]{2,1,0:T(8,128)(2,1)S(1)}, u32[]{:S(2)}, u32[]{:S(2)}) collective-permute-start(bf16[16,32,512]{2,1,0:T(8,128)(2,1)S(1)} %maximum_select_fusion.1), channel_id=1, source_target_pairs={{0,1},{1,0},{2,3},{3,2},{4,5},{5,4},{6,7},{7,6},{8,9},{9,8},{10,11... | collective-permute-start | bytes 1572872 | tf_op jit(solution)/shard_map/ppermute | solution.py:138

commit v11 on v10

--- a/solution.py
+++ b/solution.py
@@ -108,7 +108,7 @@
             out_ref[d, :, s * BOX : (s + 1) * BOX] = flip[:BOX, :BOX].astype(out_ref.dtype)
         return carry
 
-    lax.fori_loop(0, ends, body, 0, unroll=2)
+    lax.fori_loop(0, ends, body, 0, unroll=4)
 
 
 def cut_patches(tiles, req, ends, cap):

time: 87.2 us -> 88.1 us (1.010)
  transfers between devices with their start and end apart: 8 -> 8, of which waited for: 5 -> 5; matrix products, arithmetic and copies ran while one was open for 23% -> 22% of each run, Pallas kernels for 9% -> 10%
where the time goes in v11:
time: 88.1 us; the launch traced here: 87.5 us
  waiting for transfers between devices  30.2 us (34%)
  starting transfers between devices  23.1 us (26%)
  other arithmetic  9.63 us (11%)
  Pallas kernels  8.51 us (10%)
  local copies, waits for them, and re-layouts  7.79 us (9%)
  matrix products  5.21 us (6%)
  between operations  3.09 us (4%)
    all_to_all x1, waiting for transfers between devices, per_device(): lax.all_to_all(placed, 'dev', split_axis=1, concat_axis=0, tiled=True)  20.5 us
    ppermute x5, waiting for transfers between devices, double_gather(): lax.ppermute(block, 'dev', perm=[(i, i ^ step) for i in range(ndev)])  8.65 us
    pallas_call x1, Pallas kernels, cut_patches(): pl.pallas_call(functools.partial(cut_kernel, cap), out_shape=jax.ShapeDty...  8.51 us
    ppermute x5, starting transfers between devices, double_gather(): lax.ppermute(block, 'dev', perm=[(i, i ^ step) for i in range(ndev)])  8.11 us
    all_to_all x1, starting transfers between devices, per_device(): lax.all_to_all(wanted, 'dev', split_axis=0, concat_axis=0, tiled=True)  7.3 us
    all_to_all x1, starting transfers between devices, per_device(): lax.all_to_all(placed, 'dev', split_axis=1, concat_axis=0, tiled=True)  5.03 us
    convert_element_type x1, other arithmetic, back_points(): return weight.reshape(count * BOX, xs.shape[0]).astype(jnp.bfloat16)  4.48 us
    dot_general x1, matrix products, per_device(): cyl = jnp.dot(volume, sample, preferred_element_type=jnp.float32)  4.17 us
  transfers between devices with their start and end apart: 8, of which 5 were waited for; matrix products, arithmetic and copies ran while one was open for 22% of the time, Pallas kernels for 10%

profile of v11, /device:TPU:0, one launch (start us, length us, event | category | flops | bytes accessed | tf_op | source)
XLA Modules:
  0.0 87.5 jit_solution(13351135722463413740)
XLA Ops:
  0.6 0.0 copy-start
  0.6 0.0 copy-start.1
  0.7 0.7 copy.97
  1.4 0.1 fusion.12
  1.5 0.2 select_reduce_fusion.1
  1.7 0.1 iota_compare_fusion.2
  1.8 0.1 iota_compare_fusion.3
  1.9 0.1 copy.83
  2.0 0.1 broadcast_and_fusion
  2.1 0.1 select_reduce_fusion
  2.2 0.7 copy.84
  2.9 7.3 %all-to-all-start = ((s32[32,2,3]{2,1,0:T(2,128)}), s32[32,2,3]{2,1,0:T(2,128)S(1)}, u32[]{:S(2)}, u32[]{:S(2)}) async-start(s32[32,2,3]{2,1,0:T(2,128)} %copy.84), calls=%async_computation | async-start | bytes 65536 | tf_op jit(solution)/shard_map/all_to_all | solution.py:165
  10.2 0.9 %copy.76 = bf16[32,512]{0,1:T(8,128)(2,1)S(1)} copy(bf16[32,512]{1,0:T(8,128)(2,1)} %param.11) | data formatting | bytes 65536 | tf_op args[4]
  11.1 0.2 copy.77
  11.3 2.7 %collective-permute-start = (bf16[1,32,512]{1,2,0:T(8,128)(2,1)S(1)}, bf16[1,32,512]{1,2,0:T(8,128)(2,1)S(1)}, u32[]{:S(2)}, u32[]{:S(2)}) collective-permute-start(bf16[1,32,512]{1,2,0:T(8,128)(2,1)S(1)} %bitcast.83), channel_id=1, source_target_pairs={{0,16},{1,17},{2,18},{3,19},{4,20},{5,21},{6,22},{7,23},{8,24},{9,... | collective-permute-start | bytes 98312 | tf_op jit(solution)/shard_map/ppermute | solution.py:138
  15.0 0.1 mul.200
  15.1 0.1 mul.203
  15.1 0.1 mul.204
  15.2 0.1 mul.206
  15.3 0.1 mul.207
  16.1 0.1 copy.78
  16.2 0.1 mul.214
  16.3 0.1 mul.215
  16.4 1.1 %all-to-all-done = s32[32,2,3]{2,1,0:T(2,128)S(1)} async-done(((s32[32,2,3]{2,1,0:T(2,128)}), s32[32,2,3]{2,1,0:T(2,128)S(1)}, u32[]{:S(2)}, u32[]{:S(2)}) %all-to-all-start) | async-done | bytes 800 | tf_op jit(solution)/shard_map/all_to_all | solution.py:165
  17.5 0.7 reshape_reshape.10.req_ref
  18.2 8.5 %shard_map.86 = bf16[32,64,128]{2,1,0:T(8,128)(2,1)} custom-call(s32[192]{0:T(256)} %reshape_reshape.10.req_ref, bf16[2,128,4096]{2,1,0:T(8,128)(2,1)} %tiles_ref.1), custom_call_target="tpu_custom_call" | custom-call | flops 67108864 | bytes 2621440 | tf_op jit(solution)/shard_map/pallas_call | solution.py:116
  26.7 2.6 %all-to-all-start.1 = ((bf16[32,64,128]{2,1,0:T(8,128)(2,1)}), bf16[32,64,128]{2,1,0:T(8,128)(2,1)S(1)}, u32[]{:S(2)}, u32[]{:S(2)}) async-start(bf16[32,64,128]{2,1,0:T(8,128)(2,1)} %shard_map.86), calls=%async_computation.1 | async-start | bytes 1048576 | tf_op jit(solution)/shard_map/all_to_all | solution.py:171
  29.4 0.1 add_add_fusion
  29.5 0.0 collective-permute-done
  29.5 0.1 copy.79
  29.6 1.8 %collective-permute-start.1 = (bf16[2,32,512]{2,1,0:T(8,128)(2,1)S(1)}, bf16[2,32,512]{2,1,0:T(8,128)(2,1)S(1)}, u32[]{:S(2)}, u32[]{:S(2)}) collective-permute-start(bf16[2,32,512]{2,1,0:T(8,128)(2,1)S(1)} %maximum_select_fusion.4), channel_id=1, source_target_pairs={{0,8},{1,9},{2,10},{3,11},{4,12},{5,13},{6,14},{7,15},{8,0},{9,1},... | collective-permute-start | bytes 196616 | tf_op jit(solution)/shard_map/ppermute | solution.py:138
  31.4 4.5 %multiply_convert_fusion = bf16[22,64,1664]{2,1,0:T(8,128)(2,1)} fusion(f32[22,1664]{1,0:T(8,128)S(1)} %add_add_fusion, pred[22]{0:T(512)(128)(4,1)S(1)} %iota_compare_fusion.5), kind=kLoop, calls=%fused_computation.2 | loop fusion | flops 16400384 | bytes 4832278 | tf_op jit(solution)/shard_map/convert_element_type | solution.py:72
  35.9 4.0 %collective-permute-done.1 = bf16[2,32,512]{2,1,0:T(8,128)(2,1)S(1)} collective-permute-done((bf16[2,32,512]{2,1,0:T(8,128)(2,1)S(1)}, bf16[2,32,512]{2,1,0:T(8,128)(2,1)S(1)}, u32[]{:S(2)}, u32[]{:S(2)}) %collective-permute-start.1) | collective-permute-done | bytes 65568 | tf_op jit(solution)/shard_map/ppermute | solution.py:138
  39.9 1.7 %collective-permute-start.2 = (bf16[4,32,512]{2,1,0:T(8,128)(2,1)S(1)}, bf16[4,32,512]{2,1,0:T(8,128)(2,1)S(1)}, u32[]{:S(2)}, u32[]{:S(2)}) collective-permute-start(bf16[4,32,512]{2,1,0:T(8,128)(2,1)S(1)} %maximum_select_fusion.3), channel_id=1, source_target_pairs={{0,4},{1,5},{2,6},{3,7},{4,0},{5,1},{6,2},{7,3},{8,12},{9,13},{10,... | collective-permute-start | bytes 393224 | tf_op jit(solution)/shard_map/ppermute | solution.py:138
  41.7 1.2 %multiply_convert_fusion.1 = bf16[1664,512]{1,0:T(8,128)(2,1)S(1)} fusion(f32[512]{0:T(512)S(1)} %get-tuple-element.11, f32[1664]{0:T(1024)S(1)} %get-tuple-element.16, f32[512]{0:T(512)S(1)} %get-tuple-element.10, f32[1664]{0:T(1024)S(1)} %get-tuple-element.17), kind=kLoop, calls=%fused_computation.3 | loop fusion | flops 8519680 | bytes 1721344 | tf_op jit(solution)/shard_map/convert_element_type | solution.py:81
  42.9 3.0 %collective-permute-done.2 = bf16[4,32,512]{2,1,0:T(8,128)(2,1)S(1)} collective-permute-done((bf16[4,32,512]{2,1,0:T(8,128)(2,1)S(1)}, bf16[4,32,512]{2,1,0:T(8,128)(2,1)S(1)}, u32[]{:S(2)}, u32[]{:S(2)}) %collective-permute-start.2) | collective-permute-done | bytes 131104 | tf_op jit(solution)/shard_map/ppermute | solution.py:138
  45.9 1.5 %collective-permute-start.3 = (bf16[8,32,512]{2,1,0:T(8,128)(2,1)S(1)}, bf16[8,32,512]{2,1,0:T(8,128)(2,1)S(1)}, u32[]{:S(2)}, u32[]{:S(2)}) collective-permute-start(bf16[8,32,512]{2,1,0:T(8,128)(2,1)S(1)} %maximum_select_fusion.2), channel_id=1, source_target_pairs={{0,2},{1,3},{2,0},{3,1},{4,6},{5,7},{6,4},{7,5},{8,10},{9,11},{10,... | collective-permute-start | bytes 786440 | tf_op jit(solution)/shard_map/ppermute | solution.py:138
  47.4 0.6 gather_fusion
  48.1 0.2 fusion.6
  48.3 0.1 pad.4
  48.4 4.2 %multiply_reduce_fusion.1 = (f32[]{:T(128)}, bf16[64,512]{1,0:T(8,128)(2,1)S(1)}) fusion(bf16[1664,512]{1,0:T(8,128)(2,1)S(1)} %multiply_convert_fusion.1, bf16[1408,64]{1,0:T(8,128)(2,1)S(1)} %bitcast.80, bf16[1408,1664]{1,0:T(8,128)(2,1)} %bitcast.73), kind=kOutput, calls=%fused_computation.31 | convolution fusion | flops 409182208 | bytes 6635524 | tf_op jit(solution)/shard_map/dot_general | solution.py:185
  52.5 0.1 copy.85
  52.6 1.3 %gather_fusion.1 = bf16[512,64]{1,0:T(8,128)(2,1)S(1)} fusion(bf16[64,512]{0,1:T(8,128)(2,1)S(1)} %copy.85, s32[1024]{0:T(1024)S(1)} %pad_clamp_fusion), kind=kCustom, calls=%fused_computation.1 | custom fusion | bytes 133120 | tf_op jit(solution)/shard_map/jit(take_along_axis)/gather | solution.py:215
  54.0 0.1 select_bitcast_fusion
  54.1 0.1 copy.92
  54.2 0.1 mul.218
  54.3 1.1 %broadcast_multiply_fusion = bf16[1,32,32,512]{3,2,0,1:T(8,128)(2,1)} fusion(bf16[1,32,32,512]{3,2,0,1:T(8,128)(2,1)S(1)} %bitcast.77, bf16[32]{0:T(256)(128)(2,1)S(1)} %mul.215), kind=kLoop, calls=%fused_computation.18 | loop fusion | flops 524288 | bytes 2097216 | tf_op jit(solution)/shard_map/mul | solution.py:219
  55.5 5.0 %all-to-all-start.2 = ((bf16[1,32,32,512]{3,2,0,1:T(8,128)(2,1)}), bf16[1,32,32,512]{3,2,0,1:T(8,128)(2,1)S(1)}, u32[]{:S(2)}, u32[]{:S(2)}) async-start(bf16[1,32,32,512]{3,2,0,1:T(8,128)(2,1)} %broadcast_multiply_fusion), calls=%async_computation.2 | async-start | bytes 2097152 | tf_op jit(solution)/shard_map/all_to_all | solution.py:221
  60.5 0.1 maximum_select_fusion.1
  60.6 0.3 collective-permute-start.4
  61.0 1.6 %collective-permute-done.4 = bf16[16,32,512]{2,1,0:T(8,128)(2,1)S(1)} collective-permute-done((bf16[16,32,512]{2,1,0:T(8,128)(2,1)S(1)}, bf16[16,32,512]{2,1,0:T(8,128)(2,1)S(1)}, u32[]{:S(2)}, u32[]{:S(2)}) %collective-permute-start.4) | collective-permute-done | bytes 524320 | tf_op jit(solution)/shard_map/ppermute | solution.py:138
  62.6 0.2 maximum_select_fusion
  62.8 0.1 copy.82
  62.9 0.3 multiply_reduce_fusion
  63.9 0.1 copy.90
  64.0 0.1 sqrt.12
  64.1 0.3 copy.86
  64.4 0.3 fusion.4
  64.7 0.3 fusion
  65.0 0.2 copy.89
  65.1 0.5 fusion.3
  65.6 0.7 reshape.615
  66.3 20.5 %all-to-all-done.2 = bf16[1,32,32,512]{3,2,0,1:T(8,128)(2,1)S(1)} async-done(((bf16[1,32,32,512]{3,2,0,1:T(8,128)(2,1)}), bf16[1,32,32,512]{3,2,0,1:T(8,128)(2,1)S(1)}, u32[]{:S(2)}, u32[]{:S(2)}) %all-to-all-start.2) | async-done | bytes 1048608 | tf_op jit(solution)/shard_map/all_to_all | solution.py:221
  86.7 0.8 convert_reduce_fusion
  (29 shorter events, 0.4 us)
Async XLA Ops:
  0.6 28.7 %copy-start = (f32[1664]{0:T(1024)S(1)}, f32[1664]{0:T(1024)}, u32[]{:S(2)}) copy-start(f32[1664]{0:T(1024)} %constant.207.clone) | copy-start | bytes 19972
  0.6 28.7 %copy-start.1 = (f32[1664]{0:T(1024)S(1)}, f32[1664]{0:T(1024)}, u32[]{:S(2)}) copy-start(f32[1664]{0:T(1024)} %constant.208.clone) | copy-start | bytes 19972
  2.9 14.6 %all-to-all-start = ((s32[32,2,3]{2,1,0:T(2,128)}), s32[32,2,3]{2,1,0:T(2,128)S(1)}, u32[]{:S(2)}, u32[]{:S(2)}) async-start(s32[32,2,3]{2,1,0:T(2,128)} %copy.84), calls=%async_computation | async-start | bytes 65536 | tf_op jit(solution)/shard_map/all_to_all | solution.py:165
  11.3 18.2 %collective-permute-start = (bf16[1,32,512]{1,2,0:T(8,128)(2,1)S(1)}, bf16[1,32,512]{1,2,0:T(8,128)(2,1)S(1)}, u32[]{:S(2)}, u32[]{:S(2)}) collective-permute-start(bf16[1,32,512]{1,2,0:T(8,128)(2,1)S(1)} %bitcast.83), channel_id=1, source_target_pairs={{0,16},{1,17},{2,18},{3,19},{4,20},{5,21},{6,22},{7,23},{8,24},{9,... | collective-permute-start | bytes 98312 | tf_op jit(solution)/shard_map/ppermute | solution.py:138
  26.7 20.7 %all-to-all-start.1 = ((bf16[32,64,128]{2,1,0:T(8,128)(2,1)}), bf16[32,64,128]{2,1,0:T(8,128)(2,1)S(1)}, u32[]{:S(2)}, u32[]{:S(2)}) async-start(bf16[32,64,128]{2,1,0:T(8,128)(2,1)} %shard_map.86), calls=%async_computation.1 | async-start | bytes 1048576 | tf_op jit(solution)/shard_map/all_to_all | solution.py:171
  29.6 10.3 %collective-permute-start.1 = (bf16[2,32,512]{2,1,0:T(8,128)(2,1)S(1)}, bf16[2,32,512]{2,1,0:T(8,128)(2,1)S(1)}, u32[]{:S(2)}, u32[]{:S(2)}) collective-permute-start(bf16[2,32,512]{2,1,0:T(8,128)(2,1)S(1)} %maximum_select_fusion.4), channel_id=1, source_target_pairs={{0,8},{1,9},{2,10},{3,11},{4,12},{5,13},{6,14},{7,15},{8,0},{9,1},... | collective-permute-start | bytes 196616 | tf_op jit(solution)/shard_map/ppermute | solution.py:138
  39.9 6.0 %collective-permute-start.2 = (bf16[4,32,512]{2,1,0:T(8,128)(2,1)S(1)}, bf16[4,32,512]{2,1,0:T(8,128)(2,1)S(1)}, u32[]{:S(2)}, u32[]{:S(2)}) collective-permute-start(bf16[4,32,512]{2,1,0:T(8,128)(2,1)S(1)} %maximum_select_fusion.3), channel_id=1, source_target_pairs={{0,4},{1,5},{2,6},{3,7},{4,0},{5,1},{6,2},{7,3},{8,12},{9,13},{10,... | collective-permute-start | bytes 393224 | tf_op jit(solution)/shard_map/ppermute | solution.py:138
  45.9 14.6 %collective-permute-start.3 = (bf16[8,32,512]{2,1,0:T(8,128)(2,1)S(1)}, bf16[8,32,512]{2,1,0:T(8,128)(2,1)S(1)}, u32[]{:S(2)}, u32[]{:S(2)}) collective-permute-start(bf16[8,32,512]{2,1,0:T(8,128)(2,1)S(1)} %maximum_select_fusion.2), channel_id=1, source_target_pairs={{0,2},{1,3},{2,0},{3,1},{4,6},{5,7},{6,4},{7,5},{8,10},{9,11},{10,... | collective-permute-start | bytes 786440 | tf_op jit(solution)/shard_map/ppermute | solution.py:138
  55.5 31.3 %all-to-all-start.2 = ((bf16[1,32,32,512]{3,2,0,1:T(8,128)(2,1)}), bf16[1,32,32,512]{3,2,0,1:T(8,128)(2,1)S(1)}, u32[]{:S(2)}, u32[]{:S(2)}) async-start(bf16[1,32,32,512]{3,2,0,1:T(8,128)(2,1)} %broadcast_multiply_fusion), calls=%async_computation.2 | async-start | bytes 2097152 | tf_op jit(solution)/shard_map/all_to_all | solution.py:221
  60.6 2.0 %collective-permute-start.4 = (bf16[16,32,512]{2,1,0:T(8,128)(2,1)S(1)}, bf16[16,32,512]{2,1,0:T(8,128)(2,1)S(1)}, u32[]{:S(2)}, u32[]{:S(2)}) collective-permute-start(bf16[16,32,512]{2,1,0:T(8,128)(2,1)S(1)} %maximum_select_fusion.1), channel_id=1, source_target_pairs={{0,1},{1,0},{2,3},{3,2},{4,5},{5,4},{6,7},{7,6},{8,9},{9,8},{10,11... | collective-permute-start | bytes 1572872 | tf_op jit(solution)/shard_map/ppermute | solution.py:138

commit v12 on v10

--- a/solution.py
+++ b/solution.py
@@ -72,9 +72,10 @@
     return weight.reshape(count * BOX, xs.shape[0]).astype(jnp.bfloat16)
 
 
-def sample_points(xs, zs):
+def sample_points(xs, zs, turn=0):
     center = (BOX - 1) / 2.0
-    angle = jnp.arange(ROTS, dtype=jnp.float32)[None, :, None] * (2.0 * jnp.pi / ROTS)
+    steps = (jnp.arange(ROTS, dtype=jnp.int32) + turn) % ROTS
+    angle = steps.astype(jnp.float32)[None, :, None] * (2.0 * jnp.pi / ROTS)
     radius = (jnp.arange(CYCLES, dtype=jnp.float32)[None, None, :] + 0.5) * (BOX / (2.0 * CYCLES))
     wx = jnp.maximum(0.0, 1.0 - jnp.abs(xs[:, None, None] - center - radius * jnp.cos(angle)))
     wz = jnp.maximum(0.0, 1.0 - jnp.abs(zs[:, None, None] - center - radius * jnp.sin(angle)))
@@ -181,8 +182,16 @@
         "pky,kn->pyn", flipped, back_points(padded, xs, zs), preferred_element_type=jnp.float32
     )
     volume = volume.astype(jnp.bfloat16).reshape(count * BOX, xs.shape[0])
-    sample = lax.optimization_barrier(sample_points(xs, zs))
+    sample, turned_sample = lax.optimization_barrier(
+        (sample_points(xs, zs), jnp.stack([sample_points(xs, zs, q) for q in rotations]))
+    )
     cyl = jnp.dot(volume, sample, preferred_element_type=jnp.float32)
+    turned = jnp.einsum(
+        "pyk,pkn->pyn",
+        volume.reshape(count, BOX, xs.shape[0]),
+        turned_sample,
+        preferred_element_type=jnp.float32,
+    ).astype(jnp.bfloat16)
     cyl = cyl.astype(jnp.bfloat16).reshape(count, BOX, ROTS * CYCLES)
     owned = references.shape[0]
     parts = BOX // owned
@@ -210,9 +219,6 @@
         total * (power[:, None, None] + 1e-06) * (ref_power[None, :, None] + 1e-06)
     )
     scores = scores.reshape(count, CLASSES * ROTS)
-    columns = jnp.arange(ROTS * CYCLES, dtype=jnp.int32)
-    index = (columns[None, :] + rotations[:, None] * CYCLES) % (ROTS * CYCLES)
-    turned = jnp.take_along_axis(cyl, index[:, None, :], axis=2)
     member = (classes[:, None] == jnp.arange(CLASSES, dtype=jnp.int32)[None, :]).astype(
         jnp.bfloat16
     )

time: 87.2 us -> 98.5 us (1.13)
  other arithmetic: 9.63 us -> 14.3 us
  waiting for transfers between devices: 30.2 us -> 32.8 us
  matrix products: 5.21 us -> 7.78 us
  local copies, waits for them, and re-layouts: 7.79 us -> 10.1 us
  starting transfers between devices: 23.1 us -> 22.1 us
    all_to_all x1, waiting for transfers between devices: 20.5 us -> 16.6 us  [per_device(): lax.all_to_all(placed, 'dev', split_axis=1, concat_axis=0, tiled=True)]
    dot_general x0 -> x2, matrix products: none -> 3.63 us  [the longest x1 3.22 us: per_device(): jnp.einsum('pky,kn->pyn', flipped, back_points(padded, xs, zs), preferred...]
    all_to_all x1, starting transfers between devices: 7.3 us -> 3.82 us  [per_device(): lax.all_to_all(wanted, 'dev', split_axis=0, concat_axis=0, tiled=True)]
    all_to_all x1, waiting for transfers between devices: 1.12 us -> 4.55 us  [per_device(): lax.all_to_all(wanted, 'dev', split_axis=0, concat_axis=0, tiled=True)]
    dot_general x1, matrix products: 4.17 us -> 1.03 us  [per_device(): cyl = jnp.dot(volume, sample, preferred_element_type=jnp.float32)]
    ppermute x5, waiting for transfers between devices: 8.65 us -> 11.6 us  [double_gather(): lax.ppermute(block, 'dev', perm=[(i, i ^ step) for i in range(ndev)])]
    select_n x5, other arithmetic: 0.3 us -> 2.77 us  [double_gather(): jnp.where(low, jnp.concatenate([block, other], axis=0), jnp.concatenate([...]
    dot_general x2, matrix products: 0.59 us -> 2.66 us  [per_device(): jnp.einsum('pfm,cgm->pfgc', cyl_three[:, :, q], gathered[:, q], preferred...]
  transfers between devices with their start and end apart: 8 -> 8, of which waited for: 5 -> 5; matrix products, arithmetic and copies ran while one was open for 23% -> 30% of each run, Pallas kernels for 9% -> 8%
where the time goes in v12:
time: 98.5 us; the launch traced here: 97.8 us
  waiting for transfers between devices  32.8 us (33%)
  starting transfers between devices  22.1 us (22%)
  other arithmetic  14.3 us (15%)
  local copies, waits for them, and re-layouts  10.1 us (10%)
  matrix products  7.78 us (8%)
  Pallas kernels  7.63 us (8%)
  between operations  3.1 us (3%)
    all_to_all x1, waiting for transfers between devices, per_device(): lax.all_to_all(placed, 'dev', split_axis=1, concat_axis=0, tiled=True)  16.6 us
    ppermute x5, waiting for transfers between devices, double_gather(): lax.ppermute(block, 'dev', perm=[(i, i ^ step) for i in range(ndev)])  11.6 us
    ppermute x5, starting transfers between devices, double_gather(): lax.ppermute(block, 'dev', perm=[(i, i ^ step) for i in range(ndev)])  9.05 us
    pallas_call x1, Pallas kernels, cut_patches(): pl.pallas_call(functools.partial(cut_kernel, cap), out_shape=jax.ShapeDty...  7.63 us
    all_to_all x1, starting transfers between devices, per_device(): lax.all_to_all(placed, 'dev', split_axis=1, concat_axis=0, tiled=True)  5.89 us
    all_to_all x1, waiting for transfers between devices, per_device(): lax.all_to_all(wanted, 'dev', split_axis=0, concat_axis=0, tiled=True)  4.55 us
    convert_element_type x1, other arithmetic, back_points(): return weight.reshape(count * BOX, xs.shape[0]).astype(jnp.bfloat16)  4.47 us
    all_to_all x1, starting transfers between devices, per_device(): lax.all_to_all(wanted, 'dev', split_axis=0, concat_axis=0, tiled=True)  3.82 us
  transfers between devices with their start and end apart: 8, of which 5 were waited for; matrix products, arithmetic and copies ran while one was open for 30% of the time, Pallas kernels for 8%

profile of v12, /device:TPU:0, one launch (start us, length us, event | category | flops | bytes accessed | tf_op | source)
XLA Modules:
  0.0 97.8 jit_solution(8093326359326974236)
XLA Ops:
  0.7 0.9 copy.66
  1.5 0.2 copy.67
  1.7 4.1 %collective-permute-start = (bf16[1,32,512]{1,2,0:T(8,128)(2,1)S(1)}, bf16[1,32,512]{1,2,0:T(8,128)(2,1)S(1)}, u32[]{:S(2)}, u32[]{:S(2)}) collective-permute-start(bf16[1,32,512]{1,2,0:T(8,128)(2,1)S(1)} %bitcast.92), channel_id=1, source_target_pairs={{0,16},{1,17},{2,18},{3,19},{4,20},{5,21},{6,22},{7,23},{8,24},{9,... | collective-permute-start | bytes 98312 | tf_op jit(solution)/shard_map/ppermute | solution.py:139
  5.9 0.7 copy.85
  6.6 0.1 fusion.15
  6.7 0.2 select_reduce_fusion.1
  6.9 0.1 iota_compare_fusion.2
  7.0 0.1 iota_compare_fusion.3
  7.1 0.1 copy.73
  7.2 0.1 broadcast_and_fusion
  7.2 0.1 select_reduce_fusion
  7.4 0.7 copy.74
  8.1 3.8 %all-to-all-start = ((s32[32,2,3]{2,1,0:T(2,128)}), s32[32,2,3]{2,1,0:T(2,128)S(1)}, u32[]{:S(2)}, u32[]{:S(2)}) async-start(s32[32,2,3]{2,1,0:T(2,128)} %copy.74), calls=%async_computation | async-start | bytes 65536 | tf_op jit(solution)/shard_map/all_to_all | solution.py:166
  11.9 0.1 copy.68
  12.3 0.1 mul.264
  13.1 0.1 mul.274
  13.2 0.1 mul.275
  13.3 0.1 mul.278
  13.4 0.1 mul.269
  13.5 0.1 mul.270
  13.5 0.1 mul.266
  13.6 0.1 mul.267
  14.5 0.1 mul.285
  14.5 0.1 mul.286
  14.6 4.6 %all-to-all-done = s32[32,2,3]{2,1,0:T(2,128)S(1)} async-done(((s32[32,2,3]{2,1,0:T(2,128)}), s32[32,2,3]{2,1,0:T(2,128)S(1)}, u32[]{:S(2)}, u32[]{:S(2)}) %all-to-all-start) | async-done | bytes 800 | tf_op jit(solution)/shard_map/all_to_all | solution.py:166
  19.2 0.7 reshape_reshape.10.req_ref
  19.9 7.6 %shard_map.86 = bf16[32,64,128]{2,1,0:T(8,128)(2,1)} custom-call(s32[192]{0:T(256)} %reshape_reshape.10.req_ref, bf16[2,128,4096]{2,1,0:T(8,128)(2,1)} %tiles_ref.1), custom_call_target="tpu_custom_call" | custom-call | flops 67108864 | bytes 2621440 | tf_op jit(solution)/shard_map/pallas_call | solution.py:117
  27.5 3.3 %all-to-all-start.1 = ((bf16[32,64,128]{2,1,0:T(8,128)(2,1)}), bf16[32,64,128]{2,1,0:T(8,128)(2,1)}, u32[]{:S(2)}, u32[]{:S(2)}) async-start(bf16[32,64,128]{2,1,0:T(8,128)(2,1)} %shard_map.86), calls=%async_computation.1 | async-start | bytes 1048576 | tf_op jit(solution)/shard_map/all_to_all | solution.py:172
  30.9 0.1 add_add_fusion
  31.0 0.1 copy.69
  31.1 1.7 %collective-permute-start.1 = (bf16[2,32,512]{2,1,0:T(8,128)(2,1)S(1)}, bf16[2,32,512]{2,1,0:T(8,128)(2,1)S(1)}, u32[]{:S(2)}, u32[]{:S(2)}) collective-permute-start(bf16[2,32,512]{2,1,0:T(8,128)(2,1)S(1)} %maximum_select_fusion.4), channel_id=1, source_target_pairs={{0,8},{1,9},{2,10},{3,11},{4,12},{5,13},{6,14},{7,15},{8,0},{9,1},... | collective-permute-start | bytes 196616 | tf_op jit(solution)/shard_map/ppermute | solution.py:139
  32.8 4.5 %multiply_convert_fusion = bf16[22,64,1664]{2,1,0:T(8,128)(2,1)} fusion(f32[22,1664]{1,0:T(8,128)S(1)} %add_add_fusion, pred[22]{0:T(512)(128)(4,1)S(1)} %iota_compare_fusion.5), kind=kLoop, calls=%fused_computation.1 | loop fusion | flops 16400384 | bytes 4832278 | tf_op jit(solution)/shard_map/convert_element_type | solution.py:72
  37.3 3.9 %collective-permute-done.1 = bf16[2,32,512]{2,1,0:T(8,128)(2,1)S(1)} collective-permute-done((bf16[2,32,512]{2,1,0:T(8,128)(2,1)S(1)}, bf16[2,32,512]{2,1,0:T(8,128)(2,1)S(1)}, u32[]{:S(2)}, u32[]{:S(2)}) %collective-permute-start.1) | collective-permute-done | bytes 65568 | tf_op jit(solution)/shard_map/ppermute | solution.py:139
  41.2 1.8 %collective-permute-start.2 = (bf16[4,32,512]{2,1,0:T(8,128)(2,1)S(1)}, bf16[4,32,512]{2,1,0:T(8,128)(2,1)S(1)}, u32[]{:S(2)}, u32[]{:S(2)}) collective-permute-start(bf16[4,32,512]{2,1,0:T(8,128)(2,1)S(1)} %maximum_select_fusion.3), channel_id=1, source_target_pairs={{0,4},{1,5},{2,6},{3,7},{4,0},{5,1},{6,2},{7,3},{8,12},{9,13},{10,... | collective-permute-start | bytes 393224 | tf_op jit(solution)/shard_map/ppermute | solution.py:139
  43.0 1.2 %multiply_convert_fusion.2 = bf16[1664,512]{1,0:T(8,128)(2,1)S(1)} fusion(f32[512]{0:T(512)S(1)} %get-tuple-element.16, f32[1664]{0:T(1024)S(1)} %get-tuple-element.22, f32[512]{0:T(512)S(1)} %get-tuple-element.17, f32[1664]{0:T(1024)S(1)} %get-tuple-element.23), kind=kLoop, calls=%fused_computation.3 | loop fusion | flops 8519680 | bytes 1721344 | tf_op jit(solution)/shard_map/convert_element_type | solution.py:82
  44.2 3.0 %collective-permute-done.2 = bf16[4,32,512]{2,1,0:T(8,128)(2,1)S(1)} collective-permute-done((bf16[4,32,512]{2,1,0:T(8,128)(2,1)S(1)}, bf16[4,32,512]{2,1,0:T(8,128)(2,1)S(1)}, u32[]{:S(2)}, u32[]{:S(2)}) %collective-permute-start.2) | collective-permute-done | bytes 131104 | tf_op jit(solution)/shard_map/ppermute | solution.py:139
  47.2 1.5 %collective-permute-start.3 = (bf16[8,32,512]{2,1,0:T(8,128)(2,1)S(1)}, bf16[8,32,512]{2,1,0:T(8,128)(2,1)S(1)}, u32[]{:S(2)}, u32[]{:S(2)}) collective-permute-start(bf16[8,32,512]{2,1,0:T(8,128)(2,1)S(1)} %maximum_select_fusion.2), channel_id=1, source_target_pairs={{0,2},{1,3},{2,0},{3,1},{4,6},{5,7},{6,4},{7,5},{8,10},{9,11},{10,... | collective-permute-start | bytes 786440 | tf_op jit(solution)/shard_map/ppermute | solution.py:139
  48.8 1.2 %multiply_convert_fusion.1 = bf16[1,1664,512]{2,1,0:T(8,128)(2,1)S(1)} fusion(f32[512]{0:T(512)S(1)} %get-tuple-element.15, f32[1664]{0:T(1024)S(1)} %get-tuple-element.22, f32[512]{0:T(512)S(1)} %get-tuple-element.14, f32[1664]{0:T(1024)S(1)} %get-tuple-element.23), kind=kLoop, calls=%fused_computation.2 | loop fusion | flops 8519680 | bytes 1721344 | tf_op jit(solution)/shard_map/convert_element_type | solution.py:82
  50.0 4.7 %collective-permute-done.3 = bf16[8,32,512]{2,1,0:T(8,128)(2,1)S(1)} collective-permute-done((bf16[8,32,512]{2,1,0:T(8,128)(2,1)S(1)}, bf16[8,32,512]{2,1,0:T(8,128)(2,1)S(1)}, u32[]{:S(2)}, u32[]{:S(2)}) %collective-permute-start.3) | collective-permute-done | bytes 262176 | tf_op jit(solution)/shard_map/ppermute | solution.py:139
  54.7 0.9 maximum_select_fusion.1
  55.6 2.4 %gather_fusion = bf16[21,64,128]{2,1,0:T(8,128)(2,1)} fusion(bf16[32,64,128]{2,1,0:T(8,128)(2,1)} %all-to-all-done.1, s32[1024]{0:T(1024)S(1)} %pad_clamp_fusion), kind=kCustom, calls=%fused_computation | custom fusion | bytes 688212 | tf_op jit(solution)/shard_map/gather | solution.py:173
  58.0 1.3 %fusion.9 = bf16[1,21,64,64]{3,2,1,0:T(8,128)(2,1)S(1)} fusion(bf16[21,64,128]{2,1,0:T(8,128)(2,1)} %gather_fusion, pred[21]{0:T(512)(128)(4,1)S(1)} %get-tuple-element.19, pred[21]{0:T(512)(128)(4,1)S(1)} %get-tuple-element.18), kind=kLoop, calls=%fused_computation.24 | loop fusion | flops 258048 | bytes 516138 | tf_op jit(solution)/shard_map/reshape | solution.py:177
  59.3 0.1 pad.4
  59.4 3.2 %convolution_convert_fusion = bf16[64,1664]{1,0:T(8,128)(2,1)S(1)} fusion(bf16[1408,64]{1,0:T(8,128)(2,1)S(1)} %bitcast.88, bf16[1408,1664]{1,0:T(8,128)(2,1)} %bitcast.82), kind=kOutput, calls=%fused_computation.4 | convolution fusion | flops 299999232 | bytes 5079040 | tf_op jit(solution)/shard_map/pky,kn->pyn/dot_general | solution.py:181
  62.6 0.7 copy-done
  63.3 0.4 fusion.3
  63.7 0.1 mul.288
  63.8 1.1 %broadcast_multiply_fusion = bf16[1,32,32,512]{3,2,0,1:T(8,128)(2,1)} fusion(bf16[1,32,32,512]{3,2,0,1:T(8,128)(2,1)S(1)} %bitcast.85, bf16[32]{0:T(256)(128)(2,1)S(1)} %mul.286), kind=kLoop, calls=%fused_computation.20 | loop fusion | flops 524288 | bytes 2097216 | tf_op jit(solution)/shard_map/mul | solution.py:225
  64.9 5.9 %all-to-all-start.2 = ((bf16[1,32,32,512]{3,2,0,1:T(8,128)(2,1)}), bf16[1,32,32,512]{3,2,0,1:T(8,128)(2,1)S(1)}, u32[]{:S(2)}, u32[]{:S(2)}) async-start(bf16[1,32,32,512]{3,2,0,1:T(8,128)(2,1)} %broadcast_multiply_fusion), calls=%async_computation.2 | async-start | bytes 2097152 | tf_op jit(solution)/shard_map/all_to_all | solution.py:227
  70.9 1.8 %maximum_select_fusion = bf16[32,32,512]{2,1,0:T(8,128)(2,1)S(1)} fusion(bf16[16,32,512]{2,1,0:T(8,128)(2,1)} %collective-permute-done.4, bf16[16,32,512]{2,1,0:T(8,128)(2,1)} %maximum_select_fusion.1, pred[]{:T(512)S(6)} %eq.122), kind=kLoop, calls=%fused_computation.15 | loop fusion | flops 1572864 | bytes 2097153 | tf_op jit(solution)/shard_map/jit(_where)/select_n | solution.py:141
  72.7 1.1 %copy.72 = bf16[2,2,2,2,2,32,512]{6,5,3,2,1,0,4:T(8,128)(2,1)} copy(bf16[2,2,2,2,2,32,512]{6,5,0,1,2,3,4:T(8,128)(2,1)S(1)} %bitcast.83) | data formatting | bytes 2097152 | tf_op jit(solution)/shard_map/transpose | solution.py:146
  73.8 0.3 multiply_reduce_fusion
  74.1 1.0 %multiply_reduce_fusion.1 = (f32[]{:T(128)}, bf16[64,512]{1,0:T(8,128)(2,1)S(1)}) fusion(bf16[64,1664]{1,0:T(8,128)(2,1)S(1)} %copy-done.1, bf16[1664,512]{1,0:T(8,128)(2,1)S(1)} %multiply_convert_fusion.2), kind=kOutput, calls=%fused_computation.32 | convolution fusion | flops 109182976 | bytes 1982468 | tf_op jit(solution)/shard_map/dot_general | solution.py:188
  75.1 0.1 copy.75
  75.3 0.3 copy.76
  75.6 1.3 %fusion.7 = f32[16,32,32]{2,1,0:T(8,128)S(1)} fusion(bf16[16,2,32,512]{3,2,0,1:T(8,128)(2,1)} %bitcast.86, bf16[1,32,2,512]{1,3,2,0:T(8,128)(2,1)S(1)} %bitcast.89), kind=kOutput, calls=%fused_computation.18 | convolution fusion | flops 16777216 | bytes 720896 | tf_op jit(solution)/shard_map/pfm,cgm->pfgc/dot_general | solution.py:209
  76.9 1.3 %fusion.2 = f32[32,32,16]{0,1,2:T(8,128)S(1)} fusion(f32[16,32,32]{2,1,0:T(8,128)S(1)} %fusion.7, bf16[16,2,32,512]{3,2,0,1:T(8,128)(2,1)} %bitcast.87, bf16[1,32,2,512]{1,3,2,0:T(8,128)(2,1)S(1)} %bitcast.90), kind=kOutput, calls=%fused_computation.10 | convolution fusion | flops 16793600 | bytes 983040 | tf_op jit(solution)/shard_map/pfm,cgm->pfgc/dot_general | solution.py:209
  78.2 0.2 copy.79
  79.1 0.1 copy.80
  79.2 0.1 sqrt.12
  79.3 0.5 fusion.6
  79.7 0.7 reshape.689
  80.4 16.6 %all-to-all-done.2 = bf16[1,32,32,512]{3,2,0,1:T(8,128)(2,1)S(1)} async-done(((bf16[1,32,32,512]{3,2,0,1:T(8,128)(2,1)}), bf16[1,32,32,512]{3,2,0,1:T(8,128)(2,1)S(1)}, u32[]{:S(2)}, u32[]{:S(2)}) %all-to-all-start.2) | async-done | bytes 1048608 | tf_op jit(solution)/shard_map/all_to_all | solution.py:227
  97.0 0.8 convert_reduce_fusion
  (35 shorter events, 0.5 us)
Async XLA Ops:
  0.6 30.3 %copy-start.2 = (f32[1664]{0:T(1024)S(1)}, f32[1664]{0:T(1024)}, u32[]{:S(2)}) copy-start(f32[1664]{0:T(1024)} %constant.189.clone) | copy-start | bytes 19972
  0.6 30.2 %copy-start.3 = (f32[1664]{0:T(1024)S(1)}, f32[1664]{0:T(1024)}, u32[]{:S(2)}) copy-start(f32[1664]{0:T(1024)} %constant.190.clone) | copy-start | bytes 19972
  1.7 29.3 %collective-permute-start = (bf16[1,32,512]{1,2,0:T(8,128)(2,1)S(1)}, bf16[1,32,512]{1,2,0:T(8,128)(2,1)S(1)}, u32[]{:S(2)}, u32[]{:S(2)}) collective-permute-start(bf16[1,32,512]{1,2,0:T(8,128)(2,1)S(1)} %bitcast.92), channel_id=1, source_target_pairs={{0,16},{1,17},{2,18},{3,19},{4,20},{5,21},{6,22},{7,23},{8,24},{9,... | collective-permute-start | bytes 98312 | tf_op jit(solution)/shard_map/ppermute | solution.py:139
  8.1 11.1 %all-to-all-start = ((s32[32,2,3]{2,1,0:T(2,128)}), s32[32,2,3]{2,1,0:T(2,128)S(1)}, u32[]{:S(2)}, u32[]{:S(2)}) async-start(s32[32,2,3]{2,1,0:T(2,128)} %copy.74), calls=%async_computation | async-start | bytes 65536 | tf_op jit(solution)/shard_map/all_to_all | solution.py:166
  27.5 28.1 %all-to-all-start.1 = ((bf16[32,64,128]{2,1,0:T(8,128)(2,1)}), bf16[32,64,128]{2,1,0:T(8,128)(2,1)}, u32[]{:S(2)}, u32[]{:S(2)}) async-start(bf16[32,64,128]{2,1,0:T(8,128)(2,1)} %shard_map.86), calls=%async_computation.1 | async-start | bytes 1048576 | tf_op jit(solution)/shard_map/all_to_all | solution.py:172
  31.1 10.1 %collective-permute-start.1 = (bf16[2,32,512]{2,1,0:T(8,128)(2,1)S(1)}, bf16[2,32,512]{2,1,0:T(8,128)(2,1)S(1)}, u32[]{:S(2)}, u32[]{:S(2)}) collective-permute-start(bf16[2,32,512]{2,1,0:T(8,128)(2,1)S(1)} %maximum_select_fusion.4), channel_id=1, source_target_pairs={{0,8},{1,9},{2,10},{3,11},{4,12},{5,13},{6,14},{7,15},{8,0},{9,1},... | collective-permute-start | bytes 196616 | tf_op jit(solution)/shard_map/ppermute | solution.py:139
  41.2 6.0 %collective-permute-start.2 = (bf16[4,32,512]{2,1,0:T(8,128)(2,1)S(1)}, bf16[4,32,512]{2,1,0:T(8,128)(2,1)S(1)}, u32[]{:S(2)}, u32[]{:S(2)}) collective-permute-start(bf16[4,32,512]{2,1,0:T(8,128)(2,1)S(1)} %maximum_select_fusion.3), channel_id=1, source_target_pairs={{0,4},{1,5},{2,6},{3,7},{4,0},{5,1},{6,2},{7,3},{8,12},{9,13},{10,... | collective-permute-start | bytes 393224 | tf_op jit(solution)/shard_map/ppermute | solution.py:139
  47.2 7.4 %collective-permute-start.3 = (bf16[8,32,512]{2,1,0:T(8,128)(2,1)S(1)}, bf16[8,32,512]{2,1,0:T(8,128)(2,1)S(1)}, u32[]{:S(2)}, u32[]{:S(2)}) collective-permute-start(bf16[8,32,512]{2,1,0:T(8,128)(2,1)S(1)} %maximum_select_fusion.2), channel_id=1, source_target_pairs={{0,2},{1,3},{2,0},{3,1},{4,6},{5,7},{6,4},{7,5},{8,10},{9,11},{10,... | collective-permute-start | bytes 786440 | tf_op jit(solution)/shard_map/ppermute | solution.py:139
  55.6 15.3 %collective-permute-start.4 = (bf16[16,32,512]{2,1,0:T(8,128)(2,1)}, bf16[16,32,512]{2,1,0:T(8,128)(2,1)}, u32[]{:S(2)}, u32[]{:S(2)}) collective-permute-start(bf16[16,32,512]{2,1,0:T(8,128)(2,1)} %maximum_select_fusion.1), channel_id=1, source_target_pairs={{0,1},{1,0},{2,3},{3,2},{4,5},{5,4},{6,7},{7,6},{8,9},{9,8},{10,11... | collective-permute-start | bytes 1572872 | tf_op jit(solution)/shard_map/ppermute | solution.py:139
  62.6 0.7 copy-start
  64.9 9.2 %copy-start.1 = (bf16[64,1664]{1,0:T(8,128)(2,1)S(1)}, bf16[64,1664]{1,0:T(8,128)(2,1)}, u32[]{:S(2)}) copy-start(bf16[64,1664]{1,0:T(8,128)(2,1)} %copy-done) | copy-start | bytes 638980
  64.9 32.1 %all-to-all-start.2 = ((bf16[1,32,32,512]{3,2,0,1:T(8,128)(2,1)}), bf16[1,32,32,512]{3,2,0,1:T(8,128)(2,1)S(1)}, u32[]{:S(2)}, u32[]{:S(2)}) async-start(bf16[1,32,32,512]{3,2,0,1:T(8,128)(2,1)} %broadcast_multiply_fusion), calls=%async_computation.2 | async-start | bytes 2097152 | tf_op jit(solution)/shard_map/all_to_all | solution.py:227

commit v13 on v10

--- a/solution.py
+++ b/solution.py
@@ -101,8 +101,8 @@
             c = req_ref[3 * k + 2]
             r0 = pl.multiple_of(jnp.minimum((r // 16) * 16, rows - span), 16)
             c0 = pl.multiple_of(jnp.minimum((c // 128) * 128, width - WIN), 128)
-            win = tiles_ref[t, pl.ds(r0, span), pl.ds(c0, WIN)].astype(jnp.float32)
-            win = pltpu.roll(win, (WIN - (c - c0)) % WIN, 1)[:, :128]
+            win = tiles_ref[t, pl.ds(r0, span), pl.ds(c0, WIN)]
+            win = pltpu.roll(win, (WIN - (c - c0)) % WIN, 1)[:, :128].astype(jnp.float32)
             win = pltpu.roll(win, (span - (r - r0)) % span, 0)
             flip = win[:BOX, :].T
             out_ref[d, :, s * BOX : (s + 1) * BOX] = flip[:BOX, :BOX].astype(out_ref.dtype)

time: 87.2 us -> 89.3 us (1.024)
  Pallas kernels: 7.65 us -> 9.75 us
    pallas_call x1, Pallas kernels: 7.65 us -> 9.75 us  [cut_patches(): pl.pallas_call(functools.partial(cut_kernel, cap), out_shape=jax.ShapeDty...]
  transfers between devices with their start and end apart: 8 -> 8, of which waited for: 5 -> 5; matrix products, arithmetic and copies ran while one was open for 23% -> 22% of each run, Pallas kernels for 9% -> 11%
where the time goes in v13:
time: 89.3 us; the launch traced here: 88.8 us
  waiting for transfers between devices  30.2 us (34%)
  starting transfers between devices  23.1 us (26%)
  Pallas kernels  9.75 us (11%)
  other arithmetic  9.63 us (11%)
  local copies, waits for them, and re-layouts  7.79 us (9%)
  matrix products  5.21 us (6%)
  between operations  3.09 us (3%)
    all_to_all x1, waiting for transfers between devices, per_device(): lax.all_to_all(placed, 'dev', split_axis=1, concat_axis=0, tiled=True)  20.5 us
    pallas_call x1, Pallas kernels, cut_patches(): pl.pallas_call(functools.partial(cut_kernel, cap), out_shape=jax.ShapeDty...  9.75 us
    ppermute x5, waiting for transfers between devices, double_gather(): lax.ppermute(block, 'dev', perm=[(i, i ^ step) for i in range(ndev)])  8.65 us
    ppermute x5, starting transfers between devices, double_gather(): lax.ppermute(block, 'dev', perm=[(i, i ^ step) for i in range(ndev)])  8.11 us
    all_to_all x1, starting transfers between devices, per_device(): lax.all_to_all(wanted, 'dev', split_axis=0, concat_axis=0, tiled=True)  7.3 us
    all_to_all x1, starting transfers between devices, per_device(): lax.all_to_all(placed, 'dev', split_axis=1, concat_axis=0, tiled=True)  5.03 us
    convert_element_type x1, other arithmetic, back_points(): return weight.reshape(count * BOX, xs.shape[0]).astype(jnp.bfloat16)  4.48 us
    dot_general x1, matrix products, per_device(): cyl = jnp.dot(volume, sample, preferred_element_type=jnp.float32)  4.17 us
  transfers between devices with their start and end apart: 8, of which 5 were waited for; matrix products, arithmetic and copies ran while one was open for 22% of the time, Pallas kernels for 11%

profile of v13, /device:TPU:0, one launch (start us, length us, event | category | flops | bytes accessed | tf_op | source)
XLA Modules:
  0.0 88.8 jit_solution(10734346495911079300)
XLA Ops:
  0.6 0.0 copy-start
  0.6 0.0 copy-start.1
  0.7 0.7 copy.97
  1.4 0.1 fusion.12
  1.5 0.2 select_reduce_fusion.1
  1.7 0.1 iota_compare_fusion.2
  1.8 0.1 iota_compare_fusion.3
  1.9 0.1 copy.83
  2.0 0.1 broadcast_and_fusion
  2.1 0.1 select_reduce_fusion
  2.2 0.7 copy.84
  2.9 7.3 %all-to-all-start = ((s32[32,2,3]{2,1,0:T(2,128)}), s32[32,2,3]{2,1,0:T(2,128)S(1)}, u32[]{:S(2)}, u32[]{:S(2)}) async-start(s32[32,2,3]{2,1,0:T(2,128)} %copy.84), calls=%async_computation | async-start | bytes 65536 | tf_op jit(solution)/shard_map/all_to_all | solution.py:165
  10.2 0.9 copy.76
  11.1 0.2 copy.77
  11.3 2.7 %collective-permute-start = (bf16[1,32,512]{1,2,0:T(8,128)(2,1)S(1)}, bf16[1,32,512]{1,2,0:T(8,128)(2,1)S(1)}, u32[]{:S(2)}, u32[]{:S(2)}) collective-permute-start(bf16[1,32,512]{1,2,0:T(8,128)(2,1)S(1)} %bitcast.83), channel_id=1, source_target_pairs={{0,16},{1,17},{2,18},{3,19},{4,20},{5,21},{6,22},{7,23},{8,24},{9,... | collective-permute-start | bytes 98312 | tf_op jit(solution)/shard_map/ppermute | solution.py:138
  15.0 0.1 mul.200
  15.1 0.1 mul.203
  15.1 0.1 mul.204
  15.2 0.1 mul.206
  15.3 0.1 mul.207
  16.1 0.1 copy.78
  16.2 0.1 mul.214
  16.3 0.1 mul.215
  16.4 1.1 %all-to-all-done = s32[32,2,3]{2,1,0:T(2,128)S(1)} async-done(((s32[32,2,3]{2,1,0:T(2,128)}), s32[32,2,3]{2,1,0:T(2,128)S(1)}, u32[]{:S(2)}, u32[]{:S(2)}) %all-to-all-start) | async-done | bytes 800 | tf_op jit(solution)/shard_map/all_to_all | solution.py:165
  17.5 0.7 reshape_reshape.10.req_ref
  18.2 9.7 %shard_map.86 = bf16[32,64,128]{2,1,0:T(8,128)(2,1)} custom-call(s32[192]{0:T(256)} %reshape_reshape.10.req_ref, bf16[2,128,4096]{2,1,0:T(8,128)(2,1)} %tiles_ref.1), custom_call_target="tpu_custom_call" | custom-call | flops 67108864 | bytes 2621440 | tf_op jit(solution)/shard_map/pallas_call | solution.py:116
  28.0 2.6 %all-to-all-start.1 = ((bf16[32,64,128]{2,1,0:T(8,128)(2,1)}), bf16[32,64,128]{2,1,0:T(8,128)(2,1)S(1)}, u32[]{:S(2)}, u32[]{:S(2)}) async-start(bf16[32,64,128]{2,1,0:T(8,128)(2,1)} %shard_map.86), calls=%async_computation.1 | async-start | bytes 1048576 | tf_op jit(solution)/shard_map/all_to_all | solution.py:171
  30.6 0.1 add_add_fusion
  30.7 0.0 collective-permute-done
  30.7 0.1 copy.79
  30.9 1.8 %collective-permute-start.1 = (bf16[2,32,512]{2,1,0:T(8,128)(2,1)S(1)}, bf16[2,32,512]{2,1,0:T(8,128)(2,1)S(1)}, u32[]{:S(2)}, u32[]{:S(2)}) collective-permute-start(bf16[2,32,512]{2,1,0:T(8,128)(2,1)S(1)} %maximum_select_fusion.4), channel_id=1, source_target_pairs={{0,8},{1,9},{2,10},{3,11},{4,12},{5,13},{6,14},{7,15},{8,0},{9,1},... | collective-permute-start | bytes 196616 | tf_op jit(solution)/shard_map/ppermute | solution.py:138
  32.7 4.5 %multiply_convert_fusion = bf16[22,64,1664]{2,1,0:T(8,128)(2,1)} fusion(f32[22,1664]{1,0:T(8,128)S(1)} %add_add_fusion, pred[22]{0:T(512)(128)(4,1)S(1)} %iota_compare_fusion.5), kind=kLoop, calls=%fused_computation.2 | loop fusion | flops 16400384 | bytes 4832278 | tf_op jit(solution)/shard_map/convert_element_type | solution.py:72
  37.2 4.0 %collective-permute-done.1 = bf16[2,32,512]{2,1,0:T(8,128)(2,1)S(1)} collective-permute-done((bf16[2,32,512]{2,1,0:T(8,128)(2,1)S(1)}, bf16[2,32,512]{2,1,0:T(8,128)(2,1)S(1)}, u32[]{:S(2)}, u32[]{:S(2)}) %collective-permute-start.1) | collective-permute-done | bytes 65568 | tf_op jit(solution)/shard_map/ppermute | solution.py:138
  41.2 1.7 %collective-permute-start.2 = (bf16[4,32,512]{2,1,0:T(8,128)(2,1)S(1)}, bf16[4,32,512]{2,1,0:T(8,128)(2,1)S(1)}, u32[]{:S(2)}, u32[]{:S(2)}) collective-permute-start(bf16[4,32,512]{2,1,0:T(8,128)(2,1)S(1)} %maximum_select_fusion.3), channel_id=1, source_target_pairs={{0,4},{1,5},{2,6},{3,7},{4,0},{5,1},{6,2},{7,3},{8,12},{9,13},{10,... | collective-permute-start | bytes 393224 | tf_op jit(solution)/shard_map/ppermute | solution.py:138
  42.9 1.2 %multiply_convert_fusion.1 = bf16[1664,512]{1,0:T(8,128)(2,1)S(1)} fusion(f32[512]{0:T(512)S(1)} %get-tuple-element.11, f32[1664]{0:T(1024)S(1)} %get-tuple-element.16, f32[512]{0:T(512)S(1)} %get-tuple-element.10, f32[1664]{0:T(1024)S(1)} %get-tuple-element.17), kind=kLoop, calls=%fused_computation.3 | loop fusion | flops 8519680 | bytes 1721344 | tf_op jit(solution)/shard_map/convert_element_type | solution.py:81
  44.2 3.0 %collective-permute-done.2 = bf16[4,32,512]{2,1,0:T(8,128)(2,1)S(1)} collective-permute-done((bf16[4,32,512]{2,1,0:T(8,128)(2,1)S(1)}, bf16[4,32,512]{2,1,0:T(8,128)(2,1)S(1)}, u32[]{:S(2)}, u32[]{:S(2)}) %collective-permute-start.2) | collective-permute-done | bytes 131104 | tf_op jit(solution)/shard_map/ppermute | solution.py:138
  47.2 1.5 %collective-permute-start.3 = (bf16[8,32,512]{2,1,0:T(8,128)(2,1)S(1)}, bf16[8,32,512]{2,1,0:T(8,128)(2,1)S(1)}, u32[]{:S(2)}, u32[]{:S(2)}) collective-permute-start(bf16[8,32,512]{2,1,0:T(8,128)(2,1)S(1)} %maximum_select_fusion.2), channel_id=1, source_target_pairs={{0,2},{1,3},{2,0},{3,1},{4,6},{5,7},{6,4},{7,5},{8,10},{9,11},{10,... | collective-permute-start | bytes 786440 | tf_op jit(solution)/shard_map/ppermute | solution.py:138
  48.7 0.6 gather_fusion
  49.3 0.2 fusion.6
  49.5 0.1 pad.4
  49.6 4.2 %multiply_reduce_fusion.1 = (f32[]{:T(128)}, bf16[64,512]{1,0:T(8,128)(2,1)S(1)}) fusion(bf16[1664,512]{1,0:T(8,128)(2,1)S(1)} %multiply_convert_fusion.1, bf16[1408,64]{1,0:T(8,128)(2,1)S(1)} %bitcast.80, bf16[1408,1664]{1,0:T(8,128)(2,1)} %bitcast.73), kind=kOutput, calls=%fused_computation.31 | convolution fusion | flops 409182208 | bytes 6635524 | tf_op jit(solution)/shard_map/dot_general | solution.py:185
  53.8 0.1 copy.85
  53.9 1.3 %gather_fusion.1 = bf16[512,64]{1,0:T(8,128)(2,1)S(1)} fusion(bf16[64,512]{0,1:T(8,128)(2,1)S(1)} %copy.85, s32[1024]{0:T(1024)S(1)} %pad_clamp_fusion), kind=kCustom, calls=%fused_computation.1 | custom fusion | bytes 133120 | tf_op jit(solution)/shard_map/jit(take_along_axis)/gather | solution.py:215
  55.2 0.1 select_bitcast_fusion
  55.4 0.1 copy.92
  55.5 0.1 mul.218
  55.6 1.1 %broadcast_multiply_fusion = bf16[1,32,32,512]{3,2,0,1:T(8,128)(2,1)} fusion(bf16[1,32,32,512]{3,2,0,1:T(8,128)(2,1)S(1)} %bitcast.77, bf16[32]{0:T(256)(128)(2,1)S(1)} %mul.215), kind=kLoop, calls=%fused_computation.18 | loop fusion | flops 524288 | bytes 2097216 | tf_op jit(solution)/shard_map/mul | solution.py:219
  56.7 5.0 %all-to-all-start.2 = ((bf16[1,32,32,512]{3,2,0,1:T(8,128)(2,1)}), bf16[1,32,32,512]{3,2,0,1:T(8,128)(2,1)S(1)}, u32[]{:S(2)}, u32[]{:S(2)}) async-start(bf16[1,32,32,512]{3,2,0,1:T(8,128)(2,1)} %broadcast_multiply_fusion), calls=%async_computation.2 | async-start | bytes 2097152 | tf_op jit(solution)/shard_map/all_to_all | solution.py:221
  61.8 0.1 maximum_select_fusion.1
  61.9 0.3 collective-permute-start.4
  62.2 1.6 %collective-permute-done.4 = bf16[16,32,512]{2,1,0:T(8,128)(2,1)S(1)} collective-permute-done((bf16[16,32,512]{2,1,0:T(8,128)(2,1)S(1)}, bf16[16,32,512]{2,1,0:T(8,128)(2,1)S(1)}, u32[]{:S(2)}, u32[]{:S(2)}) %collective-permute-start.4) | collective-permute-done | bytes 524320 | tf_op jit(solution)/shard_map/ppermute | solution.py:138
  63.9 0.2 maximum_select_fusion
  64.0 0.1 copy.82
  64.1 0.3 multiply_reduce_fusion
  65.1 0.1 copy.90
  65.2 0.1 sqrt.12
  65.3 0.3 copy.86
  65.6 0.3 fusion.4
  65.9 0.3 fusion
  66.2 0.2 copy.89
  66.4 0.5 fusion.3
  66.8 0.7 reshape.615
  67.5 20.5 %all-to-all-done.2 = bf16[1,32,32,512]{3,2,0,1:T(8,128)(2,1)S(1)} async-done(((bf16[1,32,32,512]{3,2,0,1:T(8,128)(2,1)}), bf16[1,32,32,512]{3,2,0,1:T(8,128)(2,1)S(1)}, u32[]{:S(2)}, u32[]{:S(2)}) %all-to-all-start.2) | async-done | bytes 1048608 | tf_op jit(solution)/shard_map/all_to_all | solution.py:221
  88.0 0.8 convert_reduce_fusion
  (29 shorter events, 0.4 us)
Async XLA Ops:
  0.6 30.0 %copy-start = (f32[1664]{0:T(1024)S(1)}, f32[1664]{0:T(1024)}, u32[]{:S(2)}) copy-start(f32[1664]{0:T(1024)} %constant.207.clone) | copy-start | bytes 19972
  0.6 30.0 %copy-start.1 = (f32[1664]{0:T(1024)S(1)}, f32[1664]{0:T(1024)}, u32[]{:S(2)}) copy-start(f32[1664]{0:T(1024)} %constant.208.clone) | copy-start | bytes 19972
  2.9 14.6 %all-to-all-start = ((s32[32,2,3]{2,1,0:T(2,128)}), s32[32,2,3]{2,1,0:T(2,128)S(1)}, u32[]{:S(2)}, u32[]{:S(2)}) async-start(s32[32,2,3]{2,1,0:T(2,128)} %copy.84), calls=%async_computation | async-start | bytes 65536 | tf_op jit(solution)/shard_map/all_to_all | solution.py:165
  11.3 19.4 %collective-permute-start = (bf16[1,32,512]{1,2,0:T(8,128)(2,1)S(1)}, bf16[1,32,512]{1,2,0:T(8,128)(2,1)S(1)}, u32[]{:S(2)}, u32[]{:S(2)}) collective-permute-start(bf16[1,32,512]{1,2,0:T(8,128)(2,1)S(1)} %bitcast.83), channel_id=1, source_target_pairs={{0,16},{1,17},{2,18},{3,19},{4,20},{5,21},{6,22},{7,23},{8,24},{9,... | collective-permute-start | bytes 98312 | tf_op jit(solution)/shard_map/ppermute | solution.py:138
  28.0 20.7 %all-to-all-start.1 = ((bf16[32,64,128]{2,1,0:T(8,128)(2,1)}), bf16[32,64,128]{2,1,0:T(8,128)(2,1)S(1)}, u32[]{:S(2)}, u32[]{:S(2)}) async-start(bf16[32,64,128]{2,1,0:T(8,128)(2,1)} %shard_map.86), calls=%async_computation.1 | async-start | bytes 1048576 | tf_op jit(solution)/shard_map/all_to_all | solution.py:171
  30.9 10.3 %collective-permute-start.1 = (bf16[2,32,512]{2,1,0:T(8,128)(2,1)S(1)}, bf16[2,32,512]{2,1,0:T(8,128)(2,1)S(1)}, u32[]{:S(2)}, u32[]{:S(2)}) collective-permute-start(bf16[2,32,512]{2,1,0:T(8,128)(2,1)S(1)} %maximum_select_fusion.4), channel_id=1, source_target_pairs={{0,8},{1,9},{2,10},{3,11},{4,12},{5,13},{6,14},{7,15},{8,0},{9,1},... | collective-permute-start | bytes 196616 | tf_op jit(solution)/shard_map/ppermute | solution.py:138
  41.2 6.0 %collective-permute-start.2 = (bf16[4,32,512]{2,1,0:T(8,128)(2,1)S(1)}, bf16[4,32,512]{2,1,0:T(8,128)(2,1)S(1)}, u32[]{:S(2)}, u32[]{:S(2)}) collective-permute-start(bf16[4,32,512]{2,1,0:T(8,128)(2,1)S(1)} %maximum_select_fusion.3), channel_id=1, source_target_pairs={{0,4},{1,5},{2,6},{3,7},{4,0},{5,1},{6,2},{7,3},{8,12},{9,13},{10,... | collective-permute-start | bytes 393224 | tf_op jit(solution)/shard_map/ppermute | solution.py:138
  47.2 14.6 %collective-permute-start.3 = (bf16[8,32,512]{2,1,0:T(8,128)(2,1)S(1)}, bf16[8,32,512]{2,1,0:T(8,128)(2,1)S(1)}, u32[]{:S(2)}, u32[]{:S(2)}) collective-permute-start(bf16[8,32,512]{2,1,0:T(8,128)(2,1)S(1)} %maximum_select_fusion.2), channel_id=1, source_target_pairs={{0,2},{1,3},{2,0},{3,1},{4,6},{5,7},{6,4},{7,5},{8,10},{9,11},{10,... | collective-permute-start | bytes 786440 | tf_op jit(solution)/shard_map/ppermute | solution.py:138
  56.7 31.3 %all-to-all-start.2 = ((bf16[1,32,32,512]{3,2,0,1:T(8,128)(2,1)}), bf16[1,32,32,512]{3,2,0,1:T(8,128)(2,1)S(1)}, u32[]{:S(2)}, u32[]{:S(2)}) async-start(bf16[1,32,32,512]{3,2,0,1:T(8,128)(2,1)} %broadcast_multiply_fusion), calls=%async_computation.2 | async-start | bytes 2097152 | tf_op jit(solution)/shard_map/all_to_all | solution.py:221
  61.9 2.0 %collective-permute-start.4 = (bf16[16,32,512]{2,1,0:T(8,128)(2,1)S(1)}, bf16[16,32,512]{2,1,0:T(8,128)(2,1)S(1)}, u32[]{:S(2)}, u32[]{:S(2)}) collective-permute-start(bf16[16,32,512]{2,1,0:T(8,128)(2,1)S(1)} %maximum_select_fusion.1), channel_id=1, source_target_pairs={{0,1},{1,0},{2,3},{3,2},{4,5},{5,4},{6,7},{7,6},{8,9},{9,8},{10,11... | collective-permute-start | bytes 1572872 | tf_op jit(solution)/shard_map/ppermute | solution.py:138

commit v14 on v10

--- a/solution.py
+++ b/solution.py
@@ -210,9 +210,13 @@
         total * (power[:, None, None] + 1e-06) * (ref_power[None, :, None] + 1e-06)
     )
     scores = scores.reshape(count, CLASSES * ROTS)
-    columns = jnp.arange(ROTS * CYCLES, dtype=jnp.int32)
-    index = (columns[None, :] + rotations[:, None] * CYCLES) % (ROTS * CYCLES)
-    turned = jnp.take_along_axis(cyl, index[:, None, :], axis=2)
+    doubled = jnp.concatenate([cyl, cyl], axis=2)
+    turned = jnp.stack(
+        [
+            lax.dynamic_slice_in_dim(doubled[p], rotations[p] * CYCLES, ROTS * CYCLES, axis=1)
+            for p in range(count)
+        ]
+    )
     member = (classes[:, None] == jnp.arange(CLASSES, dtype=jnp.int32)[None, :]).astype(
         jnp.bfloat16
     )

time: 87.2 us -> 85.6 us (0.982)
  local copies, waits for them, and re-layouts: 7.79 us -> 6.35 us
    gather x1 -> x0, local copies, waits for them, and re-layouts: 1.34 us -> none  [per_device(): turned = jnp.take_along_axis(cyl, index[:, None, :], axis=2)]
  transfers between devices with their start and end apart: 8 -> 8, of which waited for: 5 -> 5; matrix products, arithmetic and copies ran while one was open for 23% -> 21% of each run, Pallas kernels for 9% -> 9%
where the time goes in v14:
time: 85.6 us; the launch traced here: 85.1 us
  waiting for transfers between devices  30.1 us (35%)
  starting transfers between devices  23 us (27%)
  other arithmetic  9.58 us (11%)
  Pallas kernels  7.65 us (9%)
  local copies, waits for them, and re-layouts  6.35 us (7%)
  matrix products  5.21 us (6%)
  between operations  3.09 us (4%)
    all_to_all x1, waiting for transfers between devices, per_device(): lax.all_to_all(placed, 'dev', split_axis=1, concat_axis=0, tiled=True)  20.3 us
    ppermute x5, waiting for transfers between devices, double_gather(): lax.ppermute(block, 'dev', perm=[(i, i ^ step) for i in range(ndev)])  8.65 us
    ppermute x5, starting transfers between devices, double_gather(): lax.ppermute(block, 'dev', perm=[(i, i ^ step) for i in range(ndev)])  8.1 us
    pallas_call x1, Pallas kernels, cut_patches(): pl.pallas_call(functools.partial(cut_kernel, cap), out_shape=jax.ShapeDty...  7.65 us
    all_to_all x1, starting transfers between devices, per_device(): lax.all_to_all(wanted, 'dev', split_axis=0, concat_axis=0, tiled=True)  7.3 us
    all_to_all x1, starting transfers between devices, per_device(): lax.all_to_all(placed, 'dev', split_axis=1, concat_axis=0, tiled=True)  5.04 us
    convert_element_type x1, other arithmetic, back_points(): return weight.reshape(count * BOX, xs.shape[0]).astype(jnp.bfloat16)  4.48 us
    dot_general x1, matrix products, per_device(): cyl = jnp.dot(volume, sample, preferred_element_type=jnp.float32)  4.17 us
  transfers between devices with their start and end apart: 8, of which 5 were waited for; matrix products, arithmetic and copies ran while one was open for 21% of the time, Pallas kernels for 9%

profile of v14, /device:TPU:0, one launch (start us, length us, event | category | flops | bytes accessed | tf_op | source)
XLA Modules:
  0.0 85.1 jit_solution(9947285463315440831)
XLA Ops:
  0.6 0.0 copy-start
  0.6 0.0 copy-start.1
  0.7 0.7 copy.85
  1.4 0.1 fusion.14
  1.5 0.2 select_reduce_fusion.1
  1.7 0.1 iota_compare_fusion.2
  1.8 0.1 iota_compare_fusion.3
  1.9 0.1 copy.73
  2.0 0.1 broadcast_and_fusion
  2.1 0.1 select_reduce_fusion
  2.2 0.7 copy.74
  2.9 7.3 %all-to-all-start = ((s32[32,2,3]{2,1,0:T(2,128)}), s32[32,2,3]{2,1,0:T(2,128)S(1)}, u32[]{:S(2)}, u32[]{:S(2)}) async-start(s32[32,2,3]{2,1,0:T(2,128)} %copy.74), calls=%async_computation | async-start | bytes 65536 | tf_op jit(solution)/shard_map/all_to_all | solution.py:165
  10.2 0.9 %copy.66 = bf16[32,512]{0,1:T(8,128)(2,1)S(1)} copy(bf16[32,512]{1,0:T(8,128)(2,1)} %param.11) | data formatting | bytes 65536 | tf_op args[4]
  11.1 0.2 copy.67
  11.3 2.7 %collective-permute-start = (bf16[1,32,512]{1,2,0:T(8,128)(2,1)S(1)}, bf16[1,32,512]{1,2,0:T(8,128)(2,1)S(1)}, u32[]{:S(2)}, u32[]{:S(2)}) collective-permute-start(bf16[1,32,512]{1,2,0:T(8,128)(2,1)S(1)} %bitcast.84), channel_id=1, source_target_pairs={{0,16},{1,17},{2,18},{3,19},{4,20},{5,21},{6,22},{7,23},{8,24},{9,... | collective-permute-start | bytes 98312 | tf_op jit(solution)/shard_map/ppermute | solution.py:138
  14.3 0.1 mul.204
  14.4 0.1 mul.207
  14.4 0.1 mul.208
  14.5 0.1 mul.210
  14.6 0.1 mul.211
  15.4 0.1 copy.68
  16.2 0.1 mul.218
  16.2 0.1 mul.219
  16.4 1.2 %all-to-all-done = s32[32,2,3]{2,1,0:T(2,128)S(1)} async-done(((s32[32,2,3]{2,1,0:T(2,128)}), s32[32,2,3]{2,1,0:T(2,128)S(1)}, u32[]{:S(2)}, u32[]{:S(2)}) %all-to-all-start) | async-done | bytes 800 | tf_op jit(solution)/shard_map/all_to_all | solution.py:165
  17.5 0.7 reshape_reshape.10.req_ref
  18.2 7.6 %shard_map.86 = bf16[32,64,128]{2,1,0:T(8,128)(2,1)} custom-call(s32[192]{0:T(256)} %reshape_reshape.10.req_ref, bf16[2,128,4096]{2,1,0:T(8,128)(2,1)} %tiles_ref.1), custom_call_target="tpu_custom_call" | custom-call | flops 67108864 | bytes 2621440 | tf_op jit(solution)/shard_map/pallas_call | solution.py:116
  25.9 2.6 %all-to-all-start.1 = ((bf16[32,64,128]{2,1,0:T(8,128)(2,1)}), bf16[32,64,128]{2,1,0:T(8,128)(2,1)S(1)}, u32[]{:S(2)}, u32[]{:S(2)}) async-start(bf16[32,64,128]{2,1,0:T(8,128)(2,1)} %shard_map.86), calls=%async_computation.1 | async-start | bytes 1048576 | tf_op jit(solution)/shard_map/all_to_all | solution.py:171
  28.5 0.1 add_add_fusion
  28.6 0.0 collective-permute-done
  28.6 0.1 copy.69
  28.7 1.8 %collective-permute-start.1 = (bf16[2,32,512]{2,1,0:T(8,128)(2,1)S(1)}, bf16[2,32,512]{2,1,0:T(8,128)(2,1)S(1)}, u32[]{:S(2)}, u32[]{:S(2)}) collective-permute-start(bf16[2,32,512]{2,1,0:T(8,128)(2,1)S(1)} %maximum_select_fusion.4), channel_id=1, source_target_pairs={{0,8},{1,9},{2,10},{3,11},{4,12},{5,13},{6,14},{7,15},{8,0},{9,1},... | collective-permute-start | bytes 196616 | tf_op jit(solution)/shard_map/ppermute | solution.py:138
  30.6 4.5 %multiply_convert_fusion = bf16[22,64,1664]{2,1,0:T(8,128)(2,1)} fusion(f32[22,1664]{1,0:T(8,128)S(1)} %add_add_fusion, pred[22]{0:T(512)(128)(4,1)S(1)} %iota_compare_fusion.5), kind=kLoop, calls=%fused_computation.1 | loop fusion | flops 16400384 | bytes 4832278 | tf_op jit(solution)/shard_map/convert_element_type | solution.py:72
  35.0 4.0 %collective-permute-done.1 = bf16[2,32,512]{2,1,0:T(8,128)(2,1)S(1)} collective-permute-done((bf16[2,32,512]{2,1,0:T(8,128)(2,1)S(1)}, bf16[2,32,512]{2,1,0:T(8,128)(2,1)S(1)}, u32[]{:S(2)}, u32[]{:S(2)}) %collective-permute-start.1) | collective-permute-done | bytes 65568 | tf_op jit(solution)/shard_map/ppermute | solution.py:138
  39.1 1.7 %collective-permute-start.2 = (bf16[4,32,512]{2,1,0:T(8,128)(2,1)S(1)}, bf16[4,32,512]{2,1,0:T(8,128)(2,1)S(1)}, u32[]{:S(2)}, u32[]{:S(2)}) collective-permute-start(bf16[4,32,512]{2,1,0:T(8,128)(2,1)S(1)} %maximum_select_fusion.3), channel_id=1, source_target_pairs={{0,4},{1,5},{2,6},{3,7},{4,0},{5,1},{6,2},{7,3},{8,12},{9,13},{10,... | collective-permute-start | bytes 393224 | tf_op jit(solution)/shard_map/ppermute | solution.py:138
  40.8 1.2 %multiply_convert_fusion.1 = bf16[1664,512]{1,0:T(8,128)(2,1)S(1)} fusion(f32[512]{0:T(512)S(1)} %get-tuple-element.11, f32[1664]{0:T(1024)S(1)} %get-tuple-element.16, f32[512]{0:T(512)S(1)} %get-tuple-element.10, f32[1664]{0:T(1024)S(1)} %get-tuple-element.17), kind=kLoop, calls=%fused_computation.2 | loop fusion | flops 8519680 | bytes 1721344 | tf_op jit(solution)/shard_map/convert_element_type | solution.py:81
  42.0 3.0 %collective-permute-done.2 = bf16[4,32,512]{2,1,0:T(8,128)(2,1)S(1)} collective-permute-done((bf16[4,32,512]{2,1,0:T(8,128)(2,1)S(1)}, bf16[4,32,512]{2,1,0:T(8,128)(2,1)S(1)}, u32[]{:S(2)}, u32[]{:S(2)}) %collective-permute-start.2) | collective-permute-done | bytes 131104 | tf_op jit(solution)/shard_map/ppermute | solution.py:138
  45.1 1.5 %collective-permute-start.3 = (bf16[8,32,512]{2,1,0:T(8,128)(2,1)S(1)}, bf16[8,32,512]{2,1,0:T(8,128)(2,1)S(1)}, u32[]{:S(2)}, u32[]{:S(2)}) collective-permute-start(bf16[8,32,512]{2,1,0:T(8,128)(2,1)S(1)} %maximum_select_fusion.2), channel_id=1, source_target_pairs={{0,2},{1,3},{2,0},{3,1},{4,6},{5,7},{6,4},{7,5},{8,10},{9,11},{10,... | collective-permute-start | bytes 786440 | tf_op jit(solution)/shard_map/ppermute | solution.py:138
  46.5 0.0 all-to-all-done.1
  46.6 0.6 gather_fusion
  47.2 0.2 fusion.6
  47.4 0.1 pad.4
  47.5 4.2 %multiply_reduce_fusion.1 = (f32[]{:T(128)}, bf16[64,512]{1,0:T(8,128)(2,1)S(1)}) fusion(bf16[1664,512]{1,0:T(8,128)(2,1)S(1)} %multiply_convert_fusion.1, bf16[1408,64]{1,0:T(8,128)(2,1)S(1)} %bitcast.79, bf16[1408,1664]{1,0:T(8,128)(2,1)} %bitcast.73), kind=kOutput, calls=%fused_computation.31 | convolution fusion | flops 409182208 | bytes 6635524 | tf_op jit(solution)/shard_map/dot_general | solution.py:185
  51.6 0.1 fusion.9
  51.8 0.1 mul.224
  51.9 1.1 %broadcast_multiply_fusion = bf16[1,32,32,512]{3,2,0,1:T(8,128)(2,1)} fusion(bf16[1,32,32,512]{3,2,0,1:T(8,128)(2,1)S(1)} %bitcast.76, bf16[32]{0:T(256)(128)(2,1)S(1)} %mul.219), kind=kLoop, calls=%fused_computation.17 | loop fusion | flops 524288 | bytes 2097216 | tf_op jit(solution)/shard_map/mul | solution.py:223
  53.0 5.0 %all-to-all-start.2 = ((bf16[1,32,32,512]{3,2,0,1:T(8,128)(2,1)}), bf16[1,32,32,512]{3,2,0,1:T(8,128)(2,1)S(1)}, u32[]{:S(2)}, u32[]{:S(2)}) async-start(bf16[1,32,32,512]{3,2,0,1:T(8,128)(2,1)} %broadcast_multiply_fusion), calls=%async_computation.2 | async-start | bytes 2097152 | tf_op jit(solution)/shard_map/all_to_all | solution.py:225
  58.1 0.0 collective-permute-done.3
  58.1 0.1 maximum_select_fusion.1
  58.2 0.3 collective-permute-start.4
  58.5 1.6 %collective-permute-done.4 = bf16[16,32,512]{2,1,0:T(8,128)(2,1)S(1)} collective-permute-done((bf16[16,32,512]{2,1,0:T(8,128)(2,1)S(1)}, bf16[16,32,512]{2,1,0:T(8,128)(2,1)S(1)}, u32[]{:S(2)}, u32[]{:S(2)}) %collective-permute-start.4) | collective-permute-done | bytes 524320 | tf_op jit(solution)/shard_map/ppermute | solution.py:138
  60.1 0.2 maximum_select_fusion
  60.3 0.1 copy.72
  60.4 0.3 multiply_reduce_fusion
  60.7 0.1 copy.75
  61.5 0.1 copy.80
  61.7 0.1 sqrt.12
  61.7 0.3 copy.76
  62.0 0.3 fusion.4
  62.3 0.3 fusion
  62.6 0.2 copy.79
  62.8 0.5 fusion.3
  63.3 0.7 reshape.494
  63.9 20.3 %all-to-all-done.2 = bf16[1,32,32,512]{3,2,0,1:T(8,128)(2,1)S(1)} async-done(((bf16[1,32,32,512]{3,2,0,1:T(8,128)(2,1)}), bf16[1,32,32,512]{3,2,0,1:T(8,128)(2,1)S(1)}, u32[]{:S(2)}, u32[]{:S(2)}) %all-to-all-start.2) | async-done | bytes 1048608 | tf_op jit(solution)/shard_map/all_to_all | solution.py:225
  84.3 0.8 convert_reduce_fusion
  (24 shorter events, 0.4 us)
Async XLA Ops:
  0.6 27.9 %copy-start = (f32[1664]{0:T(1024)S(1)}, f32[1664]{0:T(1024)}, u32[]{:S(2)}) copy-start(f32[1664]{0:T(1024)} %constant.180.clone) | copy-start | bytes 19972
  0.6 27.9 %copy-start.1 = (f32[1664]{0:T(1024)S(1)}, f32[1664]{0:T(1024)}, u32[]{:S(2)}) copy-start(f32[1664]{0:T(1024)} %constant.181.clone) | copy-start | bytes 19972
  2.9 14.6 %all-to-all-start = ((s32[32,2,3]{2,1,0:T(2,128)}), s32[32,2,3]{2,1,0:T(2,128)S(1)}, u32[]{:S(2)}, u32[]{:S(2)}) async-start(s32[32,2,3]{2,1,0:T(2,128)} %copy.74), calls=%async_computation | async-start | bytes 65536 | tf_op jit(solution)/shard_map/all_to_all | solution.py:165
  11.3 17.3 %collective-permute-start = (bf16[1,32,512]{1,2,0:T(8,128)(2,1)S(1)}, bf16[1,32,512]{1,2,0:T(8,128)(2,1)S(1)}, u32[]{:S(2)}, u32[]{:S(2)}) collective-permute-start(bf16[1,32,512]{1,2,0:T(8,128)(2,1)S(1)} %bitcast.84), channel_id=1, source_target_pairs={{0,16},{1,17},{2,18},{3,19},{4,20},{5,21},{6,22},{7,23},{8,24},{9,... | collective-permute-start | bytes 98312 | tf_op jit(solution)/shard_map/ppermute | solution.py:138
  25.9 20.7 %all-to-all-start.1 = ((bf16[32,64,128]{2,1,0:T(8,128)(2,1)}), bf16[32,64,128]{2,1,0:T(8,128)(2,1)S(1)}, u32[]{:S(2)}, u32[]{:S(2)}) async-start(bf16[32,64,128]{2,1,0:T(8,128)(2,1)} %shard_map.86), calls=%async_computation.1 | async-start | bytes 1048576 | tf_op jit(solution)/shard_map/all_to_all | solution.py:171
  28.7 10.3 %collective-permute-start.1 = (bf16[2,32,512]{2,1,0:T(8,128)(2,1)S(1)}, bf16[2,32,512]{2,1,0:T(8,128)(2,1)S(1)}, u32[]{:S(2)}, u32[]{:S(2)}) collective-permute-start(bf16[2,32,512]{2,1,0:T(8,128)(2,1)S(1)} %maximum_select_fusion.4), channel_id=1, source_target_pairs={{0,8},{1,9},{2,10},{3,11},{4,12},{5,13},{6,14},{7,15},{8,0},{9,1},... | collective-permute-start | bytes 196616 | tf_op jit(solution)/shard_map/ppermute | solution.py:138
  39.1 6.0 %collective-permute-start.2 = (bf16[4,32,512]{2,1,0:T(8,128)(2,1)S(1)}, bf16[4,32,512]{2,1,0:T(8,128)(2,1)S(1)}, u32[]{:S(2)}, u32[]{:S(2)}) collective-permute-start(bf16[4,32,512]{2,1,0:T(8,128)(2,1)S(1)} %maximum_select_fusion.3), channel_id=1, source_target_pairs={{0,4},{1,5},{2,6},{3,7},{4,0},{5,1},{6,2},{7,3},{8,12},{9,13},{10,... | collective-permute-start | bytes 393224 | tf_op jit(solution)/shard_map/ppermute | solution.py:138
  45.1 13.0 %collective-permute-start.3 = (bf16[8,32,512]{2,1,0:T(8,128)(2,1)S(1)}, bf16[8,32,512]{2,1,0:T(8,128)(2,1)S(1)}, u32[]{:S(2)}, u32[]{:S(2)}) collective-permute-start(bf16[8,32,512]{2,1,0:T(8,128)(2,1)S(1)} %maximum_select_fusion.2), channel_id=1, source_target_pairs={{0,2},{1,3},{2,0},{3,1},{4,6},{5,7},{6,4},{7,5},{8,10},{9,11},{10,... | collective-permute-start | bytes 786440 | tf_op jit(solution)/shard_map/ppermute | solution.py:138
  53.0 31.3 %all-to-all-start.2 = ((bf16[1,32,32,512]{3,2,0,1:T(8,128)(2,1)}), bf16[1,32,32,512]{3,2,0,1:T(8,128)(2,1)S(1)}, u32[]{:S(2)}, u32[]{:S(2)}) async-start(bf16[1,32,32,512]{3,2,0,1:T(8,128)(2,1)} %broadcast_multiply_fusion), calls=%async_computation.2 | async-start | bytes 2097152 | tf_op jit(solution)/shard_map/all_to_all | solution.py:225
  58.2 2.0 %collective-permute-start.4 = (bf16[16,32,512]{2,1,0:T(8,128)(2,1)S(1)}, bf16[16,32,512]{2,1,0:T(8,128)(2,1)S(1)}, u32[]{:S(2)}, u32[]{:S(2)}) collective-permute-start(bf16[16,32,512]{2,1,0:T(8,128)(2,1)S(1)} %maximum_select_fusion.1), channel_id=1, source_target_pairs={{0,1},{1,0},{2,3},{3,2},{4,5},{5,4},{6,7},{7,6},{8,9},{9,8},{10,11... | collective-permute-start | bytes 1572872 | tf_op jit(solution)/shard_map/ppermute | solution.py:138

commit v15 on v14

--- a/solution.py
+++ b/solution.py
@@ -95,10 +95,9 @@
 
     def body(d, carry):
         for s in range(cap):
-            k = d * cap + s
-            t = req_ref[3 * k]
-            r = req_ref[3 * k + 1]
-            c = req_ref[3 * k + 2]
+            t = req_ref[d, s, 0]
+            r = req_ref[d, s, 1]
+            c = req_ref[d, s, 2]
             r0 = pl.multiple_of(jnp.minimum((r // 16) * 16, rows - span), 16)
             c0 = pl.multiple_of(jnp.minimum((c // 128) * 128, width - WIN), 128)
             win = tiles_ref[t, pl.ds(r0, span), pl.ds(c0, WIN)].astype(jnp.float32)
@@ -112,7 +111,6 @@
 
 
 def cut_patches(tiles, req, ends, cap):
-    flat = req.reshape(-1)
     return pl.pallas_call(
         functools.partial(cut_kernel, cap),
         out_shape=jax.ShapeDtypeStruct((ends, BOX, cap * BOX), tiles.dtype),
@@ -127,7 +125,7 @@
             transcendentals=0,
             bytes_accessed=tiles.size * 2 + ends * cap * BOX * BOX * 2,
         ),
-    )(flat, tiles)
+    )(req, tiles)
 
 
 def double_gather(block, ndev):
@@ -163,7 +161,7 @@
     )
     wanted = jnp.sum(jnp.where(spot[..., None], values[None, None], 0), axis=2)
     asked = lax.all_to_all(wanted, "dev", split_axis=0, concat_axis=0, tiled=True)
-    patches_cut = cut_patches(tiles, asked.reshape(ndev * cap, 3), ndev, cap)
+    patches_cut = cut_patches(tiles, asked, ndev, cap)
     xs_np, zs_np = touched_points()
     xs, zs, patches_cut = lax.optimization_barrier(
         (jnp.asarray(xs_np), jnp.asarray(zs_np), patches_cut)

time: 85.6 us -> 86.1 us (level)
    unnamed x6 -> x8, local copies, waits for them, and re-layouts: 1.58 us -> 2.2 us
  transfers between devices with their start and end apart: 8 -> 8, of which waited for: 5 -> 5; matrix products, arithmetic and copies ran while one was open for 21% -> 20% of each run, Pallas kernels for 9% -> 10%
where the time goes in v15:
time: 86.1 us; the launch traced here: 85.4 us
  waiting for transfers between devices  30.1 us (35%)
  starting transfers between devices  23 us (27%)
  other arithmetic  9.57 us (11%)
  Pallas kernels  8.13 us (9%)
  local copies, waits for them, and re-layouts  6.25 us (7%)
  matrix products  5.21 us (6%)
  between operations  3.09 us (4%)
    all_to_all x1, waiting for transfers between devices, per_device(): lax.all_to_all(placed, 'dev', split_axis=1, concat_axis=0, tiled=True)  20.3 us
    ppermute x5, waiting for transfers between devices, double_gather(): lax.ppermute(block, 'dev', perm=[(i, i ^ step) for i in range(ndev)])  8.65 us
    pallas_call x1, Pallas kernels, cut_patches(): pl.pallas_call(functools.partial(cut_kernel, cap), out_shape=jax.ShapeDty...  8.13 us
    ppermute x5, starting transfers between devices, double_gather(): lax.ppermute(block, 'dev', perm=[(i, i ^ step) for i in range(ndev)])  8.1 us
    all_to_all x1, starting transfers between devices, per_device(): lax.all_to_all(wanted, 'dev', split_axis=0, concat_axis=0, tiled=True)  7.3 us
    all_to_all x1, starting transfers between devices, per_device(): lax.all_to_all(placed, 'dev', split_axis=1, concat_axis=0, tiled=True)  5.05 us
    convert_element_type x1, other arithmetic, back_points(): return weight.reshape(count * BOX, xs.shape[0]).astype(jnp.bfloat16)  4.48 us
    dot_general x1, matrix products, per_device(): cyl = jnp.dot(volume, sample, preferred_element_type=jnp.float32)  4.17 us
  transfers between devices with their start and end apart: 8, of which 5 were waited for; matrix products, arithmetic and copies ran while one was open for 20% of the time, Pallas kernels for 10%

profile of v15, /device:TPU:0, one launch (start us, length us, event | category | flops | bytes accessed | tf_op | source)
XLA Modules:
  0.0 85.4 jit_solution(4645224472106794389)
XLA Ops:
  0.6 0.0 copy-start.1
  0.6 0.0 copy-start.2
  0.7 0.7 copy.54
  1.4 0.1 fusion.14
  1.5 0.2 select_reduce_fusion.1
  1.7 0.1 iota_compare_fusion.2
  1.8 0.1 iota_compare_fusion.3
  1.9 0.1 copy.42
  2.0 0.1 broadcast_and_fusion
  2.1 0.1 select_reduce_fusion
  2.2 0.7 copy.43
  2.9 7.3 %all-to-all-start = ((s32[32,2,3]{2,1,0:T(2,128)}), s32[32,2,3]{2,1,0:T(2,128)S(1)}, u32[]{:S(2)}, u32[]{:S(2)}) async-start(s32[32,2,3]{2,1,0:T(2,128)} %copy.43), calls=%async_computation | async-start | bytes 65536 | tf_op jit(solution)/shard_map/all_to_all | solution.py:163
  10.2 0.9 %copy.35 = bf16[32,512]{0,1:T(8,128)(2,1)S(1)} copy(bf16[32,512]{1,0:T(8,128)(2,1)} %param.11) | data formatting | bytes 65536 | tf_op args[4]
  11.1 0.2 copy.36
  11.3 2.7 %collective-permute-start = (bf16[1,32,512]{1,2,0:T(8,128)(2,1)S(1)}, bf16[1,32,512]{1,2,0:T(8,128)(2,1)S(1)}, u32[]{:S(2)}, u32[]{:S(2)}) collective-permute-start(bf16[1,32,512]{1,2,0:T(8,128)(2,1)S(1)} %bitcast.84), channel_id=1, source_target_pairs={{0,16},{1,17},{2,18},{3,19},{4,20},{5,21},{6,22},{7,23},{8,24},{9,... | collective-permute-start | bytes 98312 | tf_op jit(solution)/shard_map/ppermute | solution.py:136
  14.3 0.1 mul.204
  14.4 0.1 mul.207
  14.4 0.1 mul.208
  14.5 0.1 mul.210
  14.6 0.1 mul.211
  15.4 0.1 copy.37
  16.2 0.1 mul.218
  16.2 0.1 mul.219
  16.4 1.2 %all-to-all-done.req_ref = s32[32,2,3]{2,1,0:T(2,128)S(1)} async-done(((s32[32,2,3]{2,1,0:T(2,128)}), s32[32,2,3]{2,1,0:T(2,128)S(1)}, u32[]{:S(2)}, u32[]{:S(2)}) %all-to-all-start) | async-done | bytes 800 | tf_op jit(solution)/shard_map/all_to_all | solution.py:163
  17.5 0.6 copy-done
  18.1 8.1 %shard_map.86 = bf16[32,64,128]{2,1,0:T(8,128)(2,1)} custom-call(s32[32,2,3]{2,1,0:T(2,128)} %copy-done, bf16[2,128,4096]{2,1,0:T(8,128)(2,1)} %tiles_ref.1), custom_call_target="tpu_custom_call" | custom-call | flops 67108864 | bytes 2621440 | tf_op jit(solution)/shard_map/pallas_call | solution.py:114
  26.3 2.6 %all-to-all-start.1 = ((bf16[32,64,128]{2,1,0:T(8,128)(2,1)}), bf16[32,64,128]{2,1,0:T(8,128)(2,1)S(1)}, u32[]{:S(2)}, u32[]{:S(2)}) async-start(bf16[32,64,128]{2,1,0:T(8,128)(2,1)} %shard_map.86), calls=%async_computation.1 | async-start | bytes 1048576 | tf_op jit(solution)/shard_map/all_to_all | solution.py:169
  28.9 0.1 add_add_fusion
  29.0 0.0 collective-permute-done
  29.0 0.1 copy.38
  29.1 1.8 %collective-permute-start.1 = (bf16[2,32,512]{2,1,0:T(8,128)(2,1)S(1)}, bf16[2,32,512]{2,1,0:T(8,128)(2,1)S(1)}, u32[]{:S(2)}, u32[]{:S(2)}) collective-permute-start(bf16[2,32,512]{2,1,0:T(8,128)(2,1)S(1)} %maximum_select_fusion.4), channel_id=1, source_target_pairs={{0,8},{1,9},{2,10},{3,11},{4,12},{5,13},{6,14},{7,15},{8,0},{9,1},... | collective-permute-start | bytes 196616 | tf_op jit(solution)/shard_map/ppermute | solution.py:136
  30.9 4.5 %multiply_convert_fusion = bf16[22,64,1664]{2,1,0:T(8,128)(2,1)} fusion(f32[22,1664]{1,0:T(8,128)S(1)} %add_add_fusion, pred[22]{0:T(512)(128)(4,1)S(1)} %iota_compare_fusion.5), kind=kLoop, calls=%fused_computation.1 | loop fusion | flops 16400384 | bytes 4832278 | tf_op jit(solution)/shard_map/convert_element_type | solution.py:72
  35.4 4.0 %collective-permute-done.1 = bf16[2,32,512]{2,1,0:T(8,128)(2,1)S(1)} collective-permute-done((bf16[2,32,512]{2,1,0:T(8,128)(2,1)S(1)}, bf16[2,32,512]{2,1,0:T(8,128)(2,1)S(1)}, u32[]{:S(2)}, u32[]{:S(2)}) %collective-permute-start.1) | collective-permute-done | bytes 65568 | tf_op jit(solution)/shard_map/ppermute | solution.py:136
  39.4 1.7 %collective-permute-start.2 = (bf16[4,32,512]{2,1,0:T(8,128)(2,1)S(1)}, bf16[4,32,512]{2,1,0:T(8,128)(2,1)S(1)}, u32[]{:S(2)}, u32[]{:S(2)}) collective-permute-start(bf16[4,32,512]{2,1,0:T(8,128)(2,1)S(1)} %maximum_select_fusion.3), channel_id=1, source_target_pairs={{0,4},{1,5},{2,6},{3,7},{4,0},{5,1},{6,2},{7,3},{8,12},{9,13},{10,... | collective-permute-start | bytes 393224 | tf_op jit(solution)/shard_map/ppermute | solution.py:136
  41.2 1.2 %multiply_convert_fusion.1 = bf16[1664,512]{1,0:T(8,128)(2,1)S(1)} fusion(f32[512]{0:T(512)S(1)} %get-tuple-element.11, f32[1664]{0:T(1024)S(1)} %get-tuple-element.16, f32[512]{0:T(512)S(1)} %get-tuple-element.10, f32[1664]{0:T(1024)S(1)} %get-tuple-element.17), kind=kLoop, calls=%fused_computation.2 | loop fusion | flops 8519680 | bytes 1721344 | tf_op jit(solution)/shard_map/convert_element_type | solution.py:81
  42.4 3.0 %collective-permute-done.2 = bf16[4,32,512]{2,1,0:T(8,128)(2,1)S(1)} collective-permute-done((bf16[4,32,512]{2,1,0:T(8,128)(2,1)S(1)}, bf16[4,32,512]{2,1,0:T(8,128)(2,1)S(1)}, u32[]{:S(2)}, u32[]{:S(2)}) %collective-permute-start.2) | collective-permute-done | bytes 131104 | tf_op jit(solution)/shard_map/ppermute | solution.py:136
  45.4 1.5 %collective-permute-start.3 = (bf16[8,32,512]{2,1,0:T(8,128)(2,1)S(1)}, bf16[8,32,512]{2,1,0:T(8,128)(2,1)S(1)}, u32[]{:S(2)}, u32[]{:S(2)}) collective-permute-start(bf16[8,32,512]{2,1,0:T(8,128)(2,1)S(1)} %maximum_select_fusion.2), channel_id=1, source_target_pairs={{0,2},{1,3},{2,0},{3,1},{4,6},{5,7},{6,4},{7,5},{8,10},{9,11},{10,... | collective-permute-start | bytes 786440 | tf_op jit(solution)/shard_map/ppermute | solution.py:136
  46.9 0.0 all-to-all-done.1
  46.9 0.6 gather_fusion
  47.6 0.2 fusion.6
  47.8 0.1 pad.4
  47.9 4.2 %multiply_reduce_fusion.1 = (f32[]{:T(128)}, bf16[64,512]{1,0:T(8,128)(2,1)S(1)}) fusion(bf16[1664,512]{1,0:T(8,128)(2,1)S(1)} %multiply_convert_fusion.1, bf16[1408,64]{1,0:T(8,128)(2,1)S(1)} %bitcast.79, bf16[1408,1664]{1,0:T(8,128)(2,1)} %bitcast.73), kind=kOutput, calls=%fused_computation.31 | convolution fusion | flops 409182208 | bytes 6635524 | tf_op jit(solution)/shard_map/dot_general | solution.py:183
  52.0 0.1 fusion.9
  52.2 0.1 mul.224
  52.3 1.1 %broadcast_multiply_fusion = bf16[1,32,32,512]{3,2,0,1:T(8,128)(2,1)} fusion(bf16[1,32,32,512]{3,2,0,1:T(8,128)(2,1)S(1)} %bitcast.76, bf16[32]{0:T(256)(128)(2,1)S(1)} %mul.219), kind=kLoop, calls=%fused_computation.17 | loop fusion | flops 524288 | bytes 2097216 | tf_op jit(solution)/shard_map/mul | solution.py:221
  53.4 5.0 %all-to-all-start.2 = ((bf16[1,32,32,512]{3,2,0,1:T(8,128)(2,1)}), bf16[1,32,32,512]{3,2,0,1:T(8,128)(2,1)S(1)}, u32[]{:S(2)}, u32[]{:S(2)}) async-start(bf16[1,32,32,512]{3,2,0,1:T(8,128)(2,1)} %broadcast_multiply_fusion), calls=%async_computation.2 | async-start | bytes 2097152 | tf_op jit(solution)/shard_map/all_to_all | solution.py:223
  58.5 0.0 collective-permute-done.3
  58.5 0.1 maximum_select_fusion.1
  58.6 0.3 collective-permute-start.4
  58.9 1.6 %collective-permute-done.4 = bf16[16,32,512]{2,1,0:T(8,128)(2,1)S(1)} collective-permute-done((bf16[16,32,512]{2,1,0:T(8,128)(2,1)S(1)}, bf16[16,32,512]{2,1,0:T(8,128)(2,1)S(1)}, u32[]{:S(2)}, u32[]{:S(2)}) %collective-permute-start.4) | collective-permute-done | bytes 524320 | tf_op jit(solution)/shard_map/ppermute | solution.py:136
  60.5 0.2 maximum_select_fusion
  60.7 0.1 copy.41
  60.8 0.3 multiply_reduce_fusion
  61.1 0.1 copy.44
  61.9 0.1 copy.49
  62.1 0.1 sqrt.12
  62.1 0.3 copy.45
  62.4 0.3 fusion.4
  62.7 0.3 fusion
  63.0 0.2 copy.48
  63.2 0.5 fusion.3
  63.7 0.7 reshape.494
  64.3 20.3 %all-to-all-done.2 = bf16[1,32,32,512]{3,2,0,1:T(8,128)(2,1)S(1)} async-done(((bf16[1,32,32,512]{3,2,0,1:T(8,128)(2,1)}), bf16[1,32,32,512]{3,2,0,1:T(8,128)(2,1)S(1)}, u32[]{:S(2)}, u32[]{:S(2)}) %all-to-all-start.2) | async-done | bytes 1048608 | tf_op jit(solution)/shard_map/all_to_all | solution.py:223
  84.7 0.8 convert_reduce_fusion
  (25 shorter events, 0.4 us)
Async XLA Ops:
  0.6 28.3 %copy-start.1 = (f32[1664]{0:T(1024)S(1)}, f32[1664]{0:T(1024)}, u32[]{:S(2)}) copy-start(f32[1664]{0:T(1024)} %constant.180.clone) | copy-start | bytes 19972
  0.6 28.3 %copy-start.2 = (f32[1664]{0:T(1024)S(1)}, f32[1664]{0:T(1024)}, u32[]{:S(2)}) copy-start(f32[1664]{0:T(1024)} %constant.181.clone) | copy-start | bytes 19972
  2.9 14.6 %all-to-all-start = ((s32[32,2,3]{2,1,0:T(2,128)}), s32[32,2,3]{2,1,0:T(2,128)S(1)}, u32[]{:S(2)}, u32[]{:S(2)}) async-start(s32[32,2,3]{2,1,0:T(2,128)} %copy.43), calls=%async_computation | async-start | bytes 65536 | tf_op jit(solution)/shard_map/all_to_all | solution.py:163
  11.3 17.7 %collective-permute-start = (bf16[1,32,512]{1,2,0:T(8,128)(2,1)S(1)}, bf16[1,32,512]{1,2,0:T(8,128)(2,1)S(1)}, u32[]{:S(2)}, u32[]{:S(2)}) collective-permute-start(bf16[1,32,512]{1,2,0:T(8,128)(2,1)S(1)} %bitcast.84), channel_id=1, source_target_pairs={{0,16},{1,17},{2,18},{3,19},{4,20},{5,21},{6,22},{7,23},{8,24},{9,... | collective-permute-start | bytes 98312 | tf_op jit(solution)/shard_map/ppermute | solution.py:136
  17.5 0.6 copy-start
  26.3 20.7 %all-to-all-start.1 = ((bf16[32,64,128]{2,1,0:T(8,128)(2,1)}), bf16[32,64,128]{2,1,0:T(8,128)(2,1)S(1)}, u32[]{:S(2)}, u32[]{:S(2)}) async-start(bf16[32,64,128]{2,1,0:T(8,128)(2,1)} %shard_map.86), calls=%async_computation.1 | async-start | bytes 1048576 | tf_op jit(solution)/shard_map/all_to_all | solution.py:169
  29.1 10.3 %collective-permute-start.1 = (bf16[2,32,512]{2,1,0:T(8,128)(2,1)S(1)}, bf16[2,32,512]{2,1,0:T(8,128)(2,1)S(1)}, u32[]{:S(2)}, u32[]{:S(2)}) collective-permute-start(bf16[2,32,512]{2,1,0:T(8,128)(2,1)S(1)} %maximum_select_fusion.4), channel_id=1, source_target_pairs={{0,8},{1,9},{2,10},{3,11},{4,12},{5,13},{6,14},{7,15},{8,0},{9,1},... | collective-permute-start | bytes 196616 | tf_op jit(solution)/shard_map/ppermute | solution.py:136
  39.4 6.0 %collective-permute-start.2 = (bf16[4,32,512]{2,1,0:T(8,128)(2,1)S(1)}, bf16[4,32,512]{2,1,0:T(8,128)(2,1)S(1)}, u32[]{:S(2)}, u32[]{:S(2)}) collective-permute-start(bf16[4,32,512]{2,1,0:T(8,128)(2,1)S(1)} %maximum_select_fusion.3), channel_id=1, source_target_pairs={{0,4},{1,5},{2,6},{3,7},{4,0},{5,1},{6,2},{7,3},{8,12},{9,13},{10,... | collective-permute-start | bytes 393224 | tf_op jit(solution)/shard_map/ppermute | solution.py:136
  45.4 13.0 %collective-permute-start.3 = (bf16[8,32,512]{2,1,0:T(8,128)(2,1)S(1)}, bf16[8,32,512]{2,1,0:T(8,128)(2,1)S(1)}, u32[]{:S(2)}, u32[]{:S(2)}) collective-permute-start(bf16[8,32,512]{2,1,0:T(8,128)(2,1)S(1)} %maximum_select_fusion.2), channel_id=1, source_target_pairs={{0,2},{1,3},{2,0},{3,1},{4,6},{5,7},{6,4},{7,5},{8,10},{9,11},{10,... | collective-permute-start | bytes 786440 | tf_op jit(solution)/shard_map/ppermute | solution.py:136
  53.4 31.3 %all-to-all-start.2 = ((bf16[1,32,32,512]{3,2,0,1:T(8,128)(2,1)}), bf16[1,32,32,512]{3,2,0,1:T(8,128)(2,1)S(1)}, u32[]{:S(2)}, u32[]{:S(2)}) async-start(bf16[1,32,32,512]{3,2,0,1:T(8,128)(2,1)} %broadcast_multiply_fusion), calls=%async_computation.2 | async-start | bytes 2097152 | tf_op jit(solution)/shard_map/all_to_all | solution.py:223
  58.6 2.0 %collective-permute-start.4 = (bf16[16,32,512]{2,1,0:T(8,128)(2,1)S(1)}, bf16[16,32,512]{2,1,0:T(8,128)(2,1)S(1)}, u32[]{:S(2)}, u32[]{:S(2)}) collective-permute-start(bf16[16,32,512]{2,1,0:T(8,128)(2,1)S(1)} %maximum_select_fusion.1), channel_id=1, source_target_pairs={{0,1},{1,0},{2,3},{3,2},{4,5},{5,4},{6,7},{7,6},{8,9},{9,8},{10,11... | collective-permute-start | bytes 1572872 | tf_op jit(solution)/shard_map/ppermute | solution.py:136

commit v16 on v14

--- a/solution.py
+++ b/solution.py
@@ -91,7 +91,7 @@
     ends = out_ref.shape[0]
     width = tiles_ref.shape[2]
     rows = tiles_ref.shape[1]
-    span = BOX + 16
+    span = BOX + 8
 
     def body(d, carry):
         for s in range(cap):
@@ -99,7 +99,7 @@
             t = req_ref[3 * k]
             r = req_ref[3 * k + 1]
             c = req_ref[3 * k + 2]
-            r0 = pl.multiple_of(jnp.minimum((r // 16) * 16, rows - span), 16)
+            r0 = pl.multiple_of(jnp.minimum((r // 8) * 8, rows - span), 8)
             c0 = pl.multiple_of(jnp.minimum((c // 128) * 128, width - WIN), 128)
             win = tiles_ref[t, pl.ds(r0, span), pl.ds(c0, WIN)].astype(jnp.float32)
             win = pltpu.roll(win, (WIN - (c - c0)) % WIN, 1)[:, :128]

time: 85.6 us -> 85.6 us (level)
  no operation moved by 1% of the time
where the time goes in v16:
time: 85.6 us; the launch traced here: 85.1 us
  waiting for transfers between devices  30.1 us (35%)
  starting transfers between devices  23 us (27%)
  other arithmetic  9.58 us (11%)
  Pallas kernels  7.64 us (9%)
  local copies, waits for them, and re-layouts  6.35 us (7%)
  matrix products  5.21 us (6%)
  between operations  3.09 us (4%)
    all_to_all x1, waiting for transfers between devices, per_device(): lax.all_to_all(placed, 'dev', split_axis=1, concat_axis=0, tiled=True)  20.3 us
    ppermute x5, waiting for transfers between devices, double_gather(): lax.ppermute(block, 'dev', perm=[(i, i ^ step) for i in range(ndev)])  8.65 us
    ppermute x5, starting transfers between devices, double_gather(): lax.ppermute(block, 'dev', perm=[(i, i ^ step) for i in range(ndev)])  8.1 us
    pallas_call x1, Pallas kernels, cut_patches(): pl.pallas_call(functools.partial(cut_kernel, cap), out_shape=jax.ShapeDty...  7.64 us
    all_to_all x1, starting transfers between devices, per_device(): lax.all_to_all(wanted, 'dev', split_axis=0, concat_axis=0, tiled=True)  7.3 us
    all_to_all x1, starting transfers between devices, per_device(): lax.all_to_all(placed, 'dev', split_axis=1, concat_axis=0, tiled=True)  5.04 us
    convert_element_type x1, other arithmetic, back_points(): return weight.reshape(count * BOX, xs.shape[0]).astype(jnp.bfloat16)  4.48 us
    dot_general x1, matrix products, per_device(): cyl = jnp.dot(volume, sample, preferred_element_type=jnp.float32)  4.17 us
  transfers between devices with their start and end apart: 8, of which 5 were waited for; matrix products, arithmetic and copies ran while one was open for 21% of the time, Pallas kernels for 9%

profile of v16, /device:TPU:0, one launch (start us, length us, event | category | flops | bytes accessed | tf_op | source)
XLA Modules:
  0.0 85.1 jit_solution(6690713384419624765)
XLA Ops:
  0.6 0.0 copy-start
  0.6 0.0 copy-start.1
  0.7 0.7 copy.85
  1.4 0.1 fusion.14
  1.5 0.2 select_reduce_fusion.1
  1.7 0.1 iota_compare_fusion.2
  1.8 0.1 iota_compare_fusion.3
  1.9 0.1 copy.73
  2.0 0.1 broadcast_and_fusion
  2.1 0.1 select_reduce_fusion
  2.2 0.7 copy.74
  2.9 7.3 %all-to-all-start = ((s32[32,2,3]{2,1,0:T(2,128)}), s32[32,2,3]{2,1,0:T(2,128)S(1)}, u32[]{:S(2)}, u32[]{:S(2)}) async-start(s32[32,2,3]{2,1,0:T(2,128)} %copy.74), calls=%async_computation | async-start | bytes 65536 | tf_op jit(solution)/shard_map/all_to_all | solution.py:165
  10.2 0.9 %copy.66 = bf16[32,512]{0,1:T(8,128)(2,1)S(1)} copy(bf16[32,512]{1,0:T(8,128)(2,1)} %param.11) | data formatting | bytes 65536 | tf_op args[4]
  11.1 0.2 copy.67
  11.3 2.7 %collective-permute-start = (bf16[1,32,512]{1,2,0:T(8,128)(2,1)S(1)}, bf16[1,32,512]{1,2,0:T(8,128)(2,1)S(1)}, u32[]{:S(2)}, u32[]{:S(2)}) collective-permute-start(bf16[1,32,512]{1,2,0:T(8,128)(2,1)S(1)} %bitcast.84), channel_id=1, source_target_pairs={{0,16},{1,17},{2,18},{3,19},{4,20},{5,21},{6,22},{7,23},{8,24},{9,... | collective-permute-start | bytes 98312 | tf_op jit(solution)/shard_map/ppermute | solution.py:138
  14.3 0.1 mul.204
  14.4 0.1 mul.207
  14.4 0.1 mul.208
  14.5 0.1 mul.210
  14.6 0.1 mul.211
  15.4 0.1 copy.68
  16.2 0.1 mul.218
  16.2 0.1 mul.219
  16.4 1.2 %all-to-all-done = s32[32,2,3]{2,1,0:T(2,128)S(1)} async-done(((s32[32,2,3]{2,1,0:T(2,128)}), s32[32,2,3]{2,1,0:T(2,128)S(1)}, u32[]{:S(2)}, u32[]{:S(2)}) %all-to-all-start) | async-done | bytes 800 | tf_op jit(solution)/shard_map/all_to_all | solution.py:165
  17.5 0.7 reshape_reshape.10.req_ref
  18.2 7.6 %shard_map.86 = bf16[32,64,128]{2,1,0:T(8,128)(2,1)} custom-call(s32[192]{0:T(256)} %reshape_reshape.10.req_ref, bf16[2,128,4096]{2,1,0:T(8,128)(2,1)} %tiles_ref.1), custom_call_target="tpu_custom_call" | custom-call | flops 67108864 | bytes 2621440 | tf_op jit(solution)/shard_map/pallas_call | solution.py:116
  25.9 2.6 %all-to-all-start.1 = ((bf16[32,64,128]{2,1,0:T(8,128)(2,1)}), bf16[32,64,128]{2,1,0:T(8,128)(2,1)S(1)}, u32[]{:S(2)}, u32[]{:S(2)}) async-start(bf16[32,64,128]{2,1,0:T(8,128)(2,1)} %shard_map.86), calls=%async_computation.1 | async-start | bytes 1048576 | tf_op jit(solution)/shard_map/all_to_all | solution.py:171
  28.5 0.1 add_add_fusion
  28.6 0.0 collective-permute-done
  28.6 0.1 copy.69
  28.7 1.8 %collective-permute-start.1 = (bf16[2,32,512]{2,1,0:T(8,128)(2,1)S(1)}, bf16[2,32,512]{2,1,0:T(8,128)(2,1)S(1)}, u32[]{:S(2)}, u32[]{:S(2)}) collective-permute-start(bf16[2,32,512]{2,1,0:T(8,128)(2,1)S(1)} %maximum_select_fusion.4), channel_id=1, source_target_pairs={{0,8},{1,9},{2,10},{3,11},{4,12},{5,13},{6,14},{7,15},{8,0},{9,1},... | collective-permute-start | bytes 196616 | tf_op jit(solution)/shard_map/ppermute | solution.py:138
  30.5 4.5 %multiply_convert_fusion = bf16[22,64,1664]{2,1,0:T(8,128)(2,1)} fusion(f32[22,1664]{1,0:T(8,128)S(1)} %add_add_fusion, pred[22]{0:T(512)(128)(4,1)S(1)} %iota_compare_fusion.5), kind=kLoop, calls=%fused_computation.1 | loop fusion | flops 16400384 | bytes 4832278 | tf_op jit(solution)/shard_map/convert_element_type | solution.py:72
  35.0 4.0 %collective-permute-done.1 = bf16[2,32,512]{2,1,0:T(8,128)(2,1)S(1)} collective-permute-done((bf16[2,32,512]{2,1,0:T(8,128)(2,1)S(1)}, bf16[2,32,512]{2,1,0:T(8,128)(2,1)S(1)}, u32[]{:S(2)}, u32[]{:S(2)}) %collective-permute-start.1) | collective-permute-done | bytes 65568 | tf_op jit(solution)/shard_map/ppermute | solution.py:138
  39.0 1.7 %collective-permute-start.2 = (bf16[4,32,512]{2,1,0:T(8,128)(2,1)S(1)}, bf16[4,32,512]{2,1,0:T(8,128)(2,1)S(1)}, u32[]{:S(2)}, u32[]{:S(2)}) collective-permute-start(bf16[4,32,512]{2,1,0:T(8,128)(2,1)S(1)} %maximum_select_fusion.3), channel_id=1, source_target_pairs={{0,4},{1,5},{2,6},{3,7},{4,0},{5,1},{6,2},{7,3},{8,12},{9,13},{10,... | collective-permute-start | bytes 393224 | tf_op jit(solution)/shard_map/ppermute | solution.py:138
  40.8 1.2 %multiply_convert_fusion.1 = bf16[1664,512]{1,0:T(8,128)(2,1)S(1)} fusion(f32[512]{0:T(512)S(1)} %get-tuple-element.11, f32[1664]{0:T(1024)S(1)} %get-tuple-element.16, f32[512]{0:T(512)S(1)} %get-tuple-element.10, f32[1664]{0:T(1024)S(1)} %get-tuple-element.17), kind=kLoop, calls=%fused_computation.2 | loop fusion | flops 8519680 | bytes 1721344 | tf_op jit(solution)/shard_map/convert_element_type | solution.py:81
  42.0 3.0 %collective-permute-done.2 = bf16[4,32,512]{2,1,0:T(8,128)(2,1)S(1)} collective-permute-done((bf16[4,32,512]{2,1,0:T(8,128)(2,1)S(1)}, bf16[4,32,512]{2,1,0:T(8,128)(2,1)S(1)}, u32[]{:S(2)}, u32[]{:S(2)}) %collective-permute-start.2) | collective-permute-done | bytes 131104 | tf_op jit(solution)/shard_map/ppermute | solution.py:138
  45.0 1.5 %collective-permute-start.3 = (bf16[8,32,512]{2,1,0:T(8,128)(2,1)S(1)}, bf16[8,32,512]{2,1,0:T(8,128)(2,1)S(1)}, u32[]{:S(2)}, u32[]{:S(2)}) collective-permute-start(bf16[8,32,512]{2,1,0:T(8,128)(2,1)S(1)} %maximum_select_fusion.2), channel_id=1, source_target_pairs={{0,2},{1,3},{2,0},{3,1},{4,6},{5,7},{6,4},{7,5},{8,10},{9,11},{10,... | collective-permute-start | bytes 786440 | tf_op jit(solution)/shard_map/ppermute | solution.py:138
  46.5 0.0 all-to-all-done.1
  46.5 0.6 gather_fusion
  47.2 0.2 fusion.6
  47.4 0.1 pad.4
  47.5 4.2 %multiply_reduce_fusion.1 = (f32[]{:T(128)}, bf16[64,512]{1,0:T(8,128)(2,1)S(1)}) fusion(bf16[1664,512]{1,0:T(8,128)(2,1)S(1)} %multiply_convert_fusion.1, bf16[1408,64]{1,0:T(8,128)(2,1)S(1)} %bitcast.79, bf16[1408,1664]{1,0:T(8,128)(2,1)} %bitcast.73), kind=kOutput, calls=%fused_computation.31 | convolution fusion | flops 409182208 | bytes 6635524 | tf_op jit(solution)/shard_map/dot_general | solution.py:185
  51.6 0.1 fusion.9
  51.8 0.1 mul.224
  51.9 1.1 %broadcast_multiply_fusion = bf16[1,32,32,512]{3,2,0,1:T(8,128)(2,1)} fusion(bf16[1,32,32,512]{3,2,0,1:T(8,128)(2,1)S(1)} %bitcast.76, bf16[32]{0:T(256)(128)(2,1)S(1)} %mul.219), kind=kLoop, calls=%fused_computation.17 | loop fusion | flops 524288 | bytes 2097216 | tf_op jit(solution)/shard_map/mul | solution.py:223
  53.0 5.0 %all-to-all-start.2 = ((bf16[1,32,32,512]{3,2,0,1:T(8,128)(2,1)}), bf16[1,32,32,512]{3,2,0,1:T(8,128)(2,1)S(1)}, u32[]{:S(2)}, u32[]{:S(2)}) async-start(bf16[1,32,32,512]{3,2,0,1:T(8,128)(2,1)} %broadcast_multiply_fusion), calls=%async_computation.2 | async-start | bytes 2097152 | tf_op jit(solution)/shard_map/all_to_all | solution.py:225
  58.1 0.0 collective-permute-done.3
  58.1 0.1 maximum_select_fusion.1
  58.2 0.3 collective-permute-start.4
  58.5 1.6 %collective-permute-done.4 = bf16[16,32,512]{2,1,0:T(8,128)(2,1)S(1)} collective-permute-done((bf16[16,32,512]{2,1,0:T(8,128)(2,1)S(1)}, bf16[16,32,512]{2,1,0:T(8,128)(2,1)S(1)}, u32[]{:S(2)}, u32[]{:S(2)}) %collective-permute-start.4) | collective-permute-done | bytes 524320 | tf_op jit(solution)/shard_map/ppermute | solution.py:138
  60.1 0.2 maximum_select_fusion
  60.3 0.1 copy.72
  60.4 0.3 multiply_reduce_fusion
  60.7 0.1 copy.75
  61.5 0.1 copy.80
  61.7 0.1 sqrt.12
  61.7 0.3 copy.76
  62.0 0.3 fusion.4
  62.3 0.3 fusion
  62.6 0.2 copy.79
  62.8 0.5 fusion.3
  63.3 0.7 reshape.494
  63.9 20.3 %all-to-all-done.2 = bf16[1,32,32,512]{3,2,0,1:T(8,128)(2,1)S(1)} async-done(((bf16[1,32,32,512]{3,2,0,1:T(8,128)(2,1)}), bf16[1,32,32,512]{3,2,0,1:T(8,128)(2,1)S(1)}, u32[]{:S(2)}, u32[]{:S(2)}) %all-to-all-start.2) | async-done | bytes 1048608 | tf_op jit(solution)/shard_map/all_to_all | solution.py:225
  84.3 0.8 convert_reduce_fusion
  (24 shorter events, 0.4 us)
Async XLA Ops:
  0.6 27.9 %copy-start = (f32[1664]{0:T(1024)S(1)}, f32[1664]{0:T(1024)}, u32[]{:S(2)}) copy-start(f32[1664]{0:T(1024)} %constant.180.clone) | copy-start | bytes 19972
  0.6 27.9 %copy-start.1 = (f32[1664]{0:T(1024)S(1)}, f32[1664]{0:T(1024)}, u32[]{:S(2)}) copy-start(f32[1664]{0:T(1024)} %constant.181.clone) | copy-start | bytes 19972
  2.9 14.6 %all-to-all-start = ((s32[32,2,3]{2,1,0:T(2,128)}), s32[32,2,3]{2,1,0:T(2,128)S(1)}, u32[]{:S(2)}, u32[]{:S(2)}) async-start(s32[32,2,3]{2,1,0:T(2,128)} %copy.74), calls=%async_computation | async-start | bytes 65536 | tf_op jit(solution)/shard_map/all_to_all | solution.py:165
  11.3 17.3 %collective-permute-start = (bf16[1,32,512]{1,2,0:T(8,128)(2,1)S(1)}, bf16[1,32,512]{1,2,0:T(8,128)(2,1)S(1)}, u32[]{:S(2)}, u32[]{:S(2)}) collective-permute-start(bf16[1,32,512]{1,2,0:T(8,128)(2,1)S(1)} %bitcast.84), channel_id=1, source_target_pairs={{0,16},{1,17},{2,18},{3,19},{4,20},{5,21},{6,22},{7,23},{8,24},{9,... | collective-permute-start | bytes 98312 | tf_op jit(solution)/shard_map/ppermute | solution.py:138
  25.9 20.7 %all-to-all-start.1 = ((bf16[32,64,128]{2,1,0:T(8,128)(2,1)}), bf16[32,64,128]{2,1,0:T(8,128)(2,1)S(1)}, u32[]{:S(2)}, u32[]{:S(2)}) async-start(bf16[32,64,128]{2,1,0:T(8,128)(2,1)} %shard_map.86), calls=%async_computation.1 | async-start | bytes 1048576 | tf_op jit(solution)/shard_map/all_to_all | solution.py:171
  28.7 10.3 %collective-permute-start.1 = (bf16[2,32,512]{2,1,0:T(8,128)(2,1)S(1)}, bf16[2,32,512]{2,1,0:T(8,128)(2,1)S(1)}, u32[]{:S(2)}, u32[]{:S(2)}) collective-permute-start(bf16[2,32,512]{2,1,0:T(8,128)(2,1)S(1)} %maximum_select_fusion.4), channel_id=1, source_target_pairs={{0,8},{1,9},{2,10},{3,11},{4,12},{5,13},{6,14},{7,15},{8,0},{9,1},... | collective-permute-start | bytes 196616 | tf_op jit(solution)/shard_map/ppermute | solution.py:138
  39.0 6.0 %collective-permute-start.2 = (bf16[4,32,512]{2,1,0:T(8,128)(2,1)S(1)}, bf16[4,32,512]{2,1,0:T(8,128)(2,1)S(1)}, u32[]{:S(2)}, u32[]{:S(2)}) collective-permute-start(bf16[4,32,512]{2,1,0:T(8,128)(2,1)S(1)} %maximum_select_fusion.3), channel_id=1, source_target_pairs={{0,4},{1,5},{2,6},{3,7},{4,0},{5,1},{6,2},{7,3},{8,12},{9,13},{10,... | collective-permute-start | bytes 393224 | tf_op jit(solution)/shard_map/ppermute | solution.py:138
  45.0 13.0 %collective-permute-start.3 = (bf16[8,32,512]{2,1,0:T(8,128)(2,1)S(1)}, bf16[8,32,512]{2,1,0:T(8,128)(2,1)S(1)}, u32[]{:S(2)}, u32[]{:S(2)}) collective-permute-start(bf16[8,32,512]{2,1,0:T(8,128)(2,1)S(1)} %maximum_select_fusion.2), channel_id=1, source_target_pairs={{0,2},{1,3},{2,0},{3,1},{4,6},{5,7},{6,4},{7,5},{8,10},{9,11},{10,... | collective-permute-start | bytes 786440 | tf_op jit(solution)/shard_map/ppermute | solution.py:138
  53.0 31.3 %all-to-all-start.2 = ((bf16[1,32,32,512]{3,2,0,1:T(8,128)(2,1)}), bf16[1,32,32,512]{3,2,0,1:T(8,128)(2,1)S(1)}, u32[]{:S(2)}, u32[]{:S(2)}) async-start(bf16[1,32,32,512]{3,2,0,1:T(8,128)(2,1)} %broadcast_multiply_fusion), calls=%async_computation.2 | async-start | bytes 2097152 | tf_op jit(solution)/shard_map/all_to_all | solution.py:225
  58.2 2.0 %collective-permute-start.4 = (bf16[16,32,512]{2,1,0:T(8,128)(2,1)S(1)}, bf16[16,32,512]{2,1,0:T(8,128)(2,1)S(1)}, u32[]{:S(2)}, u32[]{:S(2)}) collective-permute-start(bf16[16,32,512]{2,1,0:T(8,128)(2,1)S(1)} %maximum_select_fusion.1), channel_id=1, source_target_pairs={{0,1},{1,0},{2,3},{3,2},{4,5},{5,4},{6,7},{7,6},{8,9},{9,8},{10,11... | collective-permute-start | bytes 1572872 | tf_op jit(solution)/shard_map/ppermute | solution.py:138

commit v17 on v16

--- a/solution.py
+++ b/solution.py
@@ -185,6 +185,18 @@
     cyl = jnp.dot(volume, sample, preferred_element_type=jnp.float32)
     cyl = cyl.astype(jnp.bfloat16).reshape(count, BOX, ROTS * CYCLES)
     owned = references.shape[0]
+    doubled = jnp.concatenate([cyl, cyl], axis=2)
+    turned = jnp.stack(
+        [
+            lax.dynamic_slice_in_dim(doubled[p], rotations[p] * CYCLES, ROTS * CYCLES, axis=1)
+            for p in range(count)
+        ]
+    )
+    member = (classes[:, None] == jnp.arange(CLASSES, dtype=jnp.int32)[None, :]).astype(
+        jnp.bfloat16
+    )
+    placed = member[:, :, None, None] * turned[:, None, :, :]
+    placed = placed.reshape(count, ndev, owned, ROTS * CYCLES)
     parts = BOX // owned
     local_t = references.reshape(owned, ROTS, CYCLES).transpose(1, 0, 2).reshape(ROTS, owned * CYCLES)
     gathered = double_gather(local_t[None], ndev)
@@ -203,25 +215,14 @@
         for q in range(parts)
     )
     raw = jnp.einsum("pfgc,kfg->pck", corr, shift_table(), precision=lax.Precision.HIGHEST)
-    cyl_float = cyl.astype(jnp.float32)
+    cyl_late, _ = lax.optimization_barrier((cyl, placed))
+    cyl_float = cyl_late.astype(jnp.float32)
     power = jnp.mean(cyl_float.reshape(count, -1) ** 2, axis=1)
     total = BOX * ROTS * CYCLES
     scores = raw / jnp.sqrt(
         total * (power[:, None, None] + 1e-06) * (ref_power[None, :, None] + 1e-06)
     )
     scores = scores.reshape(count, CLASSES * ROTS)
-    doubled = jnp.concatenate([cyl, cyl], axis=2)
-    turned = jnp.stack(
-        [
-            lax.dynamic_slice_in_dim(doubled[p], rotations[p] * CYCLES, ROTS * CYCLES, axis=1)
-            for p in range(count)
-        ]
-    )
-    member = (classes[:, None] == jnp.arange(CLASSES, dtype=jnp.int32)[None, :]).astype(
-        jnp.bfloat16
-    )
-    placed = member[:, :, None, None] * turned[:, None, :, :]
-    placed = placed.reshape(count, ndev, owned, ROTS * CYCLES)
     landed = lax.all_to_all(placed, "dev", split_axis=1, concat_axis=0, tiled=True)
     class_sums = jnp.sum(landed.astype(jnp.float32), axis=(0, 1))
     return (scores, class_sums)

time: 85.6 us -> 85 us (level)
  no operation moved by 1% of the time
where the time goes in v17:
time: 85 us; the launch traced here: 84.5 us
  waiting for transfers between devices  29.5 us (35%)
  starting transfers between devices  23.1 us (27%)
  other arithmetic  10.2 us (12%)
  Pallas kernels  7.64 us (9%)
  local copies, waits for them, and re-layouts  6.35 us (7%)
  matrix products  4.58 us (5%)
  between operations  3.09 us (4%)
    all_to_all x1, waiting for transfers between devices, per_device(): lax.all_to_all(placed, 'dev', split_axis=1, concat_axis=0, tiled=True)  19.7 us
    ppermute x5, waiting for transfers between devices, double_gather(): lax.ppermute(block, 'dev', perm=[(i, i ^ step) for i in range(ndev)])  8.66 us
    ppermute x5, starting transfers between devices, double_gather(): lax.ppermute(block, 'dev', perm=[(i, i ^ step) for i in range(ndev)])  8.11 us
    pallas_call x1, Pallas kernels, cut_patches(): pl.pallas_call(functools.partial(cut_kernel, cap), out_shape=jax.ShapeDty...  7.64 us
    all_to_all x1, starting transfers between devices, per_device(): lax.all_to_all(wanted, 'dev', split_axis=0, concat_axis=0, tiled=True)  7.3 us
    all_to_all x1, starting transfers between devices, per_device(): lax.all_to_all(placed, 'dev', split_axis=1, concat_axis=0, tiled=True)  5.03 us
    convert_element_type x1, other arithmetic, back_points(): return weight.reshape(count * BOX, xs.shape[0]).astype(jnp.bfloat16)  4.47 us
    dot_general x1, matrix products, per_device(): cyl = jnp.dot(volume, sample, preferred_element_type=jnp.float32)  3.55 us
  transfers between devices with their start and end apart: 8, of which 5 were waited for; matrix products, arithmetic and copies ran while one was open for 21% of the time, Pallas kernels for 9%

profile of v17, /device:TPU:0, one launch (start us, length us, event | category | flops | bytes accessed | tf_op | source)
XLA Modules:
  0.0 84.5 jit_solution(15100938080921412004)
XLA Ops:
  0.6 0.0 copy-start
  0.6 0.0 copy-start.1
  0.7 0.7 copy.85
  1.4 0.1 fusion.14
  1.5 0.2 select_reduce_fusion.1
  1.7 0.1 iota_compare_fusion.2
  1.8 0.1 iota_compare_fusion.3
  1.9 0.1 copy.73
  2.0 0.1 broadcast_and_fusion
  2.1 0.1 select_reduce_fusion
  2.2 0.7 copy.74
  2.9 7.3 %all-to-all-start = ((s32[32,2,3]{2,1,0:T(2,128)}), s32[32,2,3]{2,1,0:T(2,128)S(1)}, u32[]{:S(2)}, u32[]{:S(2)}) async-start(s32[32,2,3]{2,1,0:T(2,128)} %copy.74), calls=%async_computation | async-start | bytes 65536 | tf_op jit(solution)/shard_map/all_to_all | solution.py:165
  10.2 0.9 %copy.66 = bf16[32,512]{0,1:T(8,128)(2,1)S(1)} copy(bf16[32,512]{1,0:T(8,128)(2,1)} %param.11) | data formatting | bytes 65536 | tf_op args[4]
  11.1 0.2 copy.67
  11.3 2.7 %collective-permute-start = (bf16[1,32,512]{1,2,0:T(8,128)(2,1)S(1)}, bf16[1,32,512]{1,2,0:T(8,128)(2,1)S(1)}, u32[]{:S(2)}, u32[]{:S(2)}) collective-permute-start(bf16[1,32,512]{1,2,0:T(8,128)(2,1)S(1)} %bitcast.85), channel_id=1, source_target_pairs={{0,16},{1,17},{2,18},{3,19},{4,20},{5,21},{6,22},{7,23},{8,24},{9,... | collective-permute-start | bytes 98312 | tf_op jit(solution)/shard_map/ppermute | solution.py:138
  14.3 0.1 mul.204
  14.4 0.1 mul.207
  14.5 0.1 mul.208
  14.6 0.1 mul.210
  14.6 0.1 mul.211
  15.4 0.1 copy.68
  16.2 0.1 mul.214
  16.2 0.1 mul.215
  16.4 1.1 %all-to-all-done = s32[32,2,3]{2,1,0:T(2,128)S(1)} async-done(((s32[32,2,3]{2,1,0:T(2,128)}), s32[32,2,3]{2,1,0:T(2,128)S(1)}, u32[]{:S(2)}, u32[]{:S(2)}) %all-to-all-start) | async-done | bytes 800 | tf_op jit(solution)/shard_map/all_to_all | solution.py:165
  17.5 0.7 reshape_reshape.10.req_ref
  18.2 7.6 %shard_map.86 = bf16[32,64,128]{2,1,0:T(8,128)(2,1)} custom-call(s32[192]{0:T(256)} %reshape_reshape.10.req_ref, bf16[2,128,4096]{2,1,0:T(8,128)(2,1)} %tiles_ref.1), custom_call_target="tpu_custom_call" | custom-call | flops 67108864 | bytes 2621440 | tf_op jit(solution)/shard_map/pallas_call | solution.py:116
  25.9 2.6 %all-to-all-start.1 = ((bf16[32,64,128]{2,1,0:T(8,128)(2,1)}), bf16[32,64,128]{2,1,0:T(8,128)(2,1)S(1)}, u32[]{:S(2)}, u32[]{:S(2)}) async-start(bf16[32,64,128]{2,1,0:T(8,128)(2,1)} %shard_map.86), calls=%async_computation.1 | async-start | bytes 1048576 | tf_op jit(solution)/shard_map/all_to_all | solution.py:171
  28.5 0.1 add_add_fusion
  28.6 0.0 collective-permute-done
  28.6 0.1 copy.69
  28.7 1.8 %collective-permute-start.1 = (bf16[2,32,512]{2,1,0:T(8,128)(2,1)S(1)}, bf16[2,32,512]{2,1,0:T(8,128)(2,1)S(1)}, u32[]{:S(2)}, u32[]{:S(2)}) collective-permute-start(bf16[2,32,512]{2,1,0:T(8,128)(2,1)S(1)} %maximum_select_fusion.4), channel_id=1, source_target_pairs={{0,8},{1,9},{2,10},{3,11},{4,12},{5,13},{6,14},{7,15},{8,0},{9,1},... | collective-permute-start | bytes 196616 | tf_op jit(solution)/shard_map/ppermute | solution.py:138
  30.6 4.5 %multiply_convert_fusion = bf16[22,64,1664]{2,1,0:T(8,128)(2,1)} fusion(f32[22,1664]{1,0:T(8,128)S(1)} %add_add_fusion, pred[22]{0:T(512)(128)(4,1)S(1)} %iota_compare_fusion.5), kind=kLoop, calls=%fused_computation.1 | loop fusion | flops 16400384 | bytes 4832278 | tf_op jit(solution)/shard_map/convert_element_type | solution.py:72
  35.0 4.0 %collective-permute-done.1 = bf16[2,32,512]{2,1,0:T(8,128)(2,1)S(1)} collective-permute-done((bf16[2,32,512]{2,1,0:T(8,128)(2,1)S(1)}, bf16[2,32,512]{2,1,0:T(8,128)(2,1)S(1)}, u32[]{:S(2)}, u32[]{:S(2)}) %collective-permute-start.1) | collective-permute-done | bytes 65568 | tf_op jit(solution)/shard_map/ppermute | solution.py:138
  39.1 1.7 %collective-permute-start.2 = (bf16[4,32,512]{2,1,0:T(8,128)(2,1)S(1)}, bf16[4,32,512]{2,1,0:T(8,128)(2,1)S(1)}, u32[]{:S(2)}, u32[]{:S(2)}) collective-permute-start(bf16[4,32,512]{2,1,0:T(8,128)(2,1)S(1)} %maximum_select_fusion.3), channel_id=1, source_target_pairs={{0,4},{1,5},{2,6},{3,7},{4,0},{5,1},{6,2},{7,3},{8,12},{9,13},{10,... | collective-permute-start | bytes 393224 | tf_op jit(solution)/shard_map/ppermute | solution.py:138
  40.8 1.2 %multiply_convert_fusion.1 = bf16[1664,512]{1,0:T(8,128)(2,1)S(1)} fusion(f32[512]{0:T(512)S(1)} %get-tuple-element.13, f32[1664]{0:T(1024)S(1)} %get-tuple-element.16, f32[512]{0:T(512)S(1)} %get-tuple-element.12, f32[1664]{0:T(1024)S(1)} %get-tuple-element.17), kind=kLoop, calls=%fused_computation.2 | loop fusion | flops 8519680 | bytes 1721344 | tf_op jit(solution)/shard_map/convert_element_type | solution.py:81
  42.1 3.0 %collective-permute-done.2 = bf16[4,32,512]{2,1,0:T(8,128)(2,1)S(1)} collective-permute-done((bf16[4,32,512]{2,1,0:T(8,128)(2,1)S(1)}, bf16[4,32,512]{2,1,0:T(8,128)(2,1)S(1)}, u32[]{:S(2)}, u32[]{:S(2)}) %collective-permute-start.2) | collective-permute-done | bytes 131104 | tf_op jit(solution)/shard_map/ppermute | solution.py:138
  45.1 1.5 %collective-permute-start.3 = (bf16[8,32,512]{2,1,0:T(8,128)(2,1)S(1)}, bf16[8,32,512]{2,1,0:T(8,128)(2,1)S(1)}, u32[]{:S(2)}, u32[]{:S(2)}) collective-permute-start(bf16[8,32,512]{2,1,0:T(8,128)(2,1)S(1)} %maximum_select_fusion.2), channel_id=1, source_target_pairs={{0,2},{1,3},{2,0},{3,1},{4,6},{5,7},{6,4},{7,5},{8,10},{9,11},{10,... | collective-permute-start | bytes 786440 | tf_op jit(solution)/shard_map/ppermute | solution.py:138
  46.6 0.0 all-to-all-done.1
  46.6 0.6 gather_fusion
  47.2 0.2 fusion.6
  47.4 0.1 pad.4
  47.5 3.5 %fusion.2 = bf16[64,512]{1,0:T(8,128)(2,1)S(1)} fusion(bf16[1664,512]{1,0:T(8,128)(2,1)S(1)} %multiply_convert_fusion.1, bf16[1408,64]{1,0:T(8,128)(2,1)S(1)} %bitcast.79, bf16[1408,1664]{1,0:T(8,128)(2,1)} %bitcast.73), kind=kOutput, calls=%fused_computation.9 | convolution fusion | flops 409083904 | bytes 6635520 | tf_op jit(solution)/shard_map/dot_general | solution.py:185
  51.0 0.1 fusion.9
  51.2 0.1 mul.220
  51.3 1.1 %broadcast_multiply_fusion = bf16[1,32,32,512]{3,2,0,1:T(8,128)(2,1)} fusion(bf16[1,32,32,512]{3,2,0,1:T(8,128)(2,1)S(1)} %bitcast.76, bf16[32]{0:T(256)(128)(2,1)S(1)} %mul.215), kind=kLoop, calls=%fused_computation.17 | loop fusion | flops 524288 | bytes 2097216 | tf_op jit(solution)/shard_map/mul | solution.py:198
  52.4 5.0 %all-to-all-start.2 = ((bf16[1,32,32,512]{3,2,0,1:T(8,128)(2,1)}), bf16[1,32,32,512]{3,2,0,1:T(8,128)(2,1)S(1)}, u32[]{:S(2)}, u32[]{:S(2)}) async-start(bf16[1,32,32,512]{3,2,0,1:T(8,128)(2,1)} %broadcast_multiply_fusion), calls=%async_computation.2 | async-start | bytes 2097152 | tf_op jit(solution)/shard_map/all_to_all | solution.py:226
  57.5 0.1 maximum_select_fusion.1
  57.6 0.3 collective-permute-start.4
  57.9 1.6 %collective-permute-done.4 = bf16[16,32,512]{2,1,0:T(8,128)(2,1)S(1)} collective-permute-done((bf16[16,32,512]{2,1,0:T(8,128)(2,1)S(1)}, bf16[16,32,512]{2,1,0:T(8,128)(2,1)S(1)}, u32[]{:S(2)}, u32[]{:S(2)}) %collective-permute-start.4) | collective-permute-done | bytes 524320 | tf_op jit(solution)/shard_map/ppermute | solution.py:138
  59.5 0.2 maximum_select_fusion
  59.7 0.1 copy.72
  59.8 0.3 multiply_reduce_fusion
  60.1 0.1 copy.75
  60.3 0.6 multiply_reduce_fusion.1
  61.6 0.1 copy.80
  61.7 0.1 sqrt.12
  61.8 0.3 copy.76
  62.1 0.3 fusion.4
  62.4 0.3 fusion
  62.6 0.2 copy.79
  62.8 0.5 fusion.3
  63.3 0.7 reshape.492
  63.9 19.7 %all-to-all-done.2 = bf16[1,32,32,512]{3,2,0,1:T(8,128)(2,1)S(1)} async-done(((bf16[1,32,32,512]{3,2,0,1:T(8,128)(2,1)}), bf16[1,32,32,512]{3,2,0,1:T(8,128)(2,1)S(1)}, u32[]{:S(2)}, u32[]{:S(2)}) %all-to-all-start.2) | async-done | bytes 1048608 | tf_op jit(solution)/shard_map/all_to_all | solution.py:226
  83.7 0.8 convert_reduce_fusion
  (25 shorter events, 0.4 us)
Async XLA Ops:
  0.6 27.9 %copy-start = (f32[1664]{0:T(1024)S(1)}, f32[1664]{0:T(1024)}, u32[]{:S(2)}) copy-start(f32[1664]{0:T(1024)} %constant.180.clone) | copy-start | bytes 19972
  0.6 27.9 %copy-start.1 = (f32[1664]{0:T(1024)S(1)}, f32[1664]{0:T(1024)}, u32[]{:S(2)}) copy-start(f32[1664]{0:T(1024)} %constant.181.clone) | copy-start | bytes 19972
  2.9 14.6 %all-to-all-start = ((s32[32,2,3]{2,1,0:T(2,128)}), s32[32,2,3]{2,1,0:T(2,128)S(1)}, u32[]{:S(2)}, u32[]{:S(2)}) async-start(s32[32,2,3]{2,1,0:T(2,128)} %copy.74), calls=%async_computation | async-start | bytes 65536 | tf_op jit(solution)/shard_map/all_to_all | solution.py:165
  11.3 17.3 %collective-permute-start = (bf16[1,32,512]{1,2,0:T(8,128)(2,1)S(1)}, bf16[1,32,512]{1,2,0:T(8,128)(2,1)S(1)}, u32[]{:S(2)}, u32[]{:S(2)}) collective-permute-start(bf16[1,32,512]{1,2,0:T(8,128)(2,1)S(1)} %bitcast.85), channel_id=1, source_target_pairs={{0,16},{1,17},{2,18},{3,19},{4,20},{5,21},{6,22},{7,23},{8,24},{9,... | collective-permute-start | bytes 98312 | tf_op jit(solution)/shard_map/ppermute | solution.py:138
  25.9 20.7 %all-to-all-start.1 = ((bf16[32,64,128]{2,1,0:T(8,128)(2,1)}), bf16[32,64,128]{2,1,0:T(8,128)(2,1)S(1)}, u32[]{:S(2)}, u32[]{:S(2)}) async-start(bf16[32,64,128]{2,1,0:T(8,128)(2,1)} %shard_map.86), calls=%async_computation.1 | async-start | bytes 1048576 | tf_op jit(solution)/shard_map/all_to_all | solution.py:171
  28.7 10.3 %collective-permute-start.1 = (bf16[2,32,512]{2,1,0:T(8,128)(2,1)S(1)}, bf16[2,32,512]{2,1,0:T(8,128)(2,1)S(1)}, u32[]{:S(2)}, u32[]{:S(2)}) collective-permute-start(bf16[2,32,512]{2,1,0:T(8,128)(2,1)S(1)} %maximum_select_fusion.4), channel_id=1, source_target_pairs={{0,8},{1,9},{2,10},{3,11},{4,12},{5,13},{6,14},{7,15},{8,0},{9,1},... | collective-permute-start | bytes 196616 | tf_op jit(solution)/shard_map/ppermute | solution.py:138
  39.1 6.0 %collective-permute-start.2 = (bf16[4,32,512]{2,1,0:T(8,128)(2,1)S(1)}, bf16[4,32,512]{2,1,0:T(8,128)(2,1)S(1)}, u32[]{:S(2)}, u32[]{:S(2)}) collective-permute-start(bf16[4,32,512]{2,1,0:T(8,128)(2,1)S(1)} %maximum_select_fusion.3), channel_id=1, source_target_pairs={{0,4},{1,5},{2,6},{3,7},{4,0},{5,1},{6,2},{7,3},{8,12},{9,13},{10,... | collective-permute-start | bytes 393224 | tf_op jit(solution)/shard_map/ppermute | solution.py:138
  45.1 12.4 %collective-permute-start.3 = (bf16[8,32,512]{2,1,0:T(8,128)(2,1)S(1)}, bf16[8,32,512]{2,1,0:T(8,128)(2,1)S(1)}, u32[]{:S(2)}, u32[]{:S(2)}) collective-permute-start(bf16[8,32,512]{2,1,0:T(8,128)(2,1)S(1)} %maximum_select_fusion.2), channel_id=1, source_target_pairs={{0,2},{1,3},{2,0},{3,1},{4,6},{5,7},{6,4},{7,5},{8,10},{9,11},{10,... | collective-permute-start | bytes 786440 | tf_op jit(solution)/shard_map/ppermute | solution.py:138
  52.4 31.3 %all-to-all-start.2 = ((bf16[1,32,32,512]{3,2,0,1:T(8,128)(2,1)}), bf16[1,32,32,512]{3,2,0,1:T(8,128)(2,1)S(1)}, u32[]{:S(2)}, u32[]{:S(2)}) async-start(bf16[1,32,32,512]{3,2,0,1:T(8,128)(2,1)} %broadcast_multiply_fusion), calls=%async_computation.2 | async-start | bytes 2097152 | tf_op jit(solution)/shard_map/all_to_all | solution.py:226
  57.6 2.0 %collective-permute-start.4 = (bf16[16,32,512]{2,1,0:T(8,128)(2,1)S(1)}, bf16[16,32,512]{2,1,0:T(8,128)(2,1)S(1)}, u32[]{:S(2)}, u32[]{:S(2)}) collective-permute-start(bf16[16,32,512]{2,1,0:T(8,128)(2,1)S(1)} %maximum_select_fusion.1), channel_id=1, source_target_pairs={{0,1},{1,0},{2,3},{3,2},{4,5},{5,4},{6,7},{7,6},{8,9},{9,8},{10,11... | collective-permute-start | bytes 1572872 | tf_op jit(solution)/shard_map/ppermute | solution.py:138

commit v18 on v17

--- a/solution.py
+++ b/solution.py
@@ -174,7 +174,7 @@
         jnp.where(slot[:, None, None] == s, rows_of[:, :, s * BOX : (s + 1) * BOX], 0)
         for s in range(cap)
     ).reshape(count, TILTS, BOX, BOX)
-    padded = TILTS + TILTS % 2
+    padded = TILTS
     flipped = jnp.pad(flipped, ((0, 0), (0, padded - TILTS), (0, 0), (0, 0)))
     flipped = flipped.reshape(count, padded * BOX, BOX)
     volume = jnp.einsum(

time: 85 us -> 83.7 us (0.985)
  other arithmetic: 10.2 us -> 5.55 us
  waiting for transfers between devices: 29.5 us -> 34.1 us
    ppermute x5, waiting for transfers between devices: 8.66 us -> 13.2 us  [double_gather(): lax.ppermute(block, 'dev', perm=[(i, i ^ step) for i in range(ndev)])]
    convert_element_type x1 -> x0, other arithmetic: 4.47 us -> none  [back_points(): return weight.reshape(count * BOX, xs.shape[0]).astype(jnp.bfloat16)]
    dot_general x1, matrix products: 3.55 us -> 2.69 us  [per_device(): cyl = jnp.dot(volume, sample, preferred_element_type=jnp.float32)]
  transfers between devices with their start and end apart: 8 -> 8, of which waited for: 5 -> 5; matrix products, arithmetic and copies ran while one was open for 21% -> 15% of each run, Pallas kernels for 9% -> 9%
where the time goes in v18:
time: 83.7 us; the launch traced here: 83.2 us
  waiting for transfers between devices  34.1 us (41%)
  starting transfers between devices  23 us (27%)
  Pallas kernels  7.61 us (9%)
  local copies, waits for them, and re-layouts  6.26 us (7%)
  other arithmetic  5.55 us (7%)
  matrix products  3.74 us (4%)
  between operations  2.94 us (4%)
    all_to_all x1, waiting for transfers between devices, per_device(): lax.all_to_all(placed, 'dev', split_axis=1, concat_axis=0, tiled=True)  19.7 us
    ppermute x5, waiting for transfers between devices, double_gather(): lax.ppermute(block, 'dev', perm=[(i, i ^ step) for i in range(ndev)])  13.2 us
    ppermute x5, starting transfers between devices, double_gather(): lax.ppermute(block, 'dev', perm=[(i, i ^ step) for i in range(ndev)])  8.02 us
    pallas_call x1, Pallas kernels, cut_patches(): pl.pallas_call(functools.partial(cut_kernel, cap), out_shape=jax.ShapeDty...  7.61 us
    all_to_all x1, starting transfers between devices, per_device(): lax.all_to_all(wanted, 'dev', split_axis=0, concat_axis=0, tiled=True)  7.3 us
    all_to_all x1, starting transfers between devices, per_device(): lax.all_to_all(placed, 'dev', split_axis=1, concat_axis=0, tiled=True)  5.08 us
    dot_general x1, matrix products, per_device(): cyl = jnp.dot(volume, sample, preferred_element_type=jnp.float32)  2.69 us
    all_to_all x1, starting transfers between devices, per_device(): lax.all_to_all(patches_cut, 'dev', split_axis=0, concat_axis=0, tiled=True)  2.6 us
  transfers between devices with their start and end apart: 8, of which 5 were waited for; matrix products, arithmetic and copies ran while one was open for 15% of the time, Pallas kernels for 9%

profile of v18, /device:TPU:0, one launch (start us, length us, event | category | flops | bytes accessed | tf_op | source)
XLA Modules:
  0.0 83.2 jit_solution(18153789587567141875)
XLA Ops:
  0.6 0.7 copy.90
  1.4 0.1 iota_compare_fusion.3
  1.4 0.1 copy.76
  1.5 0.1 fusion.23
  1.7 0.2 select_reduce_fusion.1
  1.8 0.1 iota_compare_fusion.2
  1.9 0.1 broadcast_and_fusion
  2.0 0.1 select_reduce_fusion
  2.2 0.7 copy.77
  2.9 7.3 %all-to-all-start = ((s32[32,2,3]{2,1,0:T(2,128)}), s32[32,2,3]{2,1,0:T(2,128)S(1)}, u32[]{:S(2)}, u32[]{:S(2)}) async-start(s32[32,2,3]{2,1,0:T(2,128)} %copy.77), calls=%async_computation | async-start | bytes 65536 | tf_op jit(solution)/shard_map/all_to_all | solution.py:165
  10.2 0.9 %copy.69 = bf16[32,512]{0,1:T(8,128)(2,1)S(1)} copy(bf16[32,512]{1,0:T(8,128)(2,1)} %param.11) | data formatting | bytes 65536 | tf_op args[4]
  11.1 0.2 copy.70
  11.3 2.7 %collective-permute-start = (bf16[1,32,512]{1,2,0:T(8,128)(2,1)S(1)}, bf16[1,32,512]{1,2,0:T(8,128)(2,1)S(1)}, u32[]{:S(2)}, u32[]{:S(2)}) collective-permute-start(bf16[1,32,512]{1,2,0:T(8,128)(2,1)S(1)} %bitcast.83), channel_id=1, source_target_pairs={{0,16},{1,17},{2,18},{3,19},{4,20},{5,21},{6,22},{7,23},{8,24},{9,... | collective-permute-start | bytes 98312 | tf_op jit(solution)/shard_map/ppermute | solution.py:138
  14.0 0.0 copy-start
  14.0 0.0 copy-start.1
  14.9 0.1 mul.210
  14.9 0.1 mul.211
  15.0 0.1 mul.207
  15.1 0.1 mul.208
  15.2 0.1 mul.204
  15.3 0.1 copy.71
  16.1 0.1 mul.214
  16.1 0.1 mul.215
  16.2 1.2 %all-to-all-done = s32[32,2,3]{2,1,0:T(2,128)S(1)} async-done(((s32[32,2,3]{2,1,0:T(2,128)}), s32[32,2,3]{2,1,0:T(2,128)S(1)}, u32[]{:S(2)}, u32[]{:S(2)}) %all-to-all-start) | async-done | bytes 800 | tf_op jit(solution)/shard_map/all_to_all | solution.py:165
  17.5 0.7 reshape_reshape.10.req_ref
  18.2 7.6 %shard_map.86 = bf16[32,64,128]{2,1,0:T(8,128)(2,1)} custom-call(s32[192]{0:T(256)} %reshape_reshape.10.req_ref, bf16[2,128,4096]{2,1,0:T(8,128)(2,1)} %tiles_ref.1), custom_call_target="tpu_custom_call" | custom-call | flops 67108864 | bytes 2621440 | tf_op jit(solution)/shard_map/pallas_call | solution.py:116
  25.8 2.6 %all-to-all-start.1 = ((bf16[32,64,128]{2,1,0:T(8,128)(2,1)}), bf16[32,64,128]{2,1,0:T(8,128)(2,1)S(1)}, u32[]{:S(2)}, u32[]{:S(2)}) async-start(bf16[32,64,128]{2,1,0:T(8,128)(2,1)} %shard_map.86), calls=%async_computation.1 | async-start | bytes 1048576 | tf_op jit(solution)/shard_map/all_to_all | solution.py:171
  28.4 0.0 copy-done
  28.4 0.0 copy-done.1
  28.4 0.0 collective-permute-done
  28.5 0.1 copy.72
  28.6 1.8 %collective-permute-start.1 = (bf16[2,32,512]{2,1,0:T(8,128)(2,1)S(1)}, bf16[2,32,512]{2,1,0:T(8,128)(2,1)S(1)}, u32[]{:S(2)}, u32[]{:S(2)}) collective-permute-start(bf16[2,32,512]{2,1,0:T(8,128)(2,1)S(1)} %maximum_select_fusion.4), channel_id=1, source_target_pairs={{0,8},{1,9},{2,10},{3,11},{4,12},{5,13},{6,14},{7,15},{8,0},{9,1},... | collective-permute-start | bytes 196616 | tf_op jit(solution)/shard_map/ppermute | solution.py:138
  30.3 1.2 %multiply_convert_fusion.2 = bf16[1664,512]{1,0:T(8,128)(2,1)S(1)} fusion(f32[512]{0:T(512)S(1)} %get-tuple-element.13, f32[1664]{0:T(1024)S(1)} %get-tuple-element.16, f32[512]{0:T(512)S(1)} %get-tuple-element.12, f32[1664]{0:T(1024)S(1)} %get-tuple-element.17), kind=kLoop, calls=%fused_computation.4 | loop fusion | flops 8519680 | bytes 1721344 | tf_op jit(solution)/shard_map/convert_element_type | solution.py:81
  31.6 7.3 %collective-permute-done.1 = bf16[2,32,512]{2,1,0:T(8,128)(2,1)S(1)} collective-permute-done((bf16[2,32,512]{2,1,0:T(8,128)(2,1)S(1)}, bf16[2,32,512]{2,1,0:T(8,128)(2,1)S(1)}, u32[]{:S(2)}, u32[]{:S(2)}) %collective-permute-start.1) | collective-permute-done | bytes 65568 | tf_op jit(solution)/shard_map/ppermute | solution.py:138
  38.9 1.7 %collective-permute-start.2 = (bf16[4,32,512]{2,1,0:T(8,128)(2,1)S(1)}, bf16[4,32,512]{2,1,0:T(8,128)(2,1)S(1)}, u32[]{:S(2)}, u32[]{:S(2)}) collective-permute-start(bf16[4,32,512]{2,1,0:T(8,128)(2,1)S(1)} %maximum_select_fusion.3), channel_id=1, source_target_pairs={{0,4},{1,5},{2,6},{3,7},{4,0},{5,1},{6,2},{7,3},{8,12},{9,13},{10,... | collective-permute-start | bytes 393224 | tf_op jit(solution)/shard_map/ppermute | solution.py:138
  40.6 0.1 add_add_fusion
  40.7 4.2 %collective-permute-done.2 = bf16[4,32,512]{2,1,0:T(8,128)(2,1)S(1)} collective-permute-done((bf16[4,32,512]{2,1,0:T(8,128)(2,1)S(1)}, bf16[4,32,512]{2,1,0:T(8,128)(2,1)S(1)}, u32[]{:S(2)}, u32[]{:S(2)}) %collective-permute-start.2) | collective-permute-done | bytes 131104 | tf_op jit(solution)/shard_map/ppermute | solution.py:138
  45.0 1.5 %collective-permute-start.3 = (bf16[8,32,512]{2,1,0:T(8,128)(2,1)S(1)}, bf16[8,32,512]{2,1,0:T(8,128)(2,1)S(1)}, u32[]{:S(2)}, u32[]{:S(2)}) collective-permute-start(bf16[8,32,512]{2,1,0:T(8,128)(2,1)S(1)} %maximum_select_fusion.2), channel_id=1, source_target_pairs={{0,2},{1,3},{2,0},{3,1},{4,6},{5,7},{6,4},{7,5},{8,10},{9,11},{10,... | collective-permute-start | bytes 786440 | tf_op jit(solution)/shard_map/ppermute | solution.py:138
  46.4 0.0 all-to-all-done.1
  46.4 0.6 gather_fusion
  47.1 2.7 %convolution_convert_fusion = bf16[64,512]{1,0:T(8,128)(2,1)S(1)} fusion(bf16[1664,512]{1,0:T(8,128)(2,1)S(1)} %multiply_convert_fusion.2, f32[21,1664]{1,0:T(8,128)S(1)} %add_add_fusion, pred[21]{0:T(512)(128)(4,1)S(1)} %get-tuple-element.20, bf16[21,64,128]{2,1,0:T(8,128)(2,1)S(1)} %gather_fusion, pred[21]{0:T(512)(128)(4,1)S(1)} %get-tuple-element.15, ...), kind=kOutput, calls=%fused_computation.11 | convolution fusion | flops 411365376 | bytes 2618880 | tf_op jit(solution)/shard_map/dot_general | solution.py:185
  49.8 0.1 fusion.18
  49.9 0.1 mul.220
  50.0 1.1 %broadcast_multiply_fusion = bf16[1,32,32,512]{3,2,0,1:T(8,128)(2,1)} fusion(bf16[1,32,32,512]{3,2,0,1:T(8,128)(2,1)S(1)} %bitcast.75, bf16[32]{0:T(256)(128)(2,1)S(1)} %mul.215), kind=kLoop, calls=%fused_computation.19 | loop fusion | flops 524288 | bytes 2097216 | tf_op jit(solution)/shard_map/mul | solution.py:198
  51.1 5.1 %all-to-all-start.2 = ((bf16[1,32,32,512]{3,2,0,1:T(8,128)(2,1)}), bf16[1,32,32,512]{3,2,0,1:T(8,128)(2,1)S(1)}, u32[]{:S(2)}, u32[]{:S(2)}) async-start(bf16[1,32,32,512]{3,2,0,1:T(8,128)(2,1)} %broadcast_multiply_fusion), calls=%async_computation.2 | async-start | bytes 2097152 | tf_op jit(solution)/shard_map/all_to_all | solution.py:226
  56.2 0.0 collective-permute-done.3
  56.2 0.1 maximum_select_fusion.1
  56.3 0.3 collective-permute-start.4
  56.6 1.6 %collective-permute-done.4 = bf16[16,32,512]{2,1,0:T(8,128)(2,1)S(1)} collective-permute-done((bf16[16,32,512]{2,1,0:T(8,128)(2,1)S(1)}, bf16[16,32,512]{2,1,0:T(8,128)(2,1)S(1)}, u32[]{:S(2)}, u32[]{:S(2)}) %collective-permute-start.4) | collective-permute-done | bytes 524320 | tf_op jit(solution)/shard_map/ppermute | solution.py:138
  58.3 0.2 maximum_select_fusion
  58.5 0.1 copy.75
  58.6 0.3 multiply_reduce_fusion
  58.9 0.1 copy.79
  59.0 0.3 copy.80
  59.3 0.3 fusion.6
  59.6 0.3 fusion.4
  59.9 0.2 copy.83
  60.1 0.6 multiply_reduce_fusion.1
  61.4 0.1 copy.84
  61.5 0.1 sqrt.12
  61.6 0.5 fusion.5
  62.0 0.7 reshape.445
  62.7 19.7 %all-to-all-done.2 = bf16[1,32,32,512]{3,2,0,1:T(8,128)(2,1)S(1)} async-done(((bf16[1,32,32,512]{3,2,0,1:T(8,128)(2,1)}), bf16[1,32,32,512]{3,2,0,1:T(8,128)(2,1)S(1)}, u32[]{:S(2)}, u32[]{:S(2)}) %all-to-all-start.2) | async-done | bytes 1048608 | tf_op jit(solution)/shard_map/all_to_all | solution.py:226
  82.5 0.8 convert_reduce_fusion
  (21 shorter events, 0.3 us)
Async XLA Ops:
  2.9 14.6 %all-to-all-start = ((s32[32,2,3]{2,1,0:T(2,128)}), s32[32,2,3]{2,1,0:T(2,128)S(1)}, u32[]{:S(2)}, u32[]{:S(2)}) async-start(s32[32,2,3]{2,1,0:T(2,128)} %copy.77), calls=%async_computation | async-start | bytes 65536 | tf_op jit(solution)/shard_map/all_to_all | solution.py:165
  11.3 17.2 %collective-permute-start = (bf16[1,32,512]{1,2,0:T(8,128)(2,1)S(1)}, bf16[1,32,512]{1,2,0:T(8,128)(2,1)S(1)}, u32[]{:S(2)}, u32[]{:S(2)}) collective-permute-start(bf16[1,32,512]{1,2,0:T(8,128)(2,1)S(1)} %bitcast.83), channel_id=1, source_target_pairs={{0,16},{1,17},{2,18},{3,19},{4,20},{5,21},{6,22},{7,23},{8,24},{9,... | collective-permute-start | bytes 98312 | tf_op jit(solution)/shard_map/ppermute | solution.py:138
  14.0 14.4 %copy-start = (f32[1664]{0:T(1024)S(1)}, f32[1664]{0:T(1024)}, u32[]{:S(2)}) copy-start(f32[1664]{0:T(1024)} %constant.181.clone) | copy-start | bytes 19972
  14.0 14.4 %copy-start.1 = (f32[1664]{0:T(1024)S(1)}, f32[1664]{0:T(1024)}, u32[]{:S(2)}) copy-start(f32[1664]{0:T(1024)} %constant.180.clone) | copy-start | bytes 19972
  25.8 20.6 %all-to-all-start.1 = ((bf16[32,64,128]{2,1,0:T(8,128)(2,1)}), bf16[32,64,128]{2,1,0:T(8,128)(2,1)S(1)}, u32[]{:S(2)}, u32[]{:S(2)}) async-start(bf16[32,64,128]{2,1,0:T(8,128)(2,1)} %shard_map.86), calls=%async_computation.1 | async-start | bytes 1048576 | tf_op jit(solution)/shard_map/all_to_all | solution.py:171
  28.6 10.3 %collective-permute-start.1 = (bf16[2,32,512]{2,1,0:T(8,128)(2,1)S(1)}, bf16[2,32,512]{2,1,0:T(8,128)(2,1)S(1)}, u32[]{:S(2)}, u32[]{:S(2)}) collective-permute-start(bf16[2,32,512]{2,1,0:T(8,128)(2,1)S(1)} %maximum_select_fusion.4), channel_id=1, source_target_pairs={{0,8},{1,9},{2,10},{3,11},{4,12},{5,13},{6,14},{7,15},{8,0},{9,1},... | collective-permute-start | bytes 196616 | tf_op jit(solution)/shard_map/ppermute | solution.py:138
  38.9 6.0 %collective-permute-start.2 = (bf16[4,32,512]{2,1,0:T(8,128)(2,1)S(1)}, bf16[4,32,512]{2,1,0:T(8,128)(2,1)S(1)}, u32[]{:S(2)}, u32[]{:S(2)}) collective-permute-start(bf16[4,32,512]{2,1,0:T(8,128)(2,1)S(1)} %maximum_select_fusion.3), channel_id=1, source_target_pairs={{0,4},{1,5},{2,6},{3,7},{4,0},{5,1},{6,2},{7,3},{8,12},{9,13},{10,... | collective-permute-start | bytes 393224 | tf_op jit(solution)/shard_map/ppermute | solution.py:138
  45.0 11.3 %collective-permute-start.3 = (bf16[8,32,512]{2,1,0:T(8,128)(2,1)S(1)}, bf16[8,32,512]{2,1,0:T(8,128)(2,1)S(1)}, u32[]{:S(2)}, u32[]{:S(2)}) collective-permute-start(bf16[8,32,512]{2,1,0:T(8,128)(2,1)S(1)} %maximum_select_fusion.2), channel_id=1, source_target_pairs={{0,2},{1,3},{2,0},{3,1},{4,6},{5,7},{6,4},{7,5},{8,10},{9,11},{10,... | collective-permute-start | bytes 786440 | tf_op jit(solution)/shard_map/ppermute | solution.py:138
  51.1 31.3 %all-to-all-start.2 = ((bf16[1,32,32,512]{3,2,0,1:T(8,128)(2,1)}), bf16[1,32,32,512]{3,2,0,1:T(8,128)(2,1)S(1)}, u32[]{:S(2)}, u32[]{:S(2)}) async-start(bf16[1,32,32,512]{3,2,0,1:T(8,128)(2,1)} %broadcast_multiply_fusion), calls=%async_computation.2 | async-start | bytes 2097152 | tf_op jit(solution)/shard_map/all_to_all | solution.py:226
  56.3 2.0 %collective-permute-start.4 = (bf16[16,32,512]{2,1,0:T(8,128)(2,1)S(1)}, bf16[16,32,512]{2,1,0:T(8,128)(2,1)S(1)}, u32[]{:S(2)}, u32[]{:S(2)}) collective-permute-start(bf16[16,32,512]{2,1,0:T(8,128)(2,1)S(1)} %maximum_select_fusion.1), channel_id=1, source_target_pairs={{0,1},{1,0},{2,3},{3,2},{4,5},{5,4},{6,7},{7,6},{8,9},{9,8},{10,11... | collective-permute-start | bytes 1572872 | tf_op jit(solution)/shard_map/ppermute | solution.py:138
